TPU v7x, 128 devices: a whole 4x4x4 slice. The times are simulated.
128 devices in a mesh: pair: 32 (over z, y, core), integral: 4 (over x).
Axes of the slice: x: 4, y: 4, z: 4, core: 2. Of those that a mesh axis runs over, the one named last changes fastest.
Arguments:
- occ_irrep: int32 [240], replicated, may hold values from 0 to 7
- amplitudes: bfloat16 [1920, 16384], P('pair', 'integral'), may hold values from -6 to 6
- ladder_ints: bfloat16 [16384, 16384], P('integral', 'pair'), may hold values from -0.046875 to 0.046875
- cycle_ints: bfloat16 [240, 128, 30720], P(None, 'integral', 'pair'), may hold values from -0.03125 to 0.03125
Outputs:
- residual: float32 [8, 240, 16384], P('integral', None, 'pair')
Inputs may be any that keep to these rules, and one draw needn't show every extreme that they name: `occ_irrep`: irrep labels of D2h, below 8.
All inputs are finite; a program needn't handle non-finite values.
Results may differ from a plain program's by a relative error of at most 0.0003.
Values may be sent and summed in bfloat16 or wider, within the bound.
No kernel may reach another device: no remote copies, remote signals or barrier semaphores. Data moves between devices by JAX's collectives and lax.ppermute only.
A program may use at most 192 MiB of HBM per device.

v0:
```python
import jax
import jax.numpy as jnp
from jax import lax
from jax.sharding import PartitionSpec as P


def lookup_labels(indices, labels, occ_count):
    orbital = jnp.arange(occ_count, dtype=jnp.int32)
    return jnp.sum(jnp.where(indices[:, None] == orbital[None, :], labels[None, :], 0), axis=1)


def body(occ_irrep, amplitudes, ladder_ints, cycle_ints):
    rows_local = amplitudes.shape[0]
    occ_count, vir_part, cycle_cols = cycle_ints.shape
    vir_full = amplitudes.shape[1] // vir_part
    vir_local = cycle_cols // occ_count
    row_start = lax.axis_index("pair") * rows_local
    global_row = row_start + jnp.arange(rows_local, dtype=jnp.int32)
    label_first = lookup_labels(global_row // occ_count, occ_irrep, occ_count)
    label_second = lookup_labels(global_row % occ_count, occ_irrep, occ_count)
    allowed = label_first == label_second
    amp_sym = jnp.where(allowed[:, None], amplitudes, jnp.zeros((), amplitudes.dtype))
    gathered = lax.all_gather(amp_sym, "pair", axis=0, tiled=True)
    total_rows = gathered.shape[0]
    window = total_rows // occ_count
    ladder = jnp.dot(gathered, ladder_ints, preferred_element_type=jnp.float32)
    ladder = ladder.reshape(window, occ_count, vir_local * vir_full)
    cycle_term = jnp.einsum(
        "ixa,xn->ian",
        gathered.reshape(window, occ_count * vir_part, vir_full),
        cycle_ints.reshape(occ_count * vir_part, cycle_cols),
        preferred_element_type=jnp.float32,
    )
    cycle_term = cycle_term.reshape(window, vir_full, vir_local, occ_count)
    same_irrep = (occ_irrep[:window][:, None] == occ_irrep[None, :]).astype(jnp.float32)
    cycle_term = cycle_term * same_irrep[:, None, None, :]
    regrouped = lax.all_to_all(cycle_term, "pair", split_axis=1, concat_axis=2, tiled=True)
    rows_here = regrouped.shape[0]
    moved = jnp.transpose(regrouped, (0, 3, 1, 2)).reshape(
        rows_here, occ_count, vir_local * vir_full
    )
    combined = ladder + moved
    return lax.psum_scatter(combined, "integral", scatter_dimension=0, tiled=True)


def solution(mesh):
    placed = (P(), P("pair", "integral"), P("integral", "pair"), P(None, "integral", "pair"))
    return jax.shard_map(
        body, mesh=mesh, in_specs=placed, out_specs=P("integral", None, "pair"), check_vma=False
    )
```

profile of v0, /device:TPU:1, one launch (start us, length us, event | category | flops | bytes accessed | tf_op | source)
XLA Modules:
  0.0 257.9 jit_solution(16068655335252896543)
XLA Ops:
  6.5 0.0 all-gather.3.cloned.1.call-start
  6.6 0.9 select_reduce_fusion
  7.4 1.9 select_bitcast_fusion
  9.4 0.0 all-gather.3.cloned.1.call-update
  9.4 0.0 copy-start
  9.4 0.0 slice-start
  9.4 19.3 %copy.15 = bf16[960,7680]{1,0:T(8,128)(2,1)} copy(bf16[960,7680]{0,1:T(8,128)(2,1)} %bitcast.27) | data formatting | bytes 29491200 | tf_op jit(solution)/shard_map/ixa,xn->ian/dot_general | solution.py:28
  28.7 0.0 copy-done
  28.7 0.0 slice-done
  28.7 0.1 compare_convert_fusion
  28.8 57.2 %all-gather.3.cloned.1.call-done = bf16[32,60,4096]{2,1,0:T(8,128)(2,1)} async-done(((bf16[1,60,4096]{2,1,0:T(8,128)(2,1)}), bf16[32,60,4096]{2,1,0:T(8,128)(2,1)}) %all-gather.3.cloned.1.call-update) | async-done | bytes 15728656 | tf_op jit(solution)/shard_map/all_gather | solution.py:23
  86.0 20.3 %reshape.67 = bf16[8,7680,128,1]{2,1,0,3:T(8,128)(2,1)} reshape(bf16[32,60,4096]{2,1,0:T(8,128)(2,1)} %all-gather.3.cloned.1.call-done) | data formatting | bytes 31457280 | tf_op jit(solution)/shard_map/reshape | solution.py:30
  106.3 21.9 %broadcast_multiply_fusion = f32[8,128,4,240]{1,3,2,0:T(8,128)} fusion(f32[8,240]{1,0:T(8,128)S(1)} %compare_convert_fusion, bf16[4,240,7680,1]{2,1,0,3:T(8,128)(2,1)} %bitcast.28, bf16[8,7680,128,1]{2,1,0,3:T(8,128)(2,1)} %reshape.67), kind=kOutput, calls=%fused_computation.2 | convolution fusion | flops 15100477440 | bytes 34414080 | tf_op jit(solution)/shard_map/ixa,xn->ian/dot_general | solution.py:28
  128.2 5.4 %copy.16 = f32[8,128,4,240]{3,2,0,1:T(4,128)} copy(f32[8,128,4,240]{1,3,2,0:T(8,128)} %broadcast_multiply_fusion) | data formatting | bytes 7864320 | tf_op jit(solution)/shard_map/mul | solution.py:36
  133.7 5.5 %all-to-all-start = ((f32[8,128,4,240]{3,2,0,1:T(4,128)}), f32[8,128,4,240]{3,2,0,1:T(4,128)}, u32[]{:S(2)}, u32[]{:S(2)}) async-start(f32[8,128,4,240]{3,2,0,1:T(4,128)} %copy.16), calls=%async_computation | async-start | bytes 8388608 | tf_op jit(solution)/shard_map/all_to_all | solution.py:37
  139.2 0.2 reduce-scatter.2.cloned.1.call-start
  139.4 17.9 %reshape.65 = bf16[1920,4096]{1,0:T(8,128)(2,1)} reshape(bf16[32,60,4096]{2,1,0:T(8,128)(2,1)} %all-gather.3.cloned.1.call-done) | data formatting | bytes 31457280
  157.3 14.1 %fusion.5 = f32[1920,512]{1,0:T(8,128)} fusion(bf16[1920,4096]{1,0:T(8,128)(2,1)} %reshape.65, bf16[4096,512]{1,0:T(8,128)(2,1)} %param.6), kind=kOutput, calls=%fused_computation.13 | convolution fusion | flops 8053063680 | bytes 23855104 | tf_op jit(solution)/shard_map/dot_general | solution.py:26
  171.5 18.4 %all-to-all-done = f32[8,128,4,240]{3,2,0,1:T(4,128)} async-done(((f32[8,128,4,240]{3,2,0,1:T(4,128)}), f32[8,128,4,240]{3,2,0,1:T(4,128)}, u32[]{:S(2)}, u32[]{:S(2)}) %all-to-all-start) | async-done | bytes 3932192 | tf_op jit(solution)/shard_map/all_to_all | solution.py:37
  189.8 3.2 %copy.17 = f32[8,128,4,240]{3,0,2,1:T(8,128)S(1)} copy(f32[8,128,4,240]{3,2,0,1:T(4,128)} %all-to-all-done) | data formatting | bytes 7864320 | tf_op jit(solution)/shard_map/all_to_all | solution.py:37
  193.0 2.3 copy.18
  195.3 5.3 %copy.19 = f32[8,240,512]{2,1,0:T(8,128)} copy(f32[8,240,512]{1,0,2:T(8,128)} %bitcast.26) | data formatting | bytes 7864320 | tf_op jit(solution)/shard_map/reshape | solution.py:39
  200.6 6.2 %add.36 = f32[8,240,512]{2,1,0:T(8,128)} add(f32[8,240,512]{2,1,0:T(8,128)} %bitcast.29, f32[8,240,512]{2,1,0:T(8,128)} %copy.19) | non-fusion elementwise | flops 983040 | bytes 11796480 | tf_op jit(solution)/shard_map/add | solution.py:42
  206.8 0.0 reduce-scatter.2.cloned.1.call-update
  206.9 44.2 %reduce-scatter.2.cloned.1.call-done = f32[2,240,512]{2,1,0:T(8,128)} async-done(((f32[8,240,512]{2,1,0:T(8,128)}), f32[2,240,512]{2,1,0:T(8,128)}) %reduce-scatter.2.cloned.1.call-update) | async-done | bytes 983056 | tf_op jit(solution)/shard_map/reduce_scatter | solution.py:43
  (2 shorter events, 0.0 us)
Async XLA Ops:
  6.5 79.4 %all-gather.3.cloned.1.call-start = ((), (), s32[]{:S(2)}) async-start(), calls=%async_computation.3 | async-start | bytes 17301504 | tf_op jit(solution)/shard_map/all_gather | solution.py:23
  9.4 19.3 %copy-start = (s32[240]{0:T(256)S(1)}, s32[240]{0:T(256)}, u32[]{:S(2)}) copy-start(s32[240]{0:T(256)} %param.4) | copy-start | bytes 2884
  9.4 19.3 %slice-start = ((s32[240]{0:T(256)}), s32[8]{0:T(128)S(1)}, s32[]{:S(2)}) async-start(s32[240]{0:T(256)} %param.4), calls=%async_computation.4 | async-start | bytes 1024 | tf_op jit(solution)/shard_map/slice | solution.py:35
  133.7 56.2 %all-to-all-start = ((f32[8,128,4,240]{3,2,0,1:T(4,128)}), f32[8,128,4,240]{3,2,0,1:T(4,128)}, u32[]{:S(2)}, u32[]{:S(2)}) async-start(f32[8,128,4,240]{3,2,0,1:T(4,128)} %copy.16), calls=%async_computation | async-start | bytes 8388608 | tf_op jit(solution)/shard_map/all_to_all | solution.py:37
  139.2 111.9 %reduce-scatter.2.cloned.1.call-start = ((), (), s32[]{:S(2)}) async-start(), calls=%async_computation.2 | async-start | bytes 4915200 | tf_op jit(solution)/shard_map/reduce_scatter | solution.py:43
Sparse Core Ops, SparseCore 0:
  9.6 76.3 all-gather.2
  207.0 44.0 reduce-scatter.1
where the time goes:
time: 260 us; the launch traced here: 258 us
  waiting for transfers between devices  120 us (46%)
  local copies, waits for them, and re-layouts  73.8 us (28%)
  matrix products  36.1 us (14%)
  between operations  13.4 us (5%)
  other arithmetic  9.1 us (4%)
  starting transfers between devices  5.7 us (2%)
    all_gather x1, waiting for transfers between devices, body(): gathered = lax.all_gather(amp_sym, 'pair', axis=0, tiled=True)  57.2 us
    reduce_scatter x1, waiting for transfers between devices, body(): lax.psum_scatter(combined, 'integral', scatter_dimension=0, tiled=True)  44.2 us
    dot_general x1, matrix products, body(): jnp.einsum('ixa,xn->ian', gathered.reshape(window, occ_count * vir_part,...  21.9 us
    reshape x1, local copies, waits for them, and re-layouts, body(): gathered.reshape(window, occ_count * vir_part, vir_full)  20.3 us
    dot_general x1, local copies, waits for them, and re-layouts, body(): jnp.einsum('ixa,xn->ian', gathered.reshape(window, occ_count * vir_part,...  19.3 us
    all_to_all x1, waiting for transfers between devices, body(): lax.all_to_all(cycle_term, 'pair', split_axis=1, concat_axis=2, tiled=True)  18.4 us
    unnamed x3, local copies, waits for them, and re-layouts  18 us
    dot_general x1, matrix products, body(): ladder = jnp.dot(gathered, ladder_ints, preferred_element_type=jnp.float32)  14.1 us
  transfers between devices with their start and end apart: 3, of which 3 were waited for; matrix products, arithmetic and copies ran while one was open for 20% of the time, Pallas kernels for 0%

commit v1 on v0

v1 whole, which is shorter than its diff:
```python
import functools
import jax
import jax.numpy as jnp
from jax import lax
from jax.experimental import pallas as pl
from jax.experimental.pallas import tpu as pltpu
from jax.sharding import Mesh, PartitionSpec as P

PAIR = ("z", "y", "core")
C_STEP = 4


def cycle_kernel(window, vir_full, vt_ref, g_ref, o_ref):
    step = pl.program_id(0)
    rows = vt_ref.shape[2]
    total = None
    for c in range(vt_ref.shape[0]):
        lanes = slice(c * vir_full, (c + 1) * vir_full)
        rhs = jnp.concatenate([g_ref[i * rows:(i + 1) * rows, lanes] for i in range(window)], axis=1)
        part = jnp.dot(vt_ref[c], rhs, preferred_element_type=jnp.float32)
        total = part if total is None else total + part

    @pl.when(step == 0)
    def _():
        o_ref[...] = total

    @pl.when(step > 0)
    def _():
        o_ref[...] += total


def cycle_matmul(vt, g, window, vir_full):
    vir_part, n_cols, rows = vt.shape
    steps = vir_part // C_STEP
    return pl.pallas_call(
        functools.partial(cycle_kernel, window, vir_full),
        out_shape=jax.ShapeDtypeStruct((n_cols, window * vir_full), jnp.float32),
        grid=(steps,),
        in_specs=[
            pl.BlockSpec((C_STEP, n_cols, rows), lambda s: (s, 0, 0)),
            pl.BlockSpec((g.shape[0], C_STEP * vir_full), lambda s: (0, s)),
        ],
        out_specs=pl.BlockSpec((n_cols, window * vir_full), lambda s: (0, 0)),
        compiler_params=pltpu.CompilerParams(dimension_semantics=("arbitrary",), vmem_limit_bytes=48 * 1024 * 1024),
    )(vt, g)


def body(occ_irrep, amplitudes, ladder_ints, cycle_ints):
    rows_local, cols_local = amplitudes.shape
    occ_count, vir_part, cycle_cols = cycle_ints.shape
    vir_full = cols_local // vir_part
    vir_local = cycle_cols // occ_count
    pad_rows = -(-rows_local // 16) * 16
    pidx = lax.axis_index(PAIR)
    global_row = pidx * rows_local + jnp.arange(rows_local, dtype=jnp.int32)
    allowed = occ_irrep[global_row // occ_count] == occ_irrep[global_row % occ_count]
    amp_sym = jnp.where(allowed[:, None], amplitudes, jnp.zeros((), amplitudes.dtype))
    amp_pad = jnp.pad(amp_sym, ((0, pad_rows - rows_local), (0, 0)))
    part = lax.all_gather(amp_pad, ("z", "y"), axis=0, tiled=False)
    gathered = lax.all_gather(part, "core", axis=1, tiled=False)
    n_blocks = gathered.shape[0] * gathered.shape[1]
    g2 = gathered.reshape(n_blocks * pad_rows, cols_local)
    total_rows = n_blocks * rows_local
    window = total_rows // occ_count
    per_i = n_blocks // window

    ladder = jnp.dot(g2, ladder_ints, preferred_element_type=jnp.float32)
    ladder = ladder.reshape(n_blocks, pad_rows, -1)[:, :rows_local, :]
    ladder = ladder.reshape(window, occ_count, vir_local * vir_full)

    v4 = cycle_ints.reshape(per_i, rows_local, vir_part, cycle_cols)
    v4 = jnp.pad(v4, ((0, 0), (0, pad_rows - rows_local), (0, 0), (0, 0)))
    vt = jnp.transpose(v4, (2, 3, 0, 1)).reshape(vir_part, cycle_cols, per_i * pad_rows)
    cyc = cycle_matmul(vt, g2, window, vir_full)
    cyc = cyc.reshape(vir_local, occ_count, window, vir_full)
    same_irrep = (occ_irrep[:window][:, None] == occ_irrep[None, :]).astype(jnp.float32)
    cyc = cyc * jnp.transpose(same_irrep)[None, :, :, None]
    cycle_term = jnp.transpose(cyc, (2, 3, 0, 1))
    regrouped = lax.all_to_all(cycle_term, PAIR, split_axis=1, concat_axis=2, tiled=True)
    rows_here = regrouped.shape[0]
    moved = jnp.transpose(regrouped, (0, 3, 1, 2)).reshape(rows_here, occ_count, vir_local * vir_full)
    combined = ladder + moved
    return lax.psum_scatter(combined, "x", scatter_dimension=0, tiled=True)


def solution(mesh):
    devs = mesh.devices
    n_pair, n_int = devs.shape
    fine = Mesh(devs.reshape(4, n_pair // 8, 2, n_int), ("z", "y", "core", "x"))
    placed = (P(), P(PAIR, "x"), P("x", PAIR), P(None, "x", PAIR))
    return jax.shard_map(body, mesh=fine, in_specs=placed, out_specs=P("x", None, PAIR), check_vma=False)
```

time: 260 us -> 292 us (1.12)
  waiting for transfers between devices: 120 us -> 149 us
  Pallas kernels: 0 us -> 22.9 us
  matrix products: 36.1 us -> 14.9 us
  other arithmetic: 9.1 us -> 12.4 us
    reshape x1 -> x4, local copies, waits for them, and re-layouts: 20.3 us -> 47 us  [the longest x1 21.3 us: body(): jnp.transpose(v4, (2, 3, 0, 1))]
    pallas_call x0 -> x1, Pallas kernels: none -> 22.9 us  [cycle_matmul(): pl.pallas_call(functools.partial(cycle_kernel, window, vir_full), out_sha...]
    dot_general x2 -> x1, matrix products: 36.1 us -> 14.9 us  [body(): ladder = jnp.dot(g2, ladder_ints, preferred_element_type=jnp.float32)]
    dot_general x1 -> x0, local copies, waits for them, and re-layouts: 19.3 us -> none  [body(): jnp.einsum('ixa,xn->ian', gathered.reshape(window, occ_count * vir_part,...]
    all_gather x1 -> x2, waiting for transfers between devices: 57.2 us -> 74.1 us  [the longest x1 74.1 us: body(): part = lax.all_gather(amp_pad, ('z', 'y'), axis=0, tiled=False)]
    unnamed x3, local copies, waits for them, and re-layouts: 18 us -> 2.8 us
    all_to_all x1, waiting for transfers between devices: 18.4 us -> 30.5 us  [body(): lax.all_to_all(cycle_term, PAIR, split_axis=1, concat_axis=2, tiled=True)]
    pad x0 -> x2, local copies, waits for them, and re-layouts: none -> 9.92 us  [the longest x1 9.08 us: body(): v4 = jnp.pad(v4, ((0, 0), (0, pad_rows - rows_local), (0, 0), (0, 0)))]
  transfers between devices with their start and end apart: 3 -> 4, of which waited for: 3 -> 3; matrix products, arithmetic and copies ran while one was open for 20% -> 23% of each run, Pallas kernels for 0% -> 0%
where the time goes in v1:
time: 292 us; the launch traced here: 291 us
  waiting for transfers between devices  149 us (51%)
  local copies, waits for them, and re-layouts  72.7 us (25%)
  Pallas kernels  22.9 us (8%)
  matrix products  14.9 us (5%)
  between operations  13.2 us (5%)
  other arithmetic  12.4 us (4%)
  starting transfers between devices  6.15 us (2%)
    all_gather x1, waiting for transfers between devices, body(): part = lax.all_gather(amp_pad, ('z', 'y'), axis=0, tiled=False)  74.1 us
    reduce_scatter x1, waiting for transfers between devices, body(): return lax.psum_scatter(combined, 'x', scatter_dimension=0, tiled=True)  44.2 us
    all_to_all x1, waiting for transfers between devices, body(): lax.all_to_all(cycle_term, PAIR, split_axis=1, concat_axis=2, tiled=True)  30.5 us
    pallas_call x1, Pallas kernels, cycle_matmul(): pl.pallas_call(functools.partial(cycle_kernel, window, vir_full), out_sha...  22.9 us
    reshape x1, local copies, waits for them, and re-layouts, body(): jnp.transpose(v4, (2, 3, 0, 1))  21.3 us
    reshape x1, local copies, waits for them, and re-layouts, body(): v4 = cycle_ints.reshape(per_i, rows_local, vir_part, cycle_cols)  15.3 us
    dot_general x1, matrix products, body(): ladder = jnp.dot(g2, ladder_ints, preferred_element_type=jnp.float32)  14.9 us
    pad x1, local copies, waits for them, and re-layouts, body(): v4 = jnp.pad(v4, ((0, 0), (0, pad_rows - rows_local), (0, 0), (0, 0)))  9.08 us
  transfers between devices with their start and end apart: 4, of which 3 were waited for; matrix products, arithmetic and copies ran while one was open for 23% of the time, Pallas kernels for 0%

profile of v1, /device:TPU:1, one launch (start us, length us, event | category | flops | bytes accessed | tf_op | source)
XLA Modules:
  0.0 291.1 jit_solution(4164170119097322739)
XLA Ops:
  6.5 0.0 all-gather.5.cloned.1.call-start
  6.6 1.5 gather_fusion
  8.1 1.5 gather_fusion.1
  9.5 1.1 broadcast_select_fusion
  10.7 0.8 pad.8
  11.5 0.0 all-gather.5.cloned.1.call-update
  11.6 0.0 all-gather.7.cloned.1.call-start
  11.6 74.1 %all-gather.5.cloned.1.call-done = bf16[1024,4096]{1,0:T(8,128)(2,1)} async-done(((bf16[64,4096]{1,0:T(8,128)(2,1)}), bf16[1024,4096]{1,0:T(8,128)(2,1)}) %all-gather.5.cloned.1.call-update) | async-done | bytes 8388624 | tf_op jit(solution)/shard_map/all_gather | solution.py:59
  85.7 0.0 all-gather.7.cloned.1.call-update
  85.7 15.3 %copy.7 = bf16[4,60,32,960]{3,1,0,2:T(8,128)(2,1)S(1)} copy(bf16[4,60,32,960]{3,2,1,0:T(8,128)(2,1)} %bitcast.32) | data formatting | bytes 29491200 | tf_op jit(solution)/shard_map/reshape | solution.py:71
  101.0 9.1 %pad.9 = bf16[4,64,32,960]{3,1,0,2:T(8,128)(2,1)} pad(bf16[4,60,32,960]{3,1,0,2:T(8,128)(2,1)S(1)} %copy.7, bf16[]{:T(256)} %constant.45.clone.1), padding=0_0x0_4x0_0x0_0 | pad | bytes 30474242 | tf_op jit(solution)/shard_map/jit(_pad)/pad | solution.py:72
  110.0 0.0 copy-start
  110.0 0.0 slice-start
  110.0 21.3 %copy.8.vt_ref = bf16[32,960,256]{2,1,0:T(8,128)(2,1)} copy(bf16[32,960,256]{1,2,0:T(8,128)(2,1)} %bitcast.28) | data formatting | bytes 31457280 | tf_op jit(solution)/shard_map/reshape | solution.py:73
  131.3 0.0 copy-done
  131.4 0.0 slice-done
  131.4 0.1 compare_convert_fusion
  131.4 0.0 all-gather.7.cloned.1.call-done
  131.4 22.9 %shard_map.46 = f32[960,1024]{1,0:T(8,128)S(1)} custom-call(bf16[32,960,256]{2,1,0:T(8,128)(2,1)} %copy.8.vt_ref, bf16[2048,4096]{1,0:T(8,128)(2,1)} %bitcast.29), custom_call_target="tpu_custom_call" | custom-call | tf_op jit(solution)/shard_map/pallas_call | solution.py:35
  154.3 2.8 copy.13
  157.1 5.5 %copy.9 = f32[4,240,8,128]{1,2,0,3:T(8,128)} copy(f32[4,240,8,128]{3,2,1,0:T(8,128)} %bitcast.33) | data formatting | bytes 7864320 | tf_op jit(solution)/shard_map/reshape | solution.py:75
  162.6 5.0 %multiply_bitcast_fusion = f32[8,128,4,240]{3,0,2,1:T(8,128)} fusion(f32[4,240,8,128]{1,2,0,3:T(8,128)} %copy.9, f32[240,8]{0,1:T(8,128)S(1)} %compare_convert_fusion), kind=kLoop, calls=%fused_computation.5 | loop fusion | flops 983040 | bytes 7872000 | tf_op jit(solution)/shard_map/transpose | solution.py:78
  167.6 5.9 %all-to-all-start = ((f32[8,128,4,240]{3,0,2,1:T(8,128)}), f32[8,128,4,240]{3,0,2,1:T(8,128)}, u32[]{:S(2)}, u32[]{:S(2)}) async-start(f32[8,128,4,240]{3,0,2,1:T(8,128)} %multiply_bitcast_fusion), calls=%async_computation | async-start | bytes 8388608 | tf_op jit(solution)/shard_map/all_to_all | solution.py:79
  173.5 0.2 reduce-scatter.2.cloned.1.call-start
  173.7 14.9 %fusion = f32[32,60,512]{2,1,0:T(8,128)} fusion(bf16[32,64,4096]{2,1,0:T(8,128)(2,1)} %bitcast.30, bf16[4096,512]{1,0:T(8,128)(2,1)} %param.6), kind=kOutput, calls=%fused_computation.2 | convolution fusion | flops 8053063680 | bytes 24903680 | tf_op jit(solution)/shard_map/dot_general | solution.py:67
  188.7 5.0 %reshape.118 = f32[8,240,512]{2,1,0:T(8,128)} reshape(f32[32,60,512]{2,1,0:T(8,128)} %fusion) | data formatting | bytes 7864320 | tf_op jit(solution)/shard_map/reshape | solution.py:69
  193.7 30.5 %all-to-all-done = f32[8,128,4,240]{3,0,2,1:T(8,128)} async-done(((f32[8,128,4,240]{3,0,2,1:T(8,128)}), f32[8,128,4,240]{3,0,2,1:T(8,128)}, u32[]{:S(2)}, u32[]{:S(2)}) %all-to-all-start) | async-done | bytes 3932192 | tf_op jit(solution)/shard_map/all_to_all | solution.py:79
  224.2 4.7 %copy.10 = f32[8,4,32,4,240]{4,0,3,2,1:T(8,128)} copy(f32[8,4,32,4,240]{4,0,3,1,2:T(8,128)} %bitcast.11) | data formatting | bytes 7864320 | tf_op jit(solution)/shard_map/all_to_all | solution.py:79
  228.9 5.3 %copy.12 = f32[8,240,512]{2,1,0:T(8,128)} copy(f32[8,240,512]{1,0,2:T(8,128)} %bitcast.31) | data formatting | bytes 7864320 | tf_op jit(solution)/shard_map/reshape | solution.py:81
  234.2 6.1 %add.80 = f32[8,240,512]{2,1,0:T(8,128)} add(f32[8,240,512]{2,1,0:T(8,128)} %reshape.118, f32[8,240,512]{2,1,0:T(8,128)} %copy.12) | non-fusion elementwise | flops 983040 | bytes 11796480 | tf_op jit(solution)/shard_map/add | solution.py:82
  240.4 0.0 reduce-scatter.2.cloned.1.call-update
  240.4 44.2 %reduce-scatter.2.cloned.1.call-done = f32[2,240,512]{2,1,0:T(8,128)} async-done(((f32[8,240,512]{2,1,0:T(8,128)}), f32[2,240,512]{2,1,0:T(8,128)}) %reduce-scatter.2.cloned.1.call-update) | async-done | bytes 983056 | tf_op jit(solution)/shard_map/reduce_scatter | solution.py:83
  (4 shorter events, 0.0 us)
Async XLA Ops:
  6.5 79.1 %all-gather.5.cloned.1.call-start = ((), (), s32[]{:S(2)}) async-start(), calls=%async_computation.3 | async-start | bytes 8912896 | tf_op jit(solution)/shard_map/all_gather | solution.py:59
  11.6 119.9 %all-gather.7.cloned.1.call-start = ((), (), s32[]{:S(2)}) async-start(), calls=%async_computation.4 | async-start | bytes 25165824 | tf_op jit(solution)/shard_map/all_gather | solution.py:60
  110.0 21.3 %copy-start = (s32[240]{0:T(256)S(1)}, s32[240]{0:T(256)}, u32[]{:S(2)}) copy-start(s32[240]{0:T(256)} %param.4) | copy-start | bytes 2884
  110.0 21.3 %slice-start = ((s32[240]{0:T(256)}), s32[8]{0:T(128)S(1)}, s32[]{:S(2)}) async-start(s32[240]{0:T(256)} %param.4), calls=%async_computation.5 | async-start | bytes 1024 | tf_op jit(solution)/shard_map/slice | solution.py:76
  167.6 56.6 %all-to-all-start = ((f32[8,128,4,240]{3,0,2,1:T(8,128)}), f32[8,128,4,240]{3,0,2,1:T(8,128)}, u32[]{:S(2)}, u32[]{:S(2)}) async-start(f32[8,128,4,240]{3,0,2,1:T(8,128)} %multiply_bitcast_fusion), calls=%async_computation | async-start | bytes 8388608 | tf_op jit(solution)/shard_map/all_to_all | solution.py:79
  173.5 111.1 %reduce-scatter.2.cloned.1.call-start = ((), (), s32[]{:S(2)}) async-start(), calls=%async_computation.2 | async-start | bytes 4915200 | tf_op jit(solution)/shard_map/reduce_scatter | solution.py:83
Sparse Core Ops, SparseCore 0:
  11.7 73.9 all-gather.4
  87.3 32.9 all-gather.6
  240.5 44.0 reduce-scatter.1

commit v2 on v1

--- a/solution.py
+++ b/solution.py
@@ -56,10 +56,8 @@
     allowed = occ_irrep[global_row // occ_count] == occ_irrep[global_row % occ_count]
     amp_sym = jnp.where(allowed[:, None], amplitudes, jnp.zeros((), amplitudes.dtype))
     amp_pad = jnp.pad(amp_sym, ((0, pad_rows - rows_local), (0, 0)))
-    part = lax.all_gather(amp_pad, ("z", "y"), axis=0, tiled=False)
-    gathered = lax.all_gather(part, "core", axis=1, tiled=False)
-    n_blocks = gathered.shape[0] * gathered.shape[1]
-    g2 = gathered.reshape(n_blocks * pad_rows, cols_local)
+    g2 = lax.all_gather(amp_pad, PAIR, axis=0, tiled=True)
+    n_blocks = g2.shape[0] // pad_rows
     total_rows = n_blocks * rows_local
     window = total_rows // occ_count
     per_i = n_blocks // window

time: 292 us -> 249 us (0.85)
  waiting for transfers between devices: 149 us -> 108 us
    all_gather x2 -> x1, waiting for transfers between devices: 74.1 us -> 33.2 us  [body(): g2 = lax.all_gather(amp_pad, PAIR, axis=0, tiled=True)]
  transfers between devices with their start and end apart: 4 -> 3, of which waited for: 3 -> 3; matrix products, arithmetic and copies ran while one was open for 23% -> 25% of each run, Pallas kernels for 0% -> 0%
where the time goes in v2:
time: 249 us; the launch traced here: 248 us
  waiting for transfers between devices  108 us (43%)
  local copies, waits for them, and re-layouts  70.3 us (28%)
  Pallas kernels  22.9 us (9%)
  matrix products  14.9 us (6%)
  between operations  13.5 us (5%)
  other arithmetic  12.4 us (5%)
  starting transfers between devices  5.7 us (2%)
    reduce_scatter x1, waiting for transfers between devices, body(): return lax.psum_scatter(combined, 'x', scatter_dimension=0, tiled=True)  44.2 us
    all_gather x1, waiting for transfers between devices, body(): g2 = lax.all_gather(amp_pad, PAIR, axis=0, tiled=True)  33.2 us
    all_to_all x1, waiting for transfers between devices, body(): lax.all_to_all(cycle_term, PAIR, split_axis=1, concat_axis=2, tiled=True)  30.6 us
    pallas_call x1, Pallas kernels, cycle_matmul(): pl.pallas_call(functools.partial(cycle_kernel, window, vir_full), out_sha...  22.9 us
    reshape x1, local copies, waits for them, and re-layouts, body(): jnp.transpose(v4, (2, 3, 0, 1))  21 us
    dot_general x1, matrix products, body(): ladder = jnp.dot(g2, ladder_ints, preferred_element_type=jnp.float32)  14.9 us
    reshape x1, local copies, waits for them, and re-layouts, body(): v4 = cycle_ints.reshape(per_i, rows_local, vir_part, cycle_cols)  14.9 us
    pad x1, local copies, waits for them, and re-layouts, body(): v4 = jnp.pad(v4, ((0, 0), (0, pad_rows - rows_local), (0, 0), (0, 0)))  7.36 us
  transfers between devices with their start and end apart: 3, of which 3 were waited for; matrix products, arithmetic and copies ran while one was open for 25% of the time, Pallas kernels for 0%

profile of v2, /device:TPU:1, one launch (start us, length us, event | category | flops | bytes accessed | tf_op | source)
XLA Modules:
  0.0 247.6 jit_solution(3804101962489998812)
XLA Ops:
  6.5 0.0 all-gather.2.cloned.1.call-start
  6.6 1.5 gather_fusion
  8.1 1.5 gather_fusion.1
  9.5 1.1 broadcast_select_fusion
  10.7 0.8 pad.8
  11.5 0.0 all-gather.2.cloned.1.call-update
  11.6 14.9 %copy.7 = bf16[4,60,32,960]{3,1,0,2:T(8,128)(2,1)S(1)} copy(bf16[4,60,32,960]{3,2,1,0:T(8,128)(2,1)} %bitcast.28) | data formatting | bytes 29491200 | tf_op jit(solution)/shard_map/reshape | solution.py:69
  26.4 7.4 %pad.9 = bf16[4,64,32,960]{3,1,0,2:T(8,128)(2,1)} pad(bf16[4,60,32,960]{3,1,0,2:T(8,128)(2,1)S(1)} %copy.7, bf16[]{:T(256)} %constant.45.clone.1), padding=0_0x0_4x0_0x0_0 | pad | bytes 30474242 | tf_op jit(solution)/shard_map/jit(_pad)/pad | solution.py:70
  33.8 0.0 copy-start
  33.8 0.0 slice-start
  33.8 21.0 %copy.8.vt_ref = bf16[32,960,256]{2,1,0:T(8,128)(2,1)} copy(bf16[32,960,256]{1,2,0:T(8,128)(2,1)} %bitcast.26) | data formatting | bytes 31457280 | tf_op jit(solution)/shard_map/reshape | solution.py:71
  54.8 0.0 copy-done
  54.8 0.0 slice-done
  54.8 0.1 compare_convert_fusion
  54.8 33.2 %all-gather.2.cloned.1.call-done.g_ref = bf16[2048,4096]{1,0:T(8,128)(2,1)} async-done(((bf16[64,4096]{1,0:T(8,128)(2,1)}), bf16[2048,4096]{1,0:T(8,128)(2,1)}) %all-gather.2.cloned.1.call-update) | async-done | bytes 16777232 | tf_op jit(solution)/shard_map/all_gather | solution.py:59
  88.0 22.9 %shard_map.46 = f32[960,1024]{1,0:T(8,128)S(1)} custom-call(bf16[32,960,256]{2,1,0:T(8,128)(2,1)} %copy.8.vt_ref, bf16[2048,4096]{1,0:T(8,128)(2,1)} %all-gather.2.cloned.1.call-done.g_ref), custom_call_target="tpu_custom_call" | custom-call | tf_op jit(solution)/shard_map/pallas_call | solution.py:35
  110.9 2.8 %copy.13 = f32[120,8,8,128]{3,2,1,0:T(8,128)} copy(f32[120,8,8,128]{3,1,2,0:T(8,128)S(1)} %bitcast.25) | data formatting | bytes 7864320
  113.7 5.5 %copy.9 = f32[4,240,8,128]{1,2,0,3:T(8,128)} copy(f32[4,240,8,128]{3,2,1,0:T(8,128)} %bitcast.29) | data formatting | bytes 7864320 | tf_op jit(solution)/shard_map/reshape | solution.py:73
  119.2 5.0 %multiply_bitcast_fusion = f32[8,128,4,240]{3,0,2,1:T(8,128)} fusion(f32[4,240,8,128]{1,2,0,3:T(8,128)} %copy.9, f32[240,8]{0,1:T(8,128)S(1)} %compare_convert_fusion), kind=kLoop, calls=%fused_computation.2 | loop fusion | flops 983040 | bytes 7872000 | tf_op jit(solution)/shard_map/transpose | solution.py:76
  124.2 5.5 %all-to-all-start = ((f32[8,128,4,240]{3,0,2,1:T(8,128)}), f32[8,128,4,240]{3,0,2,1:T(8,128)}, u32[]{:S(2)}, u32[]{:S(2)}) async-start(f32[8,128,4,240]{3,0,2,1:T(8,128)} %multiply_bitcast_fusion), calls=%async_computation | async-start | bytes 8388608 | tf_op jit(solution)/shard_map/all_to_all | solution.py:77
  129.7 0.2 reduce-scatter.2.cloned.1.call-start
  129.9 14.9 %fusion.3 = f32[2048,512]{1,0:T(8,128)} fusion(bf16[2048,4096]{1,0:T(8,128)(2,1)} %all-gather.2.cloned.1.call-done.g_ref, bf16[4096,512]{1,0:T(8,128)(2,1)} %param.6), kind=kOutput, calls=%fused_computation.15 | convolution fusion | flops 8589934592 | bytes 25165824 | tf_op jit(solution)/shard_map/dot_general | solution.py:65
  144.8 5.0 %reshape.116 = f32[8,240,512]{2,1,0:T(8,128)} reshape(f32[32,60,512]{2,1,0:T(8,128)} %bitcast.30) | data formatting | bytes 7864320 | tf_op jit(solution)/shard_map/reshape | solution.py:67
  149.8 30.6 %all-to-all-done = f32[8,128,4,240]{3,0,2,1:T(8,128)} async-done(((f32[8,128,4,240]{3,0,2,1:T(8,128)}), f32[8,128,4,240]{3,0,2,1:T(8,128)}, u32[]{:S(2)}, u32[]{:S(2)}) %all-to-all-start) | async-done | bytes 3932192 | tf_op jit(solution)/shard_map/all_to_all | solution.py:77
  180.4 4.7 %copy.10 = f32[8,4,32,4,240]{4,0,3,2,1:T(8,128)} copy(f32[8,4,32,4,240]{4,0,3,1,2:T(8,128)} %bitcast.8) | data formatting | bytes 7864320 | tf_op jit(solution)/shard_map/all_to_all | solution.py:77
  185.1 5.3 %copy.12 = f32[8,240,512]{2,1,0:T(8,128)} copy(f32[8,240,512]{1,0,2:T(8,128)} %bitcast.27) | data formatting | bytes 7864320 | tf_op jit(solution)/shard_map/reshape | solution.py:79
  190.4 6.1 %add.80 = f32[8,240,512]{2,1,0:T(8,128)} add(f32[8,240,512]{2,1,0:T(8,128)} %reshape.116, f32[8,240,512]{2,1,0:T(8,128)} %copy.12) | non-fusion elementwise | flops 983040 | bytes 11796480 | tf_op jit(solution)/shard_map/add | solution.py:80
  196.6 0.0 reduce-scatter.2.cloned.1.call-update
  196.6 44.2 %reduce-scatter.2.cloned.1.call-done = f32[2,240,512]{2,1,0:T(8,128)} async-done(((f32[8,240,512]{2,1,0:T(8,128)}), f32[2,240,512]{2,1,0:T(8,128)}) %reduce-scatter.2.cloned.1.call-update) | async-done | bytes 983056 | tf_op jit(solution)/shard_map/reduce_scatter | solution.py:81
  (4 shorter events, 0.0 us)
Async XLA Ops:
  6.5 81.5 %all-gather.2.cloned.1.call-start = ((), (), s32[]{:S(2)}) async-start(), calls=%async_computation.2 | async-start | bytes 17301504 | tf_op jit(solution)/shard_map/all_gather | solution.py:59
  33.8 21.0 %copy-start = (s32[240]{0:T(256)S(1)}, s32[240]{0:T(256)}, u32[]{:S(2)}) copy-start(s32[240]{0:T(256)} %param.4) | copy-start | bytes 2884
  33.8 21.0 %slice-start = ((s32[240]{0:T(256)}), s32[8]{0:T(128)S(1)}, s32[]{:S(2)}) async-start(s32[240]{0:T(256)} %param.4), calls=%async_computation.4 | async-start | bytes 1024 | tf_op jit(solution)/shard_map/slice | solution.py:74
  124.2 56.2 %all-to-all-start = ((f32[8,128,4,240]{3,0,2,1:T(8,128)}), f32[8,128,4,240]{3,0,2,1:T(8,128)}, u32[]{:S(2)}, u32[]{:S(2)}) async-start(f32[8,128,4,240]{3,0,2,1:T(8,128)} %multiply_bitcast_fusion), calls=%async_computation | async-start | bytes 8388608 | tf_op jit(solution)/shard_map/all_to_all | solution.py:77
  129.7 111.1 %reduce-scatter.2.cloned.1.call-start = ((), (), s32[]{:S(2)}) async-start(), calls=%async_computation.3 | async-start | bytes 4915200 | tf_op jit(solution)/shard_map/reduce_scatter | solution.py:81
Sparse Core Ops, SparseCore 0:
  11.7 76.2 all-gather.1
  196.7 44.0 reduce-scatter.1

commit v3 on v2

--- a/solution.py
+++ b/solution.py
@@ -20,13 +20,16 @@
         part = jnp.dot(vt_ref[c], rhs, preferred_element_type=jnp.float32)
         total = part if total is None else total + part
 
-    @pl.when(step == 0)
-    def _():
-        o_ref[...] = total
+    for i in range(window):
+        piece = total[:, i * vir_full:(i + 1) * vir_full]
 
-    @pl.when(step > 0)
-    def _():
-        o_ref[...] += total
+        @pl.when(step == 0)
+        def _():
+            o_ref[i] = piece
+
+        @pl.when(step > 0)
+        def _():
+            o_ref[i] += piece
 
 
 def cycle_matmul(vt, g, window, vir_full):
@@ -34,13 +37,13 @@
     steps = vir_part // C_STEP
     return pl.pallas_call(
         functools.partial(cycle_kernel, window, vir_full),
-        out_shape=jax.ShapeDtypeStruct((n_cols, window * vir_full), jnp.float32),
+        out_shape=jax.ShapeDtypeStruct((window, n_cols, vir_full), jnp.float32),
         grid=(steps,),
         in_specs=[
             pl.BlockSpec((C_STEP, n_cols, rows), lambda s: (s, 0, 0)),
             pl.BlockSpec((g.shape[0], C_STEP * vir_full), lambda s: (0, s)),
         ],
-        out_specs=pl.BlockSpec((n_cols, window * vir_full), lambda s: (0, 0)),
+        out_specs=pl.BlockSpec((window, n_cols, vir_full), lambda s: (0, 0, 0)),
         compiler_params=pltpu.CompilerParams(dimension_semantics=("arbitrary",), vmem_limit_bytes=48 * 1024 * 1024),
     )(vt, g)
 
@@ -70,15 +73,15 @@
     v4 = jnp.pad(v4, ((0, 0), (0, pad_rows - rows_local), (0, 0), (0, 0)))
     vt = jnp.transpose(v4, (2, 3, 0, 1)).reshape(vir_part, cycle_cols, per_i * pad_rows)
     cyc = cycle_matmul(vt, g2, window, vir_full)
-    cyc = cyc.reshape(vir_local, occ_count, window, vir_full)
     same_irrep = (occ_irrep[:window][:, None] == occ_irrep[None, :]).astype(jnp.float32)
-    cyc = cyc * jnp.transpose(same_irrep)[None, :, :, None]
-    cycle_term = jnp.transpose(cyc, (2, 3, 0, 1))
+    cyc = cyc.reshape(window, vir_local, occ_count, vir_full) * same_irrep[:, None, :, None]
+    cyc = lax.psum_scatter(cyc, "x", scatter_dimension=0, tiled=True)
+    rows_here = cyc.shape[0]
+    cycle_term = jnp.transpose(cyc, (0, 3, 1, 2))
     regrouped = lax.all_to_all(cycle_term, PAIR, split_axis=1, concat_axis=2, tiled=True)
-    rows_here = regrouped.shape[0]
     moved = jnp.transpose(regrouped, (0, 3, 1, 2)).reshape(rows_here, occ_count, vir_local * vir_full)
-    combined = ladder + moved
-    return lax.psum_scatter(combined, "x", scatter_dimension=0, tiled=True)
+    ladder = lax.psum_scatter(ladder, "x", scatter_dimension=0, tiled=True)
+    return ladder + moved
 
 
 def solution(mesh):

time: 249 us -> 214 us (0.86)
  waiting for transfers between devices: 108 us -> 76.1 us
  blocking collectives: 0 us -> 24.6 us
  local copies, waits for them, and re-layouts: 70.3 us -> 55.1 us
  other arithmetic: 12.4 us -> 5.79 us
  starting transfers between devices: 5.7 us -> 0.09 us
    all_to_all x1 -> x0, waiting for transfers between devices: 30.6 us -> none  [body(): lax.all_to_all(cycle_term, PAIR, split_axis=1, concat_axis=2, tiled=True)]
    all_to_all x0 -> x1, blocking collectives: none -> 24.6 us  [body(): lax.all_to_all(cycle_term, PAIR, split_axis=1, concat_axis=2, tiled=True)]
    reshape x1 -> x0, local copies, waits for them, and re-layouts: 5.52 us -> none  [body(): cyc = cyc.reshape(vir_local, occ_count, window, vir_full)]
    all_to_all x1 -> x0, starting transfers between devices: 5.48 us -> none  [body(): lax.all_to_all(cycle_term, PAIR, split_axis=1, concat_axis=2, tiled=True)]
    transpose x1 -> x0, other arithmetic: 4.99 us -> none  [body(): cycle_term = jnp.transpose(cyc, (2, 3, 0, 1))]
    reshape x1, local copies, waits for them, and re-layouts: 5.31 us -> 0.39 us  [body(): jnp.transpose(regrouped, (0, 3, 1, 2))]
    all_to_all x1, local copies, waits for them, and re-layouts: 4.72 us -> 0.41 us  [body(): lax.all_to_all(cycle_term, PAIR, split_axis=1, concat_axis=2, tiled=True)]
    add x1, other arithmetic: 6.14 us -> 2.34 us  [body(): return ladder + moved]
  transfers between devices with their start and end apart: 3 -> 3, of which waited for: 3 -> 3; matrix products, arithmetic and copies ran while one was open for 25% -> 31% of each run, Pallas kernels for 0% -> 0%
where the time goes in v3:
time: 214 us
  waiting for transfers between devices  76.1 us (36%)
  local copies, waits for them, and re-layouts  55.1 us (26%)
  blocking collectives  24.6 us (11%)
  Pallas kernels  23.9 us (11%)
  matrix products  14.9 us (7%)
  between operations  13.2 us (6%)
  other arithmetic  5.79 us (3%)
    all_gather x1, waiting for transfers between devices, body(): g2 = lax.all_gather(amp_pad, PAIR, axis=0, tiled=True)  33.1 us
    all_to_all x1, blocking collectives, body(): lax.all_to_all(cycle_term, PAIR, split_axis=1, concat_axis=2, tiled=True)  24.6 us
    pallas_call x1, Pallas kernels, cycle_matmul(): pl.pallas_call(functools.partial(cycle_kernel, window, vir_full), out_sha...  23.9 us
    reduce_scatter x1, waiting for transfers between devices, body(): cyc = lax.psum_scatter(cyc, 'x', scatter_dimension=0, tiled=True)  23.8 us
    reshape x1, local copies, waits for them, and re-layouts, body(): jnp.transpose(v4, (2, 3, 0, 1))  21 us
    reduce_scatter x1, waiting for transfers between devices, body(): ladder = lax.psum_scatter(ladder, 'x', scatter_dimension=0, tiled=True)  19.1 us
    reshape x1, local copies, waits for them, and re-layouts, body(): v4 = cycle_ints.reshape(per_i, rows_local, vir_part, cycle_cols)  14.9 us
    dot_general x1, matrix products, body(): ladder = jnp.dot(g2, ladder_ints, preferred_element_type=jnp.float32)  14.9 us
  transfers between devices with their start and end apart: 3, of which 3 were waited for; matrix products, arithmetic and copies ran while one was open for 31% of the time, Pallas kernels for 0%

profile of v3, /device:TPU:1, one launch (start us, length us, event | category | flops | bytes accessed | tf_op | source)
XLA Modules:
  0.0 213.6 jit_solution(13748076078099215043)
XLA Ops:
  6.5 0.0 all-gather.2.cloned.1.call-start
  6.6 1.5 gather_fusion
  8.1 1.5 gather_fusion.1
  9.5 1.1 broadcast_select_fusion
  10.7 0.8 pad.8
  11.5 0.0 all-gather.2.cloned.1.call-update
  11.6 0.0 reduce-scatter.5.cloned.1.call-start
  11.6 14.9 %copy.12 = bf16[4,60,32,960]{3,1,0,2:T(8,128)(2,1)S(1)} copy(bf16[4,60,32,960]{3,2,1,0:T(8,128)(2,1)} %bitcast.22) | data formatting | bytes 29491200 | tf_op jit(solution)/shard_map/reshape | solution.py:72
  26.5 7.4 %pad.9 = bf16[4,64,32,960]{3,1,0,2:T(8,128)(2,1)} pad(bf16[4,60,32,960]{3,1,0,2:T(8,128)(2,1)S(1)} %copy.12, bf16[]{:T(256)} %constant.45.clone.1), padding=0_0x0_4x0_0x0_0 | pad | bytes 30474242 | tf_op jit(solution)/shard_map/jit(_pad)/pad | solution.py:73
  33.9 0.0 copy-start
  33.9 0.0 slice-start
  33.9 21.0 %copy.13.vt_ref = bf16[32,960,256]{2,1,0:T(8,128)(2,1)} copy(bf16[32,960,256]{1,2,0:T(8,128)(2,1)} %bitcast.21) | data formatting | bytes 31457280 | tf_op jit(solution)/shard_map/reshape | solution.py:74
  54.8 0.0 copy-done
  54.8 0.0 slice-done
  54.8 0.1 compare_convert_fusion
  54.9 33.1 %all-gather.2.cloned.1.call-done.g_ref = bf16[2048,4096]{1,0:T(8,128)(2,1)} async-done(((bf16[64,4096]{1,0:T(8,128)(2,1)}), bf16[2048,4096]{1,0:T(8,128)(2,1)}) %all-gather.2.cloned.1.call-update) | async-done | bytes 16777232 | tf_op jit(solution)/shard_map/all_gather | solution.py:62
  88.0 23.9 %shard_map.46 = f32[8,960,128]{2,1,0:T(8,128)S(1)} custom-call(bf16[32,960,256]{2,1,0:T(8,128)(2,1)} %copy.13.vt_ref, bf16[2048,4096]{1,0:T(8,128)(2,1)} %all-gather.2.cloned.1.call-done.g_ref), custom_call_target="tpu_custom_call" | custom-call | tf_op jit(solution)/shard_map/pallas_call | solution.py:38
  111.9 2.2 %broadcast_multiply_fusion = f32[8,4,240,128]{3,2,1,0:T(8,128)} fusion(f32[8,4,240,128]{3,2,1,0:T(8,128)S(1)} %bitcast.20, f32[8,240]{1,0:T(8,128)S(1)} %compare_convert_fusion), kind=kLoop, calls=%fused_computation.2 | loop fusion | flops 983040 | bytes 7872000 | tf_op jit(solution)/shard_map/mul | solution.py:77
  114.1 0.0 reduce-scatter.5.cloned.1.call-update
  114.1 0.0 reduce-scatter.3.cloned.1.call-start
  114.1 14.9 %fusion.3 = f32[2048,512]{1,0:T(8,128)} fusion(bf16[2048,4096]{1,0:T(8,128)(2,1)} %all-gather.2.cloned.1.call-done.g_ref, bf16[4096,512]{1,0:T(8,128)(2,1)} %param.6), kind=kOutput, calls=%fused_computation.15 | convolution fusion | flops 8589934592 | bytes 25165824 | tf_op jit(solution)/shard_map/dot_general | solution.py:68
  129.0 5.0 %reshape.113 = f32[8,240,512]{2,1,0:T(8,128)} reshape(f32[32,60,512]{2,1,0:T(8,128)} %bitcast.23) | data formatting | bytes 7864320 | tf_op jit(solution)/shard_map/reshape | solution.py:70
  134.0 0.0 reduce-scatter.3.cloned.1.call-update
  134.0 23.8 %reduce-scatter.5.cloned.1.call-done = f32[2,4,240,128]{3,2,1,0:T(8,128)} async-done(((f32[8,4,240,128]{3,2,1,0:T(8,128)}), f32[2,4,240,128]{3,2,1,0:T(8,128)}) %reduce-scatter.5.cloned.1.call-update) | async-done | bytes 983056 | tf_op jit(solution)/shard_map/reduce_scatter | solution.py:78
  157.9 1.7 copy.14
  159.6 24.6 %all_to_all.18 = f32[2,128,4,240]{3,2,0,1:T(4,128)S(1)} all-to-all(f32[2,128,4,240]{3,2,0,1:T(4,128)S(1)} %copy.14), channel_id=1, replica_groups=mesh['z'=4,'y'=4,'core'=2,'x'=4] {'z','y','core'}, dimensions={1} | all-to-all | bytes 1966080 | tf_op jit(solution)/shard_map/all_to_all | solution.py:81
  184.2 0.4 copy.16
  184.6 0.6 copy.17
  185.1 0.4 reshape.117
  185.6 19.1 %reduce-scatter.3.cloned.1.call-done = f32[2,240,512]{2,1,0:T(8,128)} async-done(((f32[8,240,512]{2,1,0:T(8,128)}), f32[2,240,512]{2,1,0:T(8,128)}) %reduce-scatter.3.cloned.1.call-update) | async-done | bytes 983056 | tf_op jit(solution)/shard_map/reduce_scatter | solution.py:83
  204.7 2.3 %add.82 = f32[2,240,512]{2,1,0:T(8,128)} add(f32[2,240,512]{2,1,0:T(8,128)} %reduce-scatter.3.cloned.1.call-done, f32[2,240,512]{2,1,0:T(8,128)S(1)} %reshape.117) | non-fusion elementwise | flops 245760 | bytes 2949120 | tf_op jit(solution)/shard_map/add | solution.py:84
  (4 shorter events, 0.0 us)
Async XLA Ops:
  6.5 81.5 %all-gather.2.cloned.1.call-start = ((), (), s32[]{:S(2)}) async-start(), calls=%async_computation.3 | async-start | bytes 17301504 | tf_op jit(solution)/shard_map/all_gather | solution.py:62
  11.6 146.3 %reduce-scatter.5.cloned.1.call-start = ((), (), s32[]{:S(2)}) async-start(), calls=%async_computation.5 | async-start | bytes 4915200 | tf_op jit(solution)/shard_map/reduce_scatter | solution.py:78
  33.9 21.0 %copy-start = (s32[240]{0:T(256)S(1)}, s32[240]{0:T(256)}, u32[]{:S(2)}) copy-start(s32[240]{0:T(256)} %param.4) | copy-start | bytes 2884
  33.9 21.0 %slice-start = ((s32[240]{0:T(256)}), s32[8]{0:T(128)S(1)}, s32[]{:S(2)}) async-start(s32[240]{0:T(256)} %param.4), calls=%async_computation.6 | async-start | bytes 1024 | tf_op jit(solution)/shard_map/slice | solution.py:76
  114.1 90.6 %reduce-scatter.3.cloned.1.call-start = ((), (), s32[]{:S(2)}) async-start(), calls=%async_computation.4 | async-start | bytes 4915200 | tf_op jit(solution)/shard_map/reduce_scatter | solution.py:83
Sparse Core Ops, SparseCore 0:
  11.7 76.2 all-gather.1
  114.2 43.5 reduce-scatter.4
  160.3 44.3 reduce-scatter.2

commit v4 on v3

v4 whole, which is shorter than its diff:
```python
import functools
import jax
import jax.numpy as jnp
from jax import lax
from jax.experimental import pallas as pl
from jax.experimental.pallas import tpu as pltpu
from jax.sharding import Mesh, PartitionSpec as P

PAIR = ("z", "y", "core")
C_STEP = 4


def cycle_kernel(vir_full, vt_ref, g_ref, o_ref):
    step = pl.program_id(0)
    n_i = g_ref.shape[0]
    total = None
    for c in range(vt_ref.shape[0]):
        lanes = slice(c * vir_full, (c + 1) * vir_full)
        rhs = jnp.concatenate([g_ref[q, :, lanes] for q in range(n_i)], axis=1)
        part = jnp.dot(vt_ref[c], rhs, preferred_element_type=jnp.float32)
        total = part if total is None else total + part
    for q in range(n_i):
        piece = total[:, q * vir_full:(q + 1) * vir_full]

        @pl.when(step == 0)
        def _():
            o_ref[q] = piece

        @pl.when(step > 0)
        def _():
            o_ref[q] += piece


def cycle_matmul(vt, g4, parity, vir_full):
    vir_part, n_cols, rows = vt.shape
    n_i = g4.shape[0]
    steps = vir_part // C_STEP
    return pl.pallas_call(
        functools.partial(cycle_kernel, vir_full),
        out_shape=jax.ShapeDtypeStruct((n_i, n_cols, vir_full), jnp.float32),
        grid=(steps,),
        in_specs=[
            pl.BlockSpec((C_STEP, n_cols, rows), lambda s: (s, 0, 0)),
            pl.BlockSpec((n_i, None, rows, C_STEP * vir_full), lambda s: (0, parity, 0, s)),
        ],
        out_specs=pl.BlockSpec((n_i, n_cols, vir_full), lambda s: (0, 0, 0)),
        compiler_params=pltpu.CompilerParams(dimension_semantics=("arbitrary",), vmem_limit_bytes=48 * 1024 * 1024),
    )(vt, g4)


def body(occ_irrep, amplitudes, ladder_ints, cycle_ints):
    rows_local, cols_local = amplitudes.shape
    occ_count, vir_part, cycle_cols = cycle_ints.shape
    vir_full = cols_local // vir_part
    vir_local = cycle_cols // occ_count
    pad_rows = -(-rows_local // 16) * 16
    per_i = occ_count // rows_local
    pidx = lax.axis_index(PAIR)
    label_first = lax.dynamic_slice(occ_irrep, (pidx // per_i,), (1,))
    label_second = lax.dynamic_slice(occ_irrep, ((pidx % per_i) * rows_local,), (rows_local,))
    allowed = label_first == label_second
    amp_sym = jnp.where(allowed[:, None], amplitudes, jnp.zeros((), amplitudes.dtype))
    amp_pad = jnp.pad(amp_sym, ((0, pad_rows - rows_local), (0, 0)))
    g2 = lax.all_gather(amp_pad, PAIR, axis=0, tiled=True)
    n_blocks = g2.shape[0] // pad_rows
    window = n_blocks // per_i
    n_x = lax.axis_size("x")
    i_here = window // n_x

    v4 = cycle_ints.reshape(per_i, rows_local, vir_part, cycle_cols)
    v4 = jnp.pad(v4, ((0, 0), (0, pad_rows - rows_local), (0, 0), (0, 0)))
    vt = jnp.transpose(v4, (2, 3, 0, 1)).reshape(vir_part, cycle_cols, per_i * pad_rows)
    g4 = g2.reshape(n_x, i_here, per_i * pad_rows, cols_local)
    same_irrep = (occ_irrep[:window][:, None] == occ_irrep[None, :]).astype(jnp.float32)
    same4 = same_irrep.reshape(n_x, i_here, occ_count)

    moved_parts = []
    for parity in range(i_here):
        cyc = cycle_matmul(vt, g4, parity, vir_full)
        cyc = cyc.reshape(n_x, vir_local, occ_count, vir_full) * same4[:, parity, None, :, None]
        cyc = lax.psum_scatter(cyc, "x", scatter_dimension=0, tiled=True)
        cycle_term = jnp.transpose(cyc, (0, 3, 1, 2))
        regrouped = lax.all_to_all(cycle_term, PAIR, split_axis=1, concat_axis=2, tiled=True)
        moved_parts.append(jnp.transpose(regrouped, (0, 3, 1, 2)).reshape(1, occ_count, vir_local * vir_full))

    ladder = jnp.dot(g2, ladder_ints, preferred_element_type=jnp.float32)
    ladder = ladder.reshape(n_blocks, pad_rows, -1)[:, :rows_local, :]
    ladder = ladder.reshape(window, occ_count, vir_local * vir_full)
    ladder = lax.psum_scatter(ladder, "x", scatter_dimension=0, tiled=True)
    return ladder + jnp.concatenate(moved_parts, axis=0)


def solution(mesh):
    devs = mesh.devices
    n_pair, n_int = devs.shape
    fine = Mesh(devs.reshape(4, n_pair // 8, 2, n_int), ("z", "y", "core", "x"))
    placed = (P(), P(PAIR, "x"), P("x", PAIR), P(None, "x", PAIR))
    return jax.shard_map(body, mesh=fine, in_specs=placed, out_specs=P("x", None, PAIR), check_vma=False)
```

time: 214 us -> 220 us (1.028)
  blocking collectives: 24.6 us -> 0 us
  starting transfers between devices: 0.09 us -> 13.3 us
  waiting for transfers between devices: 76.1 us -> 83.3 us
  Pallas kernels: 23.9 us -> 29.6 us
    all_to_all x1 -> x0, blocking collectives: 24.6 us -> none  [body(): lax.all_to_all(cycle_term, PAIR, split_axis=1, concat_axis=2, tiled=True)]
    all_to_all x0 -> x2, starting transfers between devices: none -> 13.1 us  [body(): lax.all_to_all(cycle_term, PAIR, split_axis=1, concat_axis=2, tiled=True)]
    all_to_all x0 -> x2, waiting for transfers between devices: none -> 10.8 us  [body(): lax.all_to_all(cycle_term, PAIR, split_axis=1, concat_axis=2, tiled=True)]
    reduce_scatter x1 -> x2, waiting for transfers between devices: 23.8 us -> 14.6 us  [body(): cyc = lax.psum_scatter(cyc, 'x', scatter_dimension=0, tiled=True)]
    pallas_call x1 -> x2, Pallas kernels: 23.9 us -> 29.6 us  [cycle_matmul(): pl.pallas_call(functools.partial(cycle_kernel, vir_full), out_shape=jax.S...]
    reduce_scatter x1, waiting for transfers between devices: 19.1 us -> 24.9 us  [body(): ladder = lax.psum_scatter(ladder, 'x', scatter_dimension=0, tiled=True)]
    gather x2 -> x0, local copies, waits for them, and re-layouts: 2.95 us -> none  [the longest x1 1.47 us: body(): occ_irrep[global_row // occ_count] == occ_irrep[global_row % occ_count]]
    transpose x1 -> x2, local copies, waits for them, and re-layouts: 1.7 us -> 4.04 us  [body(): cycle_term = jnp.transpose(cyc, (0, 3, 1, 2))]
  transfers between devices with their start and end apart: 3 -> 6, of which waited for: 3 -> 4; matrix products, arithmetic and copies ran while one was open for 31% -> 32% of each run, Pallas kernels for 0% -> 7%
where the time goes in v4:
time: 220 us; the launch traced here: 218 us
  waiting for transfers between devices  83.3 us (38%)
  local copies, waits for them, and re-layouts  55.6 us (25%)
  Pallas kernels  29.6 us (13%)
  matrix products  15 us (7%)
  starting transfers between devices  13.3 us (6%)
  between operations  13.2 us (6%)
  other arithmetic  7.92 us (4%)
    all_gather x1, waiting for transfers between devices, body(): g2 = lax.all_gather(amp_pad, PAIR, axis=0, tiled=True)  32.9 us
    pallas_call x2, Pallas kernels, cycle_matmul(): pl.pallas_call(functools.partial(cycle_kernel, vir_full), out_shape=jax.S...  29.6 us
    reduce_scatter x1, waiting for transfers between devices, body(): ladder = lax.psum_scatter(ladder, 'x', scatter_dimension=0, tiled=True)  24.9 us
    reshape x1, local copies, waits for them, and re-layouts, body(): jnp.transpose(v4, (2, 3, 0, 1))  21 us
    dot_general x1, matrix products, body(): ladder = jnp.dot(g2, ladder_ints, preferred_element_type=jnp.float32)  15 us
    reshape x1, local copies, waits for them, and re-layouts, body(): v4 = cycle_ints.reshape(per_i, rows_local, vir_part, cycle_cols)  14.9 us
    reduce_scatter x2, waiting for transfers between devices, body(): cyc = lax.psum_scatter(cyc, 'x', scatter_dimension=0, tiled=True)  14.6 us
    all_to_all x2, starting transfers between devices, body(): lax.all_to_all(cycle_term, PAIR, split_axis=1, concat_axis=2, tiled=True)  13.1 us
  transfers between devices with their start and end apart: 6, of which 4 were waited for; matrix products, arithmetic and copies ran while one was open for 32% of the time, Pallas kernels for 7%

profile of v4, /device:TPU:1, one launch (start us, length us, event | category | flops | bytes accessed | tf_op | source)
XLA Modules:
  0.0 218.0 jit_solution(3946682122570544138)
XLA Ops:
  6.5 0.0 all-gather.2.cloned.1.call-start
  6.5 1.3 dynamic_slice.6
  7.8 1.4 dynamic-slice_compare_fusion
  9.2 1.1 broadcast_select_fusion
  10.4 0.8 pad.8
  11.2 0.0 all-gather.2.cloned.1.call-update
  11.2 0.0 reduce-scatter.6.cloned.1.call-start
  11.3 14.9 %copy.19 = bf16[4,60,32,960]{3,1,0,2:T(8,128)(2,1)S(1)} copy(bf16[4,60,32,960]{3,2,1,0:T(8,128)(2,1)} %bitcast.35) | data formatting | bytes 29491200 | tf_op jit(solution)/shard_map/reshape | solution.py:70
  26.1 7.4 %pad.9 = bf16[4,64,32,960]{3,1,0,2:T(8,128)(2,1)} pad(bf16[4,60,32,960]{3,1,0,2:T(8,128)(2,1)S(1)} %copy.19, bf16[]{:T(256)} %constant.50.clone.1), padding=0_0x0_4x0_0x0_0 | pad | bytes 30474242 | tf_op jit(solution)/shard_map/jit(_pad)/pad | solution.py:71
  33.5 0.0 slice-start
  33.5 0.0 copy-start
  33.5 21.0 %copy.20.vt_ref = bf16[32,960,256]{2,1,0:T(8,128)(2,1)} copy(bf16[32,960,256]{1,2,0:T(8,128)(2,1)} %bitcast.34) | data formatting | bytes 31457280 | tf_op jit(solution)/shard_map/reshape | solution.py:72
  54.5 0.0 slice-done
  54.5 0.1 eq.31
  54.5 0.1 copy.21
  54.6 0.0 copy-done
  54.6 0.1 compare_convert_fusion
  54.7 32.9 %all-gather.2.cloned.1.call-done = bf16[2048,4096]{1,0:T(8,128)(2,1)} async-done(((bf16[64,4096]{1,0:T(8,128)(2,1)}), bf16[2048,4096]{1,0:T(8,128)(2,1)}) %all-gather.2.cloned.1.call-update) | async-done | bytes 16777232 | tf_op jit(solution)/shard_map/all_gather | solution.py:64
  87.7 14.8 %shard_map.46 = f32[4,960,128]{2,1,0:T(8,128)S(1)} custom-call(bf16[32,960,256]{2,1,0:T(8,128)(2,1)} %copy.20.vt_ref, bf16[4,2,256,4096]{3,2,1,0:T(8,128)(2,1)} %bitcast.32), custom_call_target="tpu_custom_call" | custom-call | tf_op jit(solution)/shard_map/pallas_call | solution.py:38
  102.4 1.5 broadcast_multiply_fusion.1
  103.9 0.0 reduce-scatter.6.cloned.1.call-update
  104.0 0.0 reduce-scatter.8.cloned.1.call-start
  104.0 14.9 %shard_map.47 = f32[4,960,128]{2,1,0:T(8,128)S(1)} custom-call(bf16[32,960,256]{2,1,0:T(8,128)(2,1)} %copy.20.vt_ref, bf16[4,2,256,4096]{3,2,1,0:T(8,128)(2,1)} %bitcast.33), custom_call_target="tpu_custom_call" | custom-call | tf_op jit(solution)/shard_map/pallas_call | solution.py:38
  118.9 1.5 broadcast_multiply_fusion
  120.4 0.0 reduce-scatter.8.cloned.1.call-update
  120.4 0.0 reduce-scatter.4.cloned.1.call-start
  120.4 15.0 %fusion = f32[2048,512]{1,0:T(8,128)} fusion(bf16[2048,4096]{1,0:T(8,128)(2,1)} %all-gather.2.cloned.1.call-done, bf16[4096,512]{1,0:T(8,128)(2,1)} %param.6), kind=kOutput, calls=%fused_computation.8 | convolution fusion | flops 8589934592 | bytes 25165824 | tf_op jit(solution)/shard_map/dot_general | solution.py:86
  135.4 5.0 %reshape.50 = f32[8,240,512]{2,1,0:T(8,128)} reshape(f32[32,60,512]{2,1,0:T(8,128)} %bitcast.36) | data formatting | bytes 7864320 | tf_op jit(solution)/shard_map/reshape | solution.py:88
  140.4 0.0 reduce-scatter.4.cloned.1.call-update
  140.4 0.0 reduce-scatter.6.cloned.1.call-done
  140.4 2.0 copy.22
  142.5 5.4 %all-to-all-start = ((f32[1,128,4,240]{3,2,0,1:T(4,128)}), f32[1,128,4,240]{3,2,0,1:T(4,128)S(1)}, u32[]{:S(2)}, u32[]{:S(2)}) async-start(f32[1,128,4,240]{3,2,0,1:T(4,128)} %copy.22), calls=%async_computation.2 | async-start | bytes 1048576 | tf_op jit(solution)/shard_map/all_to_all | solution.py:83
  147.8 14.6 %reduce-scatter.8.cloned.1.call-done = f32[1,4,240,128]{3,2,1,0:T(8,128)} async-done(((f32[4,4,240,128]{3,2,1,0:T(8,128)}), f32[1,4,240,128]{3,2,1,0:T(8,128)}) %reduce-scatter.8.cloned.1.call-update) | async-done | bytes 491536 | tf_op jit(solution)/shard_map/reduce_scatter | solution.py:81
  162.4 2.0 copy.26
  164.5 0.0 all-to-all-done
  164.5 7.8 %all-to-all-start.1 = ((f32[1,128,4,240]{3,2,0,1:T(4,128)}), f32[1,128,4,240]{3,2,0,1:T(4,128)S(1)}, u32[]{:S(2)}, u32[]{:S(2)}) async-start(f32[1,128,4,240]{3,2,0,1:T(4,128)} %copy.26), calls=%async_computation.4 | async-start | bytes 1048576 | tf_op jit(solution)/shard_map/all_to_all | solution.py:83
  172.3 0.1 copy.23
  172.4 0.3 copy.24
  172.7 0.2 reshape.55
  172.9 10.8 %all-to-all-done.1 = f32[1,128,4,240]{3,2,0,1:T(4,128)S(1)} async-done(((f32[1,128,4,240]{3,2,0,1:T(4,128)}), f32[1,128,4,240]{3,2,0,1:T(4,128)S(1)}, u32[]{:S(2)}, u32[]{:S(2)}) %all-to-all-start.1) | async-done | bytes 491552 | tf_op jit(solution)/shard_map/all_to_all | solution.py:83
  183.7 0.1 copy.27
  183.8 0.3 copy.28
  184.1 0.2 reshape.57
  184.3 24.9 %reduce-scatter.4.cloned.1.call-done = f32[2,240,512]{2,1,0:T(8,128)} async-done(((f32[8,240,512]{2,1,0:T(8,128)}), f32[2,240,512]{2,1,0:T(8,128)}) %reduce-scatter.4.cloned.1.call-update) | async-done | bytes 983056 | tf_op jit(solution)/shard_map/reduce_scatter | solution.py:89
  209.2 2.3 %maximum_add_fusion = f32[2,240,512]{2,1,0:T(8,128)} fusion(f32[2,240,512]{2,1,0:T(8,128)} %reduce-scatter.4.cloned.1.call-done, f32[1,240,512]{2,1,0:T(8,128)S(1)} %reshape.57, f32[1,240,512]{2,1,0:T(8,128)S(1)} %reshape.55), kind=kLoop, calls=%fused_computation | loop fusion | flops 491520 | bytes 2949120 | tf_op jit(solution)/shard_map/add | solution.py:90
  (1 shorter events, 0.0 us)
Async XLA Ops:
  6.5 81.1 %all-gather.2.cloned.1.call-start = ((), (), s32[]{:S(2)}) async-start(), calls=%async_computation.5 | async-start | bytes 17301504 | tf_op jit(solution)/shard_map/all_gather | solution.py:64
  11.2 129.2 %reduce-scatter.6.cloned.1.call-start = ((), (), s32[]{:S(2)}) async-start(), calls=%async_computation.7 | async-start | bytes 2457600 | tf_op jit(solution)/shard_map/reduce_scatter | solution.py:81
  33.5 21.0 %slice-start = ((s32[240]{0:T(256)}), s32[8]{0:T(128)S(1)}, s32[]{:S(2)}) async-start(s32[240]{0:T(256)} %param.4), calls=%async_computation.9 | async-start | bytes 1024 | tf_op jit(solution)/shard_map/slice | solution.py:74
  33.5 21.1 %copy-start = (s32[240]{0:T(256)S(1)}, s32[240]{0:T(256)}, u32[]{:S(2)}) copy-start(s32[240]{0:T(256)} %param.4) | copy-start | bytes 2884
  104.0 58.5 %reduce-scatter.8.cloned.1.call-start = ((), (), s32[]{:S(2)}) async-start(), calls=%async_computation.8 | async-start | bytes 2457600 | tf_op jit(solution)/shard_map/reduce_scatter | solution.py:81
  120.4 88.8 %reduce-scatter.4.cloned.1.call-start = ((), (), s32[]{:S(2)}) async-start(), calls=%async_computation.6 | async-start | bytes 4915200 | tf_op jit(solution)/shard_map/reduce_scatter | solution.py:89
  142.5 22.0 %all-to-all-start = ((f32[1,128,4,240]{3,2,0,1:T(4,128)}), f32[1,128,4,240]{3,2,0,1:T(4,128)S(1)}, u32[]{:S(2)}, u32[]{:S(2)}) async-start(f32[1,128,4,240]{3,2,0,1:T(4,128)} %copy.22), calls=%async_computation.2 | async-start | bytes 1048576 | tf_op jit(solution)/shard_map/all_to_all | solution.py:83
  164.5 19.2 %all-to-all-start.1 = ((f32[1,128,4,240]{3,2,0,1:T(4,128)}), f32[1,128,4,240]{3,2,0,1:T(4,128)S(1)}, u32[]{:S(2)}, u32[]{:S(2)}) async-start(f32[1,128,4,240]{3,2,0,1:T(4,128)} %copy.26), calls=%async_computation.4 | async-start | bytes 1048576 | tf_op jit(solution)/shard_map/all_to_all | solution.py:83
Sparse Core Ops, SparseCore 0:
  11.3 76.2 all-gather.1
  104.1 27.5 reduce-scatter.5
  134.1 28.3 reduce-scatter.7
  164.7 44.4 reduce-scatter.3

commit v5 on v3

--- a/solution.py
+++ b/solution.py
@@ -48,22 +48,40 @@
     )(vt, g)
 
 
+def ring_reduce_scatter(blocks, axis):
+    n = lax.axis_size(axis)
+    me = lax.axis_index(axis)
+    per = blocks.shape[0] // n
+    blocks = blocks.reshape((n, per) + blocks.shape[1:])
+    half = per // 2
+    lo, hi = blocks[:, :half], blocks[:, half:]
+    fwd = [(j, (j + 1) % n) for j in range(n)]
+    bwd = [(j, (j - 1) % n) for j in range(n)]
+    acc_lo = lax.dynamic_index_in_dim(lo, (me - 1) % n, axis=0, keepdims=False)
+    acc_hi = lax.dynamic_index_in_dim(hi, (me + 1) % n, axis=0, keepdims=False)
+    for step in range(1, n):
+        acc_lo = lax.ppermute(acc_lo, axis, fwd) + lax.dynamic_index_in_dim(lo, (me - 1 - step) % n, axis=0, keepdims=False)
+        acc_hi = lax.ppermute(acc_hi, axis, bwd) + lax.dynamic_index_in_dim(hi, (me + 1 + step) % n, axis=0, keepdims=False)
+    return jnp.concatenate([acc_lo, acc_hi], axis=0)
+
+
 def body(occ_irrep, amplitudes, ladder_ints, cycle_ints):
     rows_local, cols_local = amplitudes.shape
     occ_count, vir_part, cycle_cols = cycle_ints.shape
     vir_full = cols_local // vir_part
     vir_local = cycle_cols // occ_count
     pad_rows = -(-rows_local // 16) * 16
+    per_i = occ_count // rows_local
     pidx = lax.axis_index(PAIR)
-    global_row = pidx * rows_local + jnp.arange(rows_local, dtype=jnp.int32)
-    allowed = occ_irrep[global_row // occ_count] == occ_irrep[global_row % occ_count]
+    label_first = lax.dynamic_slice(occ_irrep, (pidx // per_i,), (1,))
+    label_second = lax.dynamic_slice(occ_irrep, ((pidx % per_i) * rows_local,), (rows_local,))
+    allowed = label_first == label_second
     amp_sym = jnp.where(allowed[:, None], amplitudes, jnp.zeros((), amplitudes.dtype))
     amp_pad = jnp.pad(amp_sym, ((0, pad_rows - rows_local), (0, 0)))
     g2 = lax.all_gather(amp_pad, PAIR, axis=0, tiled=True)
     n_blocks = g2.shape[0] // pad_rows
     total_rows = n_blocks * rows_local
     window = total_rows // occ_count
-    per_i = n_blocks // window
 
     ladder = jnp.dot(g2, ladder_ints, preferred_element_type=jnp.float32)
     ladder = ladder.reshape(n_blocks, pad_rows, -1)[:, :rows_local, :]
@@ -80,7 +98,7 @@
     cycle_term = jnp.transpose(cyc, (0, 3, 1, 2))
     regrouped = lax.all_to_all(cycle_term, PAIR, split_axis=1, concat_axis=2, tiled=True)
     moved = jnp.transpose(regrouped, (0, 3, 1, 2)).reshape(rows_here, occ_count, vir_local * vir_full)
-    ladder = lax.psum_scatter(ladder, "x", scatter_dimension=0, tiled=True)
+    ladder = ring_reduce_scatter(ladder, "x")
     return ladder + moved
 
 

time: 214 us -> 219 us (1.023)
  blocking collectives: 24.6 us -> 0 us
  starting transfers between devices: 0.09 us -> 17 us
  other arithmetic: 5.79 us -> 15.2 us
  local copies, waits for them, and re-layouts: 55.1 us -> 58.3 us
    ppermute x0 -> x6, waiting for transfers between devices: none -> 42.1 us  [the longest x3 29.3 us: ring_reduce_scatter(): lax.ppermute(acc_hi, axis, bwd)]
    all_to_all x1 -> x0, blocking collectives: 24.6 us -> none  [body(): lax.all_to_all(cycle_term, PAIR, split_axis=1, concat_axis=2, tiled=True)]
    reduce_scatter x1, waiting for transfers between devices: 23.8 us -> 0.01 us  [body(): cyc = lax.psum_scatter(cyc, 'x', scatter_dimension=0, tiled=True)]
    reduce_scatter x1 -> x0, waiting for transfers between devices: 19.1 us -> none  [body(): ladder = lax.psum_scatter(ladder, 'x', scatter_dimension=0, tiled=True)]
    ppermute x0 -> x6, starting transfers between devices: none -> 9.99 us  [the longest x3 9.91 us: ring_reduce_scatter(): lax.ppermute(acc_hi, axis, bwd)]
    add x0 -> x6, other arithmetic: none -> 9.25 us  [the longest x3 5.65 us: ring_reduce_scatter(): lax.ppermute(acc_lo, axis, fwd)]
    all_to_all x0 -> x1, starting transfers between devices: none -> 6.95 us  [body(): lax.all_to_all(cycle_term, PAIR, split_axis=1, concat_axis=2, tiled=True)]
    reshape x1 -> x0, local copies, waits for them, and re-layouts: 4.98 us -> none  [body(): ladder = ladder.reshape(window, occ_count, vir_local * vir_full)]
  transfers between devices with their start and end apart: 3 -> 9, of which waited for: 3 -> 4; matrix products, arithmetic and copies ran while one was open for 31% -> 36% of each run, Pallas kernels for 0% -> 0%
where the time goes in v5:
time: 219 us; the launch traced here: 218 us
  waiting for transfers between devices  75.1 us (34%)
  local copies, waits for them, and re-layouts  58.3 us (27%)
  Pallas kernels  23.9 us (11%)
  starting transfers between devices  17 us (8%)
  other arithmetic  15.2 us (7%)
  matrix products  14.9 us (7%)
  between operations  13.6 us (6%)
    all_gather x1, waiting for transfers between devices, body(): g2 = lax.all_gather(amp_pad, PAIR, axis=0, tiled=True)  33 us
    ppermute x3, waiting for transfers between devices, ring_reduce_scatter(): lax.ppermute(acc_hi, axis, bwd)  29.3 us
    pallas_call x1, Pallas kernels, cycle_matmul(): pl.pallas_call(functools.partial(cycle_kernel, window, vir_full), out_sha...  23.9 us
    reshape x1, local copies, waits for them, and re-layouts, body(): jnp.transpose(v4, (2, 3, 0, 1))  21 us
    dot_general x1, matrix products, body(): ladder = jnp.dot(g2, ladder_ints, preferred_element_type=jnp.float32)  14.9 us
    reshape x1, local copies, waits for them, and re-layouts, body(): v4 = cycle_ints.reshape(per_i, rows_local, vir_part, cycle_cols)  14.9 us
    ppermute x3, waiting for transfers between devices, ring_reduce_scatter(): lax.ppermute(acc_lo, axis, fwd)  12.8 us
    ppermute x3, starting transfers between devices, ring_reduce_scatter(): lax.ppermute(acc_hi, axis, bwd)  9.91 us
  transfers between devices with their start and end apart: 9, of which 4 were waited for; matrix products, arithmetic and copies ran while one was open for 36% of the time, Pallas kernels for 0%

profile of v5, /device:TPU:1, one launch (start us, length us, event | category | flops | bytes accessed | tf_op | source)
XLA Modules:
  0.0 217.9 jit_solution(3091797995981088563)
XLA Ops:
  6.5 0.0 all-gather.2.cloned.1.call-start
  6.5 1.3 dynamic_slice.31
  7.8 1.4 dynamic-slice_compare_fusion
  9.2 1.1 broadcast_select_fusion
  10.4 0.8 pad.8
  11.2 0.0 all-gather.2.cloned.1.call-update
  11.2 0.0 reduce-scatter.2.cloned.1.call-start
  11.3 14.9 %copy.16 = bf16[4,60,32,960]{3,1,0,2:T(8,128)(2,1)S(1)} copy(bf16[4,60,32,960]{3,2,1,0:T(8,128)(2,1)} %bitcast.35) | data formatting | bytes 29491200 | tf_op jit(solution)/shard_map/reshape | solution.py:90
  26.1 7.4 %pad.9 = bf16[4,64,32,960]{3,1,0,2:T(8,128)(2,1)} pad(bf16[4,60,32,960]{3,1,0,2:T(8,128)(2,1)S(1)} %copy.16, bf16[]{:T(256)} %constant.114.clone.1), padding=0_0x0_4x0_0x0_0 | pad | bytes 30474242 | tf_op jit(solution)/shard_map/jit(_pad)/pad | solution.py:91
  33.6 21.0 %copy.17.vt_ref = bf16[32,960,256]{2,1,0:T(8,128)(2,1)} copy(bf16[32,960,256]{1,2,0:T(8,128)(2,1)} %bitcast.34) | data formatting | bytes 31457280 | tf_op jit(solution)/shard_map/reshape | solution.py:92
  54.6 0.0 copy-done.2
  54.6 0.0 slice-done
  54.6 0.1 compare_convert_fusion
  54.7 33.0 %all-gather.2.cloned.1.call-done.g_ref = bf16[2048,4096]{1,0:T(8,128)(2,1)} async-done(((bf16[64,4096]{1,0:T(8,128)(2,1)}), bf16[2048,4096]{1,0:T(8,128)(2,1)}) %all-gather.2.cloned.1.call-update) | async-done | bytes 16777232 | tf_op jit(solution)/shard_map/all_gather | solution.py:81
  87.7 23.9 %shard_map.46 = f32[8,960,128]{2,1,0:T(8,128)S(1)} custom-call(bf16[32,960,256]{2,1,0:T(8,128)(2,1)} %copy.17.vt_ref, bf16[2048,4096]{1,0:T(8,128)(2,1)} %all-gather.2.cloned.1.call-done.g_ref), custom_call_target="tpu_custom_call" | custom-call | tf_op jit(solution)/shard_map/pallas_call | solution.py:38
  111.5 2.2 %broadcast_multiply_fusion = f32[8,4,240,128]{3,2,1,0:T(8,128)} fusion(f32[8,4,240,128]{3,2,1,0:T(8,128)S(1)} %bitcast.33, f32[8,240]{1,0:T(8,128)S(1)} %compare_convert_fusion), kind=kLoop, calls=%fused_computation | loop fusion | flops 983040 | bytes 7872000 | tf_op jit(solution)/shard_map/mul | solution.py:95
  113.7 0.0 reduce-scatter.2.cloned.1.call-update
  113.8 14.9 %fusion.1 = f32[2048,512]{1,0:T(8,128)} fusion(bf16[2048,4096]{1,0:T(8,128)(2,1)} %all-gather.2.cloned.1.call-done.g_ref, bf16[4096,512]{1,0:T(8,128)(2,1)} %param.6), kind=kOutput, calls=%fused_computation.14 | convolution fusion | flops 8589934592 | bytes 25165824 | tf_op jit(solution)/shard_map/dot_general | solution.py:86
  128.7 5.0 %reshape_reshape.3 = f32[4,2,240,512]{3,2,1,0:T(8,128)} reshape(f32[32,60,512]{2,1,0:T(8,128)} %bitcast.36) | data formatting | bytes 7864320 | tf_op jit(solution)/shard_map/reshape;reshape | solution.py:55
  133.6 2.6 %fusion = (f32[4,1,240,512]{3,2,1,0:T(8,128)S(1)}, f32[4,1,240,512]{3,2,1,0:T(8,128)S(1)}) fusion(f32[4,2,240,512]{3,2,1,0:T(8,128)} %reshape_reshape.3), kind=kLoop, calls=%fused_computation.13 | loop fusion | bytes 7864320 | tf_op jit(solution)/shard_map/slice | solution.py:57
  136.2 0.0 copy-start
  136.2 1.3 copy-done
  137.5 2.5 %collective-permute-start.3 = (f32[1,240,512]{2,1,0:T(8,128)S(1)}, f32[1,240,512]{2,1,0:T(8,128)S(1)}, u32[]{:S(2)}, u32[]{:S(2)}) collective-permute-start(f32[1,240,512]{2,1,0:T(8,128)S(1)} %dynamic-slice_bitcast_fusion), channel_id=1, source_target_pairs={{0,3},{1,0},{2,1},{3,2},{4,7},{5,4},{6,5},{7,6},{8,11},{9,8},{10,9... | collective-permute-start | bytes 1474568 | tf_op jit(solution)/shard_map/ppermute | solution.py:64
  140.1 0.1 collective-permute-start
  140.2 21.4 %collective-permute-done.3 = f32[1,240,512]{2,1,0:T(8,128)S(1)} collective-permute-done((f32[1,240,512]{2,1,0:T(8,128)S(1)}, f32[1,240,512]{2,1,0:T(8,128)S(1)}, u32[]{:S(2)}, u32[]{:S(2)}) %collective-permute-start.3) | collective-permute-done | bytes 491552 | tf_op jit(solution)/shard_map/ppermute | solution.py:64
  161.6 1.1 bitcast_add_fusion.2
  162.7 3.6 %collective-permute-start.4 = (f32[1,240,512]{2,1,0:T(8,128)S(1)}, f32[1,240,512]{2,1,0:T(8,128)}, u32[]{:S(2)}, u32[]{:S(2)}) collective-permute-start(f32[1,240,512]{2,1,0:T(8,128)S(1)} %bitcast_add_fusion.2), channel_id=1, source_target_pairs={{0,3},{1,0},{2,1},{3,2},{4,7},{5,4},{6,5},{7,6},{8,11},{9,8},{10,9... | collective-permute-start | bytes 1474568 | tf_op jit(solution)/shard_map/ppermute | solution.py:64
  166.3 0.0 collective-permute-done
  166.3 1.9 bitcast_add_fusion.5
  168.2 0.0 collective-permute-start.1
  168.2 7.9 %collective-permute-done.4 = f32[1,240,512]{2,1,0:T(8,128)} collective-permute-done((f32[1,240,512]{2,1,0:T(8,128)S(1)}, f32[1,240,512]{2,1,0:T(8,128)}, u32[]{:S(2)}, u32[]{:S(2)}) %collective-permute-start.4) | collective-permute-done | bytes 491552 | tf_op jit(solution)/shard_map/ppermute | solution.py:64
  176.1 1.3 bitcast_add_fusion.1
  177.4 3.8 %collective-permute-start.5 = (f32[1,240,512]{2,1,0:T(8,128)S(1)}, f32[1,240,512]{2,1,0:T(8,128)}, u32[]{:S(2)}, u32[]{:S(2)}) collective-permute-start(f32[1,240,512]{2,1,0:T(8,128)S(1)} %bitcast_add_fusion.1), channel_id=1, source_target_pairs={{0,3},{1,0},{2,1},{3,2},{4,7},{5,4},{6,5},{7,6},{8,11},{9,8},{10,9... | collective-permute-start | bytes 1474568 | tf_op jit(solution)/shard_map/ppermute | solution.py:64
  181.1 2.6 %copy.18 = f32[2,128,4,240]{3,2,0,1:T(4,128)} copy(f32[2,128,4,240]{1,3,2,0:T(8,128)} %bitcast.39) | data formatting | bytes 1966080 | tf_op jit(solution)/shard_map/transpose | solution.py:98
  183.7 6.9 %all-to-all-start = ((f32[2,128,4,240]{3,2,0,1:T(4,128)}), f32[2,128,4,240]{3,2,0,1:T(4,128)S(1)}, u32[]{:S(2)}, u32[]{:S(2)}) async-start(f32[2,128,4,240]{3,2,0,1:T(4,128)} %copy.18), calls=%async_computation.1 | async-start | bytes 2097152 | tf_op jit(solution)/shard_map/all_to_all | solution.py:99
  190.7 0.0 collective-permute-done.1
  190.7 1.9 bitcast_add_fusion.4
  192.6 0.0 collective-permute-start.2
  192.6 0.0 collective-permute-done.5
  192.6 1.3 bitcast_add_fusion
  193.8 12.8 %collective-permute-done.2 = f32[1,240,512]{2,1,0:T(8,128)} collective-permute-done((f32[1,240,512]{2,1,0:T(8,128)}, f32[1,240,512]{2,1,0:T(8,128)}, u32[]{:S(2)}, u32[]{:S(2)}) %collective-permute-start.2) | collective-permute-done | bytes 491552 | tf_op jit(solution)/shard_map/ppermute | solution.py:63
  206.6 1.9 bitcast_add_fusion.3
  208.5 0.0 all-to-all-done
  208.5 0.4 copy.20
  208.9 0.6 copy.21
  209.5 0.4 reshape.47
  209.9 0.0 copy-done.1
  209.9 1.1 maximum_add_fusion
  (6 shorter events, 0.1 us)
Async XLA Ops:
  6.5 81.1 %all-gather.2.cloned.1.call-start = ((), (), s32[]{:S(2)}) async-start(), calls=%async_computation.2 | async-start | bytes 17301504 | tf_op jit(solution)/shard_map/all_gather | solution.py:81
  11.2 169.9 %reduce-scatter.2.cloned.1.call-start = ((), (), s32[]{:S(2)}) async-start(), calls=%async_computation.3 | async-start | bytes 4915200 | tf_op jit(solution)/shard_map/reduce_scatter | solution.py:96
  33.5 21.0 %copy-start.2 = (s32[240]{0:T(256)S(1)}, s32[240]{0:T(256)}, u32[]{:S(2)}) copy-start(s32[240]{0:T(256)} %param.4) | copy-start | bytes 2884
  33.6 21.0 %slice-start = ((s32[240]{0:T(256)}), s32[8]{0:T(128)S(1)}, s32[]{:S(2)}) async-start(s32[240]{0:T(256)} %param.4), calls=%async_computation.4 | async-start | bytes 1024 | tf_op jit(solution)/shard_map/slice | solution.py:94
  136.2 1.3 copy-start
  137.5 24.1 %collective-permute-start.3 = (f32[1,240,512]{2,1,0:T(8,128)S(1)}, f32[1,240,512]{2,1,0:T(8,128)S(1)}, u32[]{:S(2)}, u32[]{:S(2)}) collective-permute-start(f32[1,240,512]{2,1,0:T(8,128)S(1)} %dynamic-slice_bitcast_fusion), channel_id=1, source_target_pairs={{0,3},{1,0},{2,1},{3,2},{4,7},{5,4},{6,5},{7,6},{8,11},{9,8},{10,9... | collective-permute-start | bytes 1474568 | tf_op jit(solution)/shard_map/ppermute | solution.py:64
  140.1 26.2 %collective-permute-start = (f32[1,240,512]{2,1,0:T(8,128)S(1)}, f32[1,240,512]{2,1,0:T(8,128)}, u32[]{:S(2)}, u32[]{:S(2)}) collective-permute-start(f32[1,240,512]{2,1,0:T(8,128)S(1)} %dynamic-slice_bitcast_fusion.1), channel_id=1, source_target_pairs={{0,1},{1,2},{2,3},{3,0},{4,5},{5,6},{6,7},{7,4},{8,9},{9,10},{10,1... | collective-permute-start | bytes 1474568 | tf_op jit(solution)/shard_map/ppermute | solution.py:63
  162.7 13.4 %collective-permute-start.4 = (f32[1,240,512]{2,1,0:T(8,128)S(1)}, f32[1,240,512]{2,1,0:T(8,128)}, u32[]{:S(2)}, u32[]{:S(2)}) collective-permute-start(f32[1,240,512]{2,1,0:T(8,128)S(1)} %bitcast_add_fusion.2), channel_id=1, source_target_pairs={{0,3},{1,0},{2,1},{3,2},{4,7},{5,4},{6,5},{7,6},{8,11},{9,8},{10,9... | collective-permute-start | bytes 1474568 | tf_op jit(solution)/shard_map/ppermute | solution.py:64
  168.2 22.5 %collective-permute-start.1 = (f32[1,240,512]{2,1,0:T(8,128)}, f32[1,240,512]{2,1,0:T(8,128)}, u32[]{:S(2)}, u32[]{:S(2)}) collective-permute-start(f32[1,240,512]{2,1,0:T(8,128)} %bitcast_add_fusion.5), channel_id=1, source_target_pairs={{0,1},{1,2},{2,3},{3,0},{4,5},{5,6},{6,7},{7,4},{8,9},{9,10},{10,1... | collective-permute-start | bytes 1474568 | tf_op jit(solution)/shard_map/ppermute | solution.py:63
  177.4 15.2 %collective-permute-start.5 = (f32[1,240,512]{2,1,0:T(8,128)S(1)}, f32[1,240,512]{2,1,0:T(8,128)}, u32[]{:S(2)}, u32[]{:S(2)}) collective-permute-start(f32[1,240,512]{2,1,0:T(8,128)S(1)} %bitcast_add_fusion.1), channel_id=1, source_target_pairs={{0,3},{1,0},{2,1},{3,2},{4,7},{5,4},{6,5},{7,6},{8,11},{9,8},{10,9... | collective-permute-start | bytes 1474568 | tf_op jit(solution)/shard_map/ppermute | solution.py:64
  183.7 24.8 %all-to-all-start = ((f32[2,128,4,240]{3,2,0,1:T(4,128)}), f32[2,128,4,240]{3,2,0,1:T(4,128)S(1)}, u32[]{:S(2)}, u32[]{:S(2)}) async-start(f32[2,128,4,240]{3,2,0,1:T(4,128)} %copy.18), calls=%async_computation.1 | async-start | bytes 2097152 | tf_op jit(solution)/shard_map/all_to_all | solution.py:99
  192.6 14.1 %collective-permute-start.2 = (f32[1,240,512]{2,1,0:T(8,128)}, f32[1,240,512]{2,1,0:T(8,128)}, u32[]{:S(2)}, u32[]{:S(2)}) collective-permute-start(f32[1,240,512]{2,1,0:T(8,128)} %bitcast_add_fusion.4), channel_id=1, source_target_pairs={{0,1},{1,2},{2,3},{3,0},{4,5},{5,6},{6,7},{7,4},{8,9},{9,10},{10,1... | collective-permute-start | bytes 1474568 | tf_op jit(solution)/shard_map/ppermute | solution.py:63
  208.5 1.4 copy-start.1
Sparse Core Ops, SparseCore 0:
  11.3 76.2 all-gather.1
  113.9 54.1 reduce-scatter.1

commit v6 on v3

v6 whole, which is shorter than its diff:
```python
import functools
import jax
import jax.numpy as jnp
from jax import lax
from jax.experimental import pallas as pl
from jax.experimental.pallas import tpu as pltpu
from jax.sharding import Mesh, PartitionSpec as P

PAIR = ("z", "y", "core")
C_STEP = 4
N_CHUNKS = 2


def cycle_kernel(window, vir_full, vt_ref, g_ref, *refs):
    o_ref = refs[-1]
    init_ref = refs[0] if len(refs) == 2 else None
    step = pl.program_id(0)
    rows = vt_ref.shape[2]
    total = None
    for c in range(vt_ref.shape[0]):
        lanes = slice(c * vir_full, (c + 1) * vir_full)
        rhs = jnp.concatenate([g_ref[i * rows:(i + 1) * rows, lanes] for i in range(window)], axis=1)
        part = jnp.dot(vt_ref[c], rhs, preferred_element_type=jnp.float32)
        total = part if total is None else total + part
    for i in range(window):
        piece = total[:, i * vir_full:(i + 1) * vir_full]

        @pl.when(step == 0)
        def _():
            if init_ref is None:
                o_ref[i] = piece
            else:
                o_ref[i] = init_ref[i] + piece

        @pl.when(step > 0)
        def _():
            o_ref[i] += piece


def cycle_matmul(vt, g, window, vir_full, init=None):
    vir_part, n_cols, rows = vt.shape
    steps = vir_part // C_STEP
    out_block = pl.BlockSpec((window, n_cols, vir_full), lambda s: (0, 0, 0))
    in_specs = [
        pl.BlockSpec((C_STEP, n_cols, rows), lambda s: (s, 0, 0)),
        pl.BlockSpec((g.shape[0], C_STEP * vir_full), lambda s: (0, s)),
    ]
    operands = [vt, g]
    aliases = {}
    if init is not None:
        in_specs.append(out_block)
        operands.append(init)
        aliases = {2: 0}
    return pl.pallas_call(
        functools.partial(cycle_kernel, window, vir_full),
        out_shape=jax.ShapeDtypeStruct((window, n_cols, vir_full), jnp.float32),
        grid=(steps,),
        in_specs=in_specs,
        out_specs=out_block,
        input_output_aliases=aliases,
        compiler_params=pltpu.CompilerParams(dimension_semantics=("arbitrary",), vmem_limit_bytes=48 * 1024 * 1024),
    )(*operands)


def body(occ_irrep, amplitudes, ladder_ints, cycle_ints):
    rows_local, cols_local = amplitudes.shape
    occ_count, vir_part, cycle_cols = cycle_ints.shape
    vir_full = cols_local // vir_part
    vir_local = cycle_cols // occ_count
    pad_rows = -(-rows_local // 16) * 16
    per_i = occ_count // rows_local
    pidx = lax.axis_index(PAIR)
    label_first = lax.dynamic_slice(occ_irrep, (pidx // per_i,), (1,))
    label_second = lax.dynamic_slice(occ_irrep, ((pidx % per_i) * rows_local,), (rows_local,))
    allowed = label_first == label_second
    amp_sym = jnp.where(allowed[:, None], amplitudes, jnp.zeros((), amplitudes.dtype))
    amp_pad = jnp.pad(amp_sym, ((0, pad_rows - rows_local), (0, 0)))
    chunk_cols = cols_local // N_CHUNKS
    chunk_c = vir_part // N_CHUNKS
    gathered = [
        lax.all_gather(amp_pad[:, q * chunk_cols:(q + 1) * chunk_cols], PAIR, axis=0, tiled=True)
        for q in range(N_CHUNKS)
    ]
    n_blocks = gathered[0].shape[0] // pad_rows
    total_rows = n_blocks * rows_local
    window = total_rows // occ_count

    v4 = cycle_ints.reshape(per_i, rows_local, vir_part, cycle_cols)
    v4 = jnp.pad(v4, ((0, 0), (0, pad_rows - rows_local), (0, 0), (0, 0)))
    vt = jnp.transpose(v4, (2, 3, 0, 1)).reshape(vir_part, cycle_cols, per_i * pad_rows)

    cyc = None
    ladder = None
    for q in range(N_CHUNKS):
        cyc = cycle_matmul(vt[q * chunk_c:(q + 1) * chunk_c], gathered[q], window, vir_full, cyc)
        part = jnp.dot(gathered[q], ladder_ints[q * chunk_cols:(q + 1) * chunk_cols],
                       preferred_element_type=jnp.float32)
        ladder = part if ladder is None else ladder + part

    same_irrep = (occ_irrep[:window][:, None] == occ_irrep[None, :]).astype(jnp.float32)
    cyc = cyc.reshape(window, vir_local, occ_count, vir_full) * same_irrep[:, None, :, None]
    cyc = lax.psum_scatter(cyc, "x", scatter_dimension=0, tiled=True)
    rows_here = cyc.shape[0]
    cycle_term = jnp.transpose(cyc, (0, 3, 1, 2))
    regrouped = lax.all_to_all(cycle_term, PAIR, split_axis=1, concat_axis=2, tiled=True)
    moved = jnp.transpose(regrouped, (0, 3, 1, 2)).reshape(rows_here, occ_count, vir_local * vir_full)

    ladder = ladder.reshape(n_blocks, pad_rows, -1)[:, :rows_local, :]
    ladder = ladder.reshape(window, occ_count, vir_local * vir_full)
    ladder = lax.psum_scatter(ladder, "x", scatter_dimension=0, tiled=True)
    return ladder + moved


def solution(mesh):
    devs = mesh.devices
    n_pair, n_int = devs.shape
    fine = Mesh(devs.reshape(4, n_pair // 8, 2, n_int), ("z", "y", "core", "x"))
    placed = (P(), P(PAIR, "x"), P("x", PAIR), P(None, "x", PAIR))
    return jax.shard_map(body, mesh=fine, in_specs=placed, out_specs=P("x", None, PAIR), check_vma=False)
```

time: 214 us -> 241 us (1.13)
  waiting for transfers between devices: 76.1 us -> 87.7 us
  local copies, waits for them, and re-layouts: 55.1 us -> 62.7 us
  matrix products: 14.9 us -> 17.7 us
    slice x0 -> x4, local copies, waits for them, and re-layouts: none -> 31.3 us  [the longest x3 30.4 us: body(): vt[q * chunk_c:(q + 1) * chunk_c]]
    reshape x1 -> x0, local copies, waits for them, and re-layouts: 21 us -> none  [body(): jnp.transpose(v4, (2, 3, 0, 1))]
    all_gather x1 -> x2, waiting for transfers between devices: 33.1 us -> 47.1 us  [body(): lax.all_gather(amp_pad[:, q * chunk_cols:(q + 1) * chunk_cols], PAIR, axi...]
    pad x2 -> x0, local copies, waits for them, and re-layouts: 8.22 us -> none  [the longest x1 7.39 us: body(): v4 = jnp.pad(v4, ((0, 0), (0, pad_rows - rows_local), (0, 0), (0, 0)))]
    unnamed x2 -> x8, local copies, waits for them, and re-layouts: 0.01 us -> 3.97 us
    transpose x0 -> x1, local copies, waits for them, and re-layouts: none -> 3.28 us  [body(): jnp.transpose(v4, (2, 3, 0, 1))]
    reduce_scatter x1, waiting for transfers between devices: 23.8 us -> 20.9 us  [body(): cyc = lax.psum_scatter(cyc, 'x', scatter_dimension=0, tiled=True)]
    gather x2 -> x0, local copies, waits for them, and re-layouts: 2.95 us -> none  [the longest x1 1.47 us: body(): occ_irrep[global_row // occ_count] == occ_irrep[global_row % occ_count]]
  transfers between devices with their start and end apart: 3 -> 4, of which waited for: 3 -> 4; matrix products, arithmetic and copies ran while one was open for 31% -> 31% of each run, Pallas kernels for 0% -> 5%
where the time goes in v6:
time: 241 us; the launch traced here: 240 us
  waiting for transfers between devices  87.7 us (36%)
  local copies, waits for them, and re-layouts  62.7 us (26%)
  Pallas kernels  26.3 us (11%)
  blocking collectives  24.6 us (10%)
  matrix products  17.7 us (7%)
  between operations  13.2 us (5%)
  other arithmetic  7.13 us (3%)
    all_gather x2, waiting for transfers between devices, body(): lax.all_gather(amp_pad[:, q * chunk_cols:(q + 1) * chunk_cols], PAIR, axi...  47.1 us
    slice x3, local copies, waits for them, and re-layouts, body(): vt[q * chunk_c:(q + 1) * chunk_c]  30.4 us
    pallas_call x2, Pallas kernels, cycle_matmul(): pl.pallas_call(functools.partial(cycle_kernel, window, vir_full), out_sha...  26.3 us
    all_to_all x1, blocking collectives, body(): lax.all_to_all(cycle_term, PAIR, split_axis=1, concat_axis=2, tiled=True)  24.6 us
    reduce_scatter x1, waiting for transfers between devices, body(): cyc = lax.psum_scatter(cyc, 'x', scatter_dimension=0, tiled=True)  20.9 us
    reduce_scatter x1, waiting for transfers between devices, body(): ladder = lax.psum_scatter(ladder, 'x', scatter_dimension=0, tiled=True)  19 us
    dot_general x2, matrix products, body(): jnp.dot(gathered[q], ladder_ints[q * chunk_cols:(q + 1) * chunk_cols], pr...  17.7 us
    reshape x1, local copies, waits for them, and re-layouts, body(): v4 = cycle_ints.reshape(per_i, rows_local, vir_part, cycle_cols)  14.9 us
  transfers between devices with their start and end apart: 4, of which 4 were waited for; matrix products, arithmetic and copies ran while one was open for 31% of the time, Pallas kernels for 5%

profile of v6, /device:TPU:1, one launch (start us, length us, event | category | flops | bytes accessed | tf_op | source)
XLA Modules:
  0.0 239.6 jit_solution(17110126382599930864)
XLA Ops:
  6.5 0.0 all-gather.3.cloned.1.call-start
  6.5 1.3 dynamic_slice.6
  7.8 1.4 dynamic-slice_compare_fusion
  9.2 1.1 broadcast_select_fusion
  10.4 0.8 pad_slice_fusion
  11.2 0.0 all-gather.3.cloned.1.call-update
  11.2 0.0 all-gather.5.cloned.1.call-start
  11.3 0.7 all-gather.5.cloned.1.call-update
  12.0 0.0 reduce-scatter.5.cloned.1.call-start
  12.0 14.9 %copy.14 = bf16[4,60,32,960]{3,1,0,2:T(8,128)(2,1)S(1)} copy(bf16[4,60,32,960]{3,2,1,0:T(8,128)(2,1)} %bitcast.21) | data formatting | bytes 29491200 | tf_op jit(solution)/shard_map/reshape | solution.py:88
  26.9 3.3 %pad_bitcast_fusion = bf16[32,960,4,64]{1,3,2,0:T(8,128)(2,1)S(1)} fusion(bf16[4,60,32,960]{3,1,0,2:T(8,128)(2,1)S(1)} %copy.14), kind=kLoop, calls=%fused_computation | loop fusion | bytes 30474240 | tf_op jit(solution)/shard_map/transpose | solution.py:90
  30.2 6.3 %fusion.3 = (bf16[16,960,4,64]{1,3,2,0:T(8,128)(2,1)}, bf16[16,960,4,64]{1,3,2,0:T(8,128)(2,1)}) fusion(bf16[32,960,4,64]{1,3,2,0:T(8,128)(2,1)S(1)} %pad_bitcast_fusion), kind=kLoop, calls=%fused_computation.11 | loop fusion | bytes 31457280 | tf_op jit(solution)/shard_map/slice | solution.py:95
  36.5 11.8 %copy.15.vt_ref = bf16[16,960,256]{2,1,0:T(8,128)(2,1)} copy(bf16[16,960,256]{1,2,0:T(8,128)(2,1)} %bitcast.20) | data formatting | bytes 15728640 | tf_op jit(solution)/shard_map/slice | solution.py:95
  48.3 0.0 copy-start.2
  48.3 0.0 slice-start
  48.3 12.3 %copy.16.vt_ref = bf16[16,960,256]{2,1,0:T(8,128)(2,1)} copy(bf16[16,960,256]{1,2,0:T(8,128)(2,1)} %bitcast.19) | data formatting | bytes 15728640 | tf_op jit(solution)/shard_map/slice | solution.py:95
  60.6 0.0 copy-done.2
  60.6 0.0 slice-done
  60.6 0.1 compare_convert_fusion
  60.7 7.2 %all-gather.3.cloned.1.call-done.g_ref = bf16[2048,2048]{1,0:T(8,128)(2,1)} async-done(((bf16[64,2048]{1,0:T(8,128)(2,1)}), bf16[2048,2048]{1,0:T(8,128)(2,1)}) %all-gather.3.cloned.1.call-update) | async-done | bytes 8388624 | tf_op jit(solution)/shard_map/all_gather | solution.py:81
  67.9 12.9 %shard_map.46.refs_0_ = f32[8,960,128]{2,1,0:T(8,128)S(1)} custom-call(bf16[16,960,256]{2,1,0:T(8,128)(2,1)} %copy.15.vt_ref, bf16[2048,2048]{1,0:T(8,128)(2,1)} %all-gather.3.cloned.1.call-done.g_ref), custom_call_target="tpu_custom_call" | custom-call | tf_op jit(solution)/shard_map/pallas_call | solution.py:54
  80.8 0.0 copy-start
  80.8 1.8 copy-done
  82.6 39.9 %all-gather.5.cloned.1.call-done.g_ref = bf16[2048,2048]{1,0:T(8,128)(2,1)} async-done(((bf16[64,2048]{1,0:T(8,128)(2,1)}), bf16[2048,2048]{1,0:T(8,128)(2,1)}) %all-gather.5.cloned.1.call-update) | async-done | bytes 8388624 | tf_op jit(solution)/shard_map/all_gather | solution.py:81
  122.5 0.0 copy-start.1
  122.5 2.1 copy-done.1
  124.6 13.3 %shard_map.47 = f32[8,960,128]{2,1,0:T(8,128)S(1)} custom-call(bf16[16,960,256]{2,1,0:T(8,128)(2,1)} %copy.16.vt_ref, bf16[2048,2048]{1,0:T(8,128)(2,1)} %all-gather.5.cloned.1.call-done.g_ref, f32[8,960,128]{2,1,0:T(8,128)S(1)} %copy-done.1), custom_call_target="tpu_custom_call", output_to_operand_aliasing={{}: (2, {})} | custom-call | tf_op jit(solution)/shard_map/pallas_call | solution.py:54
  138.0 2.2 broadcast_multiply_fusion
  140.1 0.0 reduce-scatter.5.cloned.1.call-update
  140.2 0.2 reduce-scatter.3.cloned.1.call-start
  140.4 0.0 copy-start.3
  140.4 7.7 %fusion.1 = f32[2048,512]{1,0:T(8,128)S(1)} fusion(bf16[2048,2048]{1,0:T(8,128)(2,1)} %all-gather.3.cloned.1.call-done.g_ref, bf16[4096,512]{1,0:T(8,128)(2,1)} %param.6), kind=kOutput, calls=%fused_computation.3 | convolution fusion | flops 4294967296 | bytes 14680064 | tf_op jit(solution)/shard_map/dot_general | solution.py:96
  148.1 0.0 copy-done.3
  148.1 10.0 %convolution_add_fusion = f32[2048,512]{1,0:T(8,128)} fusion(f32[2048,512]{1,0:T(8,128)S(1)} %fusion.1, bf16[2048,2048]{1,0:T(8,128)(2,1)} %all-gather.5.cloned.1.call-done.g_ref, bf16[4096,512]{1,0:T(8,128)(2,1)S(1)} %copy-done.3), kind=kOutput, calls=%fused_computation.1 | convolution fusion | flops 4296015872 | bytes 18874368 | tf_op jit(solution)/shard_map/dot_general | solution.py:96
  158.1 5.0 %reshape.47 = f32[8,240,512]{2,1,0:T(8,128)} reshape(f32[32,60,512]{2,1,0:T(8,128)} %bitcast.22) | data formatting | bytes 7864320 | tf_op jit(solution)/shard_map/reshape | solution.py:109
  163.1 0.0 reduce-scatter.3.cloned.1.call-update
  163.2 20.9 %reduce-scatter.5.cloned.1.call-done = f32[2,4,240,128]{3,2,1,0:T(8,128)} async-done(((f32[8,4,240,128]{3,2,1,0:T(8,128)}), f32[2,4,240,128]{3,2,1,0:T(8,128)}) %reduce-scatter.5.cloned.1.call-update) | async-done | bytes 983056 | tf_op jit(solution)/shard_map/reduce_scatter | solution.py:102
  184.0 1.7 copy.17
  185.7 24.6 %all_to_all.18 = f32[2,128,4,240]{3,2,0,1:T(4,128)S(1)} all-to-all(f32[2,128,4,240]{3,2,0,1:T(4,128)S(1)} %copy.17), channel_id=1, replica_groups=mesh['z'=4,'y'=4,'core'=2,'x'=4] {'z','y','core'}, dimensions={1} | all-to-all | bytes 1966080 | tf_op jit(solution)/shard_map/all_to_all | solution.py:105
  210.3 0.4 copy.19
  210.7 0.6 copy.20
  211.3 0.4 reshape.50
  211.7 19.0 %reduce-scatter.3.cloned.1.call-done = f32[2,240,512]{2,1,0:T(8,128)} async-done(((f32[8,240,512]{2,1,0:T(8,128)}), f32[2,240,512]{2,1,0:T(8,128)}) %reduce-scatter.3.cloned.1.call-update) | async-done | bytes 983056 | tf_op jit(solution)/shard_map/reduce_scatter | solution.py:110
  230.7 2.3 add.37
Async XLA Ops:
  6.5 61.3 %all-gather.3.cloned.1.call-start = ((), (), s32[]{:S(2)}) async-start(), calls=%async_computation.3 | async-start | bytes 8650752 | tf_op jit(solution)/shard_map/all_gather | solution.py:81
  11.2 111.3 %all-gather.5.cloned.1.call-start = ((), (), s32[]{:S(2)}) async-start(), calls=%async_computation.4 | async-start | bytes 8650752 | tf_op jit(solution)/shard_map/all_gather | solution.py:81
  12.0 172.0 %reduce-scatter.5.cloned.1.call-start = ((), (), s32[]{:S(2)}) async-start(), calls=%async_computation.6 | async-start | bytes 4915200 | tf_op jit(solution)/shard_map/reduce_scatter | solution.py:102
  48.3 12.3 %copy-start.2 = (s32[240]{0:T(256)S(1)}, s32[240]{0:T(256)}, u32[]{:S(2)}) copy-start(s32[240]{0:T(256)} %param.4) | copy-start | bytes 2884
  48.3 12.3 %slice-start = ((s32[240]{0:T(256)}), s32[8]{0:T(128)S(1)}, s32[]{:S(2)}) async-start(s32[240]{0:T(256)} %param.4), calls=%async_computation.7 | async-start | bytes 1024 | tf_op jit(solution)/shard_map/slice | solution.py:100
  80.8 1.9 copy-start
  122.5 2.1 copy-start.1
  140.2 90.6 %reduce-scatter.3.cloned.1.call-start = ((), (), s32[]{:S(2)}) async-start(), calls=%async_computation.5 | async-start | bytes 4915200 | tf_op jit(solution)/shard_map/reduce_scatter | solution.py:110
  140.4 7.7 %copy-start.3 = (bf16[4096,512]{1,0:T(8,128)(2,1)S(1)}, bf16[4096,512]{1,0:T(8,128)(2,1)}, u32[]{:S(2)}) copy-start(bf16[4096,512]{1,0:T(8,128)(2,1)} %param.6) | copy-start | bytes 12582916
Sparse Core Ops, SparseCore 0:
  11.3 56.4 all-gather.2
  70.1 52.3 all-gather.4
  140.3 43.6 reduce-scatter.4
  186.3 44.4 reduce-scatter.2

commit v7 on v3

--- a/solution.py
+++ b/solution.py
@@ -7,11 +7,12 @@
 from jax.sharding import Mesh, PartitionSpec as P
 
 PAIR = ("z", "y", "core")
-C_STEP = 4
+C_STEP = 8
 
 
-def cycle_kernel(window, vir_full, vt_ref, g_ref, o_ref):
+def cycle_kernel(window, vir_full, vt_ref, g_ref, m_ref, o_ref):
     step = pl.program_id(0)
+    last = pl.num_programs(0) - 1
     rows = vt_ref.shape[2]
     total = None
     for c in range(vt_ref.shape[0]):
@@ -31,8 +32,12 @@
         def _():
             o_ref[i] += piece
 
+        @pl.when(step == last)
+        def _():
+            o_ref[i] = o_ref[i] * m_ref[i]
 
-def cycle_matmul(vt, g, window, vir_full):
+
+def cycle_matmul(vt, g, mask, window, vir_full):
     vir_part, n_cols, rows = vt.shape
     steps = vir_part // C_STEP
     return pl.pallas_call(
@@ -42,10 +47,11 @@
         in_specs=[
             pl.BlockSpec((C_STEP, n_cols, rows), lambda s: (s, 0, 0)),
             pl.BlockSpec((g.shape[0], C_STEP * vir_full), lambda s: (0, s)),
+            pl.BlockSpec(mask.shape, lambda s: (0, 0, 0)),
         ],
         out_specs=pl.BlockSpec((window, n_cols, vir_full), lambda s: (0, 0, 0)),
         compiler_params=pltpu.CompilerParams(dimension_semantics=("arbitrary",), vmem_limit_bytes=48 * 1024 * 1024),
-    )(vt, g)
+    )(vt, g, mask)
 
 
 def body(occ_irrep, amplitudes, ladder_ints, cycle_ints):
@@ -54,16 +60,17 @@
     vir_full = cols_local // vir_part
     vir_local = cycle_cols // occ_count
     pad_rows = -(-rows_local // 16) * 16
+    per_i = occ_count // rows_local
     pidx = lax.axis_index(PAIR)
-    global_row = pidx * rows_local + jnp.arange(rows_local, dtype=jnp.int32)
-    allowed = occ_irrep[global_row // occ_count] == occ_irrep[global_row % occ_count]
+    label_first = lax.dynamic_slice(occ_irrep, (pidx // per_i,), (1,))
+    label_second = lax.dynamic_slice(occ_irrep, ((pidx % per_i) * rows_local,), (rows_local,))
+    allowed = label_first == label_second
     amp_sym = jnp.where(allowed[:, None], amplitudes, jnp.zeros((), amplitudes.dtype))
     amp_pad = jnp.pad(amp_sym, ((0, pad_rows - rows_local), (0, 0)))
     g2 = lax.all_gather(amp_pad, PAIR, axis=0, tiled=True)
     n_blocks = g2.shape[0] // pad_rows
     total_rows = n_blocks * rows_local
     window = total_rows // occ_count
-    per_i = n_blocks // window
 
     ladder = jnp.dot(g2, ladder_ints, preferred_element_type=jnp.float32)
     ladder = ladder.reshape(n_blocks, pad_rows, -1)[:, :rows_local, :]
@@ -72,9 +79,10 @@
     v4 = cycle_ints.reshape(per_i, rows_local, vir_part, cycle_cols)
     v4 = jnp.pad(v4, ((0, 0), (0, pad_rows - rows_local), (0, 0), (0, 0)))
     vt = jnp.transpose(v4, (2, 3, 0, 1)).reshape(vir_part, cycle_cols, per_i * pad_rows)
-    cyc = cycle_matmul(vt, g2, window, vir_full)
     same_irrep = (occ_irrep[:window][:, None] == occ_irrep[None, :]).astype(jnp.float32)
-    cyc = cyc.reshape(window, vir_local, occ_count, vir_full) * same_irrep[:, None, :, None]
+    mask = jnp.broadcast_to(same_irrep[:, None, :], (window, vir_local, occ_count)).reshape(window, cycle_cols, 1)
+    cyc = cycle_matmul(vt, g2, mask, window, vir_full)
+    cyc = cyc.reshape(window, vir_local, occ_count, vir_full)
     cyc = lax.psum_scatter(cyc, "x", scatter_dimension=0, tiled=True)
     rows_here = cyc.shape[0]
     cycle_term = jnp.transpose(cyc, (0, 3, 1, 2))

time: 214 us -> 216 us (level)
  waiting for transfers between devices: 76.1 us -> 72.1 us
  local copies, waits for them, and re-layouts: 55.1 us -> 59 us
  Pallas kernels: 23.9 us -> 26.5 us
    all_gather x1, waiting for transfers between devices: 33.1 us -> 29.3 us  [body(): g2 = lax.all_gather(amp_pad, PAIR, axis=0, tiled=True)]
    reshape x0 -> x1, local copies, waits for them, and re-layouts: none -> 3.77 us  [body(): jnp.broadcast_to(same_irrep[:, None, :], (window, vir_local, occ_count))]
    gather x2 -> x0, local copies, waits for them, and re-layouts: 2.95 us -> none  [the longest x1 1.47 us: body(): occ_irrep[global_row // occ_count] == occ_irrep[global_row % occ_count]]
    pallas_call x1, Pallas kernels: 23.9 us -> 26.5 us  [cycle_matmul(): pl.pallas_call(functools.partial(cycle_kernel, window, vir_full), out_sha...]
    mul x1 -> x0, other arithmetic: 2.2 us -> none  [body(): cyc.reshape(window, vir_local, occ_count, vir_full)]
  transfers between devices with their start and end apart: 3 -> 3, of which waited for: 3 -> 3; matrix products, arithmetic and copies ran while one was open for 31% -> 32% of each run, Pallas kernels for 0% -> 0%
where the time goes in v7:
time: 216 us
  waiting for transfers between devices  72.1 us (33%)
  local copies, waits for them, and re-layouts  59 us (27%)
  Pallas kernels  26.5 us (12%)
  blocking collectives  24.6 us (11%)
  matrix products  14.9 us (7%)
  between operations  13.2 us (6%)
  other arithmetic  4.95 us (2%)
    all_gather x1, waiting for transfers between devices, body(): g2 = lax.all_gather(amp_pad, PAIR, axis=0, tiled=True)  29.3 us
    pallas_call x1, Pallas kernels, cycle_matmul(): pl.pallas_call(functools.partial(cycle_kernel, window, vir_full), out_sha...  26.5 us
    all_to_all x1, blocking collectives, body(): lax.all_to_all(cycle_term, PAIR, split_axis=1, concat_axis=2, tiled=True)  24.6 us
    reduce_scatter x1, waiting for transfers between devices, body(): cyc = lax.psum_scatter(cyc, 'x', scatter_dimension=0, tiled=True)  23.6 us
    reshape x1, local copies, waits for them, and re-layouts, body(): jnp.transpose(v4, (2, 3, 0, 1))  21 us
    reduce_scatter x1, waiting for transfers between devices, body(): ladder = lax.psum_scatter(ladder, 'x', scatter_dimension=0, tiled=True)  19.1 us
    reshape x1, local copies, waits for them, and re-layouts, body(): v4 = cycle_ints.reshape(per_i, rows_local, vir_part, cycle_cols)  14.9 us
    dot_general x1, matrix products, body(): ladder = jnp.dot(g2, ladder_ints, preferred_element_type=jnp.float32)  14.9 us
  transfers between devices with their start and end apart: 3, of which 3 were waited for; matrix products, arithmetic and copies ran while one was open for 32% of the time, Pallas kernels for 0%

profile of v7, /device:TPU:1, one launch (start us, length us, event | category | flops | bytes accessed | tf_op | source)
XLA Modules:
  0.0 215.5 jit_solution(710505132443941855)
XLA Ops:
  6.5 0.0 all-gather.2.cloned.1.call-start
  6.5 1.3 dynamic_slice.6
  7.8 1.4 dynamic-slice_compare_fusion
  9.2 1.1 broadcast_select_fusion
  10.4 0.8 pad.8
  11.2 0.0 all-gather.2.cloned.1.call-update
  11.2 0.0 reduce-scatter.5.cloned.1.call-start
  11.3 14.9 %copy.13 = bf16[4,60,32,960]{3,1,0,2:T(8,128)(2,1)S(1)} copy(bf16[4,60,32,960]{3,2,1,0:T(8,128)(2,1)} %bitcast.19) | data formatting | bytes 29491200 | tf_op jit(solution)/shard_map/reshape | solution.py:79
  26.1 7.4 %pad.9 = bf16[4,64,32,960]{3,1,0,2:T(8,128)(2,1)} pad(bf16[4,60,32,960]{3,1,0,2:T(8,128)(2,1)S(1)} %copy.13, bf16[]{:T(256)} %constant.50.clone.1), padding=0_0x0_4x0_0x0_0 | pad | bytes 30474242 | tf_op jit(solution)/shard_map/jit(_pad)/pad | solution.py:80
  33.5 0.0 copy-start.1
  33.5 0.0 slice-start
  33.5 21.0 %copy.14.vt_ref = bf16[32,960,256]{2,1,0:T(8,128)(2,1)} copy(bf16[32,960,256]{1,2,0:T(8,128)(2,1)} %bitcast.18) | data formatting | bytes 31457280 | tf_op jit(solution)/shard_map/reshape | solution.py:81
  54.5 0.0 copy-done.1
  54.5 0.0 slice-done
  54.5 0.1 compare_convert_fusion
  54.6 3.8 %reshape.53.m_ref = f32[8,960,1]{2,1,0:T(8,128)} reshape(f32[8,4,240]{2,1,0:T(4,128)S(1)} %broadcast_in_dim.23) | data formatting | bytes 61440 | tf_op jit(solution)/shard_map/reshape | solution.py:83
  58.4 29.3 %all-gather.2.cloned.1.call-done.g_ref = bf16[2048,4096]{1,0:T(8,128)(2,1)} async-done(((bf16[64,4096]{1,0:T(8,128)(2,1)}), bf16[2048,4096]{1,0:T(8,128)(2,1)}) %all-gather.2.cloned.1.call-update) | async-done | bytes 16777232 | tf_op jit(solution)/shard_map/all_gather | solution.py:70
  87.7 26.5 %shard_map.46 = f32[8,960,128]{2,1,0:T(8,128)S(1)} custom-call(bf16[32,960,256]{2,1,0:T(8,128)(2,1)} %copy.14.vt_ref, bf16[2048,4096]{1,0:T(8,128)(2,1)} %all-gather.2.cloned.1.call-done.g_ref, f32[8,960,1]{2,1,0:T(8,128)} %reshape.53.m_ref), custom_call_target="tpu_custom_call" | custom-call | tf_op jit(solution)/shard_map/pallas_call | solution.py:43
  114.2 0.0 copy-start
  114.2 1.9 copy-done
  116.0 0.0 reduce-scatter.5.cloned.1.call-update
  116.1 0.2 reduce-scatter.3.cloned.1.call-start
  116.3 14.9 %fusion = f32[2048,512]{1,0:T(8,128)} fusion(bf16[2048,4096]{1,0:T(8,128)(2,1)} %all-gather.2.cloned.1.call-done.g_ref, bf16[4096,512]{1,0:T(8,128)(2,1)} %param.6), kind=kOutput, calls=%fused_computation.3 | convolution fusion | flops 8589934592 | bytes 25165824 | tf_op jit(solution)/shard_map/dot_general | solution.py:75
  131.1 5.0 %reshape.47 = f32[8,240,512]{2,1,0:T(8,128)} reshape(f32[32,60,512]{2,1,0:T(8,128)} %bitcast.20) | data formatting | bytes 7864320 | tf_op jit(solution)/shard_map/reshape | solution.py:77
  136.1 0.0 reduce-scatter.3.cloned.1.call-update
  136.1 23.6 %reduce-scatter.5.cloned.1.call-done = f32[2,4,240,128]{3,2,1,0:T(8,128)} async-done(((f32[8,4,240,128]{3,2,1,0:T(8,128)}), f32[2,4,240,128]{3,2,1,0:T(8,128)}) %reduce-scatter.5.cloned.1.call-update) | async-done | bytes 983056 | tf_op jit(solution)/shard_map/reduce_scatter | solution.py:86
  159.8 1.7 copy.16
  161.5 24.6 %all_to_all.18 = f32[2,128,4,240]{3,2,0,1:T(4,128)S(1)} all-to-all(f32[2,128,4,240]{3,2,0,1:T(4,128)S(1)} %copy.16), channel_id=1, replica_groups=mesh['z'=4,'y'=4,'core'=2,'x'=4] {'z','y','core'}, dimensions={1} | all-to-all | bytes 1966080 | tf_op jit(solution)/shard_map/all_to_all | solution.py:89
  186.1 0.4 copy.18
  186.5 0.6 copy.19
  187.1 0.4 reshape.52
  187.5 19.1 %reduce-scatter.3.cloned.1.call-done = f32[2,240,512]{2,1,0:T(8,128)} async-done(((f32[8,240,512]{2,1,0:T(8,128)}), f32[2,240,512]{2,1,0:T(8,128)}) %reduce-scatter.3.cloned.1.call-update) | async-done | bytes 983056 | tf_op jit(solution)/shard_map/reduce_scatter | solution.py:91
  206.7 2.3 %add.33 = f32[2,240,512]{2,1,0:T(8,128)} add(f32[2,240,512]{2,1,0:T(8,128)} %reduce-scatter.3.cloned.1.call-done, f32[2,240,512]{2,1,0:T(8,128)S(1)} %reshape.52) | non-fusion elementwise | flops 245760 | bytes 2949120 | tf_op jit(solution)/shard_map/add | solution.py:92
  (1 shorter events, 0.0 us)
Async XLA Ops:
  6.5 81.1 %all-gather.2.cloned.1.call-start = ((), (), s32[]{:S(2)}) async-start(), calls=%async_computation.3 | async-start | bytes 17301504 | tf_op jit(solution)/shard_map/all_gather | solution.py:70
  11.2 148.6 %reduce-scatter.5.cloned.1.call-start = ((), (), s32[]{:S(2)}) async-start(), calls=%async_computation.5 | async-start | bytes 4915200 | tf_op jit(solution)/shard_map/reduce_scatter | solution.py:86
  33.5 21.0 %copy-start.1 = (s32[240]{0:T(256)S(1)}, s32[240]{0:T(256)}, u32[]{:S(2)}) copy-start(s32[240]{0:T(256)} %param.4) | copy-start | bytes 2884
  33.5 21.0 %slice-start = ((s32[240]{0:T(256)}), s32[8]{0:T(128)S(1)}, s32[]{:S(2)}) async-start(s32[240]{0:T(256)} %param.4), calls=%async_computation.6 | async-start | bytes 1024 | tf_op jit(solution)/shard_map/slice | solution.py:82
  114.2 1.9 copy-start
  116.1 90.6 %reduce-scatter.3.cloned.1.call-start = ((), (), s32[]{:S(2)}) async-start(), calls=%async_computation.4 | async-start | bytes 4915200 | tf_op jit(solution)/shard_map/reduce_scatter | solution.py:91
Sparse Core Ops, SparseCore 0:
  11.3 76.2 all-gather.1
  116.2 43.5 reduce-scatter.4
  162.2 44.4 reduce-scatter.2

commit v8 on v3

--- a/solution.py
+++ b/solution.py
@@ -13,13 +13,17 @@
 def cycle_kernel(window, vir_full, vt_ref, g_ref, o_ref):
     step = pl.program_id(0)
     rows = vt_ref.shape[2]
-    total = None
-    for c in range(vt_ref.shape[0]):
-        lanes = slice(c * vir_full, (c + 1) * vir_full)
-        rhs = jnp.concatenate([g_ref[i * rows:(i + 1) * rows, lanes] for i in range(window)], axis=1)
-        part = jnp.dot(vt_ref[c], rhs, preferred_element_type=jnp.float32)
-        total = part if total is None else total + part
-
+    lhs = jnp.concatenate([vt_ref[c] for c in range(vt_ref.shape[0])], axis=1)
+    rhs = jnp.concatenate(
+        [
+            jnp.concatenate(
+                [g_ref[i * rows:(i + 1) * rows, c * vir_full:(c + 1) * vir_full] for i in range(window)], axis=1
+            )
+            for c in range(vt_ref.shape[0])
+        ],
+        axis=0,
+    )
+    total = jnp.dot(lhs, rhs, preferred_element_type=jnp.float32)
     for i in range(window):
         piece = total[:, i * vir_full:(i + 1) * vir_full]
 

time: 214 us -> 215 us (level)
  no operation moved by 1% of the time
where the time goes in v8:
time: 215 us; the launch traced here: 214 us
  waiting for transfers between devices  76.1 us (35%)
  local copies, waits for them, and re-layouts  55.1 us (26%)
  blocking collectives  24.6 us (11%)
  Pallas kernels  24.4 us (11%)
  matrix products  14.9 us (7%)
  between operations  13.2 us (6%)
  other arithmetic  5.79 us (3%)
    all_gather x1, waiting for transfers between devices, body(): g2 = lax.all_gather(amp_pad, PAIR, axis=0, tiled=True)  33.1 us
    all_to_all x1, blocking collectives, body(): lax.all_to_all(cycle_term, PAIR, split_axis=1, concat_axis=2, tiled=True)  24.6 us
    pallas_call x1, Pallas kernels, cycle_matmul(): pl.pallas_call(functools.partial(cycle_kernel, window, vir_full), out_sha...  24.4 us
    reduce_scatter x1, waiting for transfers between devices, body(): cyc = lax.psum_scatter(cyc, 'x', scatter_dimension=0, tiled=True)  23.8 us
    reshape x1, local copies, waits for them, and re-layouts, body(): jnp.transpose(v4, (2, 3, 0, 1))  21 us
    reduce_scatter x1, waiting for transfers between devices, body(): ladder = lax.psum_scatter(ladder, 'x', scatter_dimension=0, tiled=True)  19.1 us
    reshape x1, local copies, waits for them, and re-layouts, body(): v4 = cycle_ints.reshape(per_i, rows_local, vir_part, cycle_cols)  14.9 us
    dot_general x1, matrix products, body(): ladder = jnp.dot(g2, ladder_ints, preferred_element_type=jnp.float32)  14.9 us
  transfers between devices with their start and end apart: 3, of which 3 were waited for; matrix products, arithmetic and copies ran while one was open for 31% of the time, Pallas kernels for 0%

profile of v8, /device:TPU:1, one launch (start us, length us, event | category | flops | bytes accessed | tf_op | source)
XLA Modules:
  0.0 214.1 jit_solution(3923565491924260484)
XLA Ops:
  6.5 0.0 all-gather.2.cloned.1.call-start
  6.6 1.5 gather_fusion
  8.1 1.5 gather_fusion.1
  9.5 1.1 broadcast_select_fusion
  10.7 0.8 pad.8
  11.5 0.0 all-gather.2.cloned.1.call-update
  11.6 0.0 reduce-scatter.5.cloned.1.call-start
  11.6 14.9 %copy.12 = bf16[4,60,32,960]{3,1,0,2:T(8,128)(2,1)S(1)} copy(bf16[4,60,32,960]{3,2,1,0:T(8,128)(2,1)} %bitcast.22) | data formatting | bytes 29491200 | tf_op jit(solution)/shard_map/reshape | solution.py:76
  26.5 7.4 %pad.9 = bf16[4,64,32,960]{3,1,0,2:T(8,128)(2,1)} pad(bf16[4,60,32,960]{3,1,0,2:T(8,128)(2,1)S(1)} %copy.12, bf16[]{:T(256)} %constant.45.clone.1), padding=0_0x0_4x0_0x0_0 | pad | bytes 30474242 | tf_op jit(solution)/shard_map/jit(_pad)/pad | solution.py:77
  33.9 0.0 copy-start
  33.9 0.0 slice-start
  33.9 21.0 %copy.13.vt_ref = bf16[32,960,256]{2,1,0:T(8,128)(2,1)} copy(bf16[32,960,256]{1,2,0:T(8,128)(2,1)} %bitcast.21) | data formatting | bytes 31457280 | tf_op jit(solution)/shard_map/reshape | solution.py:78
  54.8 0.0 copy-done
  54.8 0.0 slice-done
  54.8 0.1 compare_convert_fusion
  54.9 33.1 %all-gather.2.cloned.1.call-done.g_ref = bf16[2048,4096]{1,0:T(8,128)(2,1)} async-done(((bf16[64,4096]{1,0:T(8,128)(2,1)}), bf16[2048,4096]{1,0:T(8,128)(2,1)}) %all-gather.2.cloned.1.call-update) | async-done | bytes 16777232 | tf_op jit(solution)/shard_map/all_gather | solution.py:66
  88.0 24.4 %shard_map.46 = f32[8,960,128]{2,1,0:T(8,128)S(1)} custom-call(bf16[32,960,256]{2,1,0:T(8,128)(2,1)} %copy.13.vt_ref, bf16[2048,4096]{1,0:T(8,128)(2,1)} %all-gather.2.cloned.1.call-done.g_ref), custom_call_target="tpu_custom_call" | custom-call | tf_op jit(solution)/shard_map/pallas_call | solution.py:42
  112.4 2.2 %broadcast_multiply_fusion = f32[8,4,240,128]{3,2,1,0:T(8,128)} fusion(f32[8,4,240,128]{3,2,1,0:T(8,128)S(1)} %bitcast.20, f32[8,240]{1,0:T(8,128)S(1)} %compare_convert_fusion), kind=kLoop, calls=%fused_computation.2 | loop fusion | flops 983040 | bytes 7872000 | tf_op jit(solution)/shard_map/mul | solution.py:81
  114.6 0.0 reduce-scatter.5.cloned.1.call-update
  114.6 0.0 reduce-scatter.3.cloned.1.call-start
  114.7 14.9 %fusion.3 = f32[2048,512]{1,0:T(8,128)} fusion(bf16[2048,4096]{1,0:T(8,128)(2,1)} %all-gather.2.cloned.1.call-done.g_ref, bf16[4096,512]{1,0:T(8,128)(2,1)} %param.6), kind=kOutput, calls=%fused_computation.15 | convolution fusion | flops 8589934592 | bytes 25165824 | tf_op jit(solution)/shard_map/dot_general | solution.py:72
  129.5 5.0 %reshape.113 = f32[8,240,512]{2,1,0:T(8,128)} reshape(f32[32,60,512]{2,1,0:T(8,128)} %bitcast.23) | data formatting | bytes 7864320 | tf_op jit(solution)/shard_map/reshape | solution.py:74
  134.5 0.0 reduce-scatter.3.cloned.1.call-update
  134.5 23.8 %reduce-scatter.5.cloned.1.call-done = f32[2,4,240,128]{3,2,1,0:T(8,128)} async-done(((f32[8,4,240,128]{3,2,1,0:T(8,128)}), f32[2,4,240,128]{3,2,1,0:T(8,128)}) %reduce-scatter.5.cloned.1.call-update) | async-done | bytes 983056 | tf_op jit(solution)/shard_map/reduce_scatter | solution.py:82
  158.4 1.7 copy.14
  160.1 24.6 %all_to_all.18 = f32[2,128,4,240]{3,2,0,1:T(4,128)S(1)} all-to-all(f32[2,128,4,240]{3,2,0,1:T(4,128)S(1)} %copy.14), channel_id=1, replica_groups=mesh['z'=4,'y'=4,'core'=2,'x'=4] {'z','y','core'}, dimensions={1} | all-to-all | bytes 1966080 | tf_op jit(solution)/shard_map/all_to_all | solution.py:85
  184.7 0.4 copy.16
  185.1 0.6 copy.17
  185.7 0.4 reshape.117
  186.1 19.1 %reduce-scatter.3.cloned.1.call-done = f32[2,240,512]{2,1,0:T(8,128)} async-done(((f32[8,240,512]{2,1,0:T(8,128)}), f32[2,240,512]{2,1,0:T(8,128)}) %reduce-scatter.3.cloned.1.call-update) | async-done | bytes 983056 | tf_op jit(solution)/shard_map/reduce_scatter | solution.py:87
  205.2 2.3 %add.82 = f32[2,240,512]{2,1,0:T(8,128)} add(f32[2,240,512]{2,1,0:T(8,128)} %reduce-scatter.3.cloned.1.call-done, f32[2,240,512]{2,1,0:T(8,128)S(1)} %reshape.117) | non-fusion elementwise | flops 245760 | bytes 2949120 | tf_op jit(solution)/shard_map/add | solution.py:88
  (4 shorter events, 0.0 us)
Async XLA Ops:
  6.5 81.5 %all-gather.2.cloned.1.call-start = ((), (), s32[]{:S(2)}) async-start(), calls=%async_computation.3 | async-start | bytes 17301504 | tf_op jit(solution)/shard_map/all_gather | solution.py:66
  11.6 146.8 %reduce-scatter.5.cloned.1.call-start = ((), (), s32[]{:S(2)}) async-start(), calls=%async_computation.5 | async-start | bytes 4915200 | tf_op jit(solution)/shard_map/reduce_scatter | solution.py:82
  33.9 21.0 %copy-start = (s32[240]{0:T(256)S(1)}, s32[240]{0:T(256)}, u32[]{:S(2)}) copy-start(s32[240]{0:T(256)} %param.4) | copy-start | bytes 2884
  33.9 21.0 %slice-start = ((s32[240]{0:T(256)}), s32[8]{0:T(128)S(1)}, s32[]{:S(2)}) async-start(s32[240]{0:T(256)} %param.4), calls=%async_computation.6 | async-start | bytes 1024 | tf_op jit(solution)/shard_map/slice | solution.py:80
  114.6 90.6 %reduce-scatter.3.cloned.1.call-start = ((), (), s32[]{:S(2)}) async-start(), calls=%async_computation.4 | async-start | bytes 4915200 | tf_op jit(solution)/shard_map/reduce_scatter | solution.py:87
Sparse Core Ops, SparseCore 0:
  11.7 76.2 all-gather.1
  114.8 43.5 reduce-scatter.4
  160.8 44.4 reduce-scatter.2

commit v9 on v3

--- a/solution.py
+++ b/solution.py
@@ -55,15 +55,18 @@
     vir_local = cycle_cols // occ_count
     pad_rows = -(-rows_local // 16) * 16
     pidx = lax.axis_index(PAIR)
-    global_row = pidx * rows_local + jnp.arange(rows_local, dtype=jnp.int32)
-    allowed = occ_irrep[global_row // occ_count] == occ_irrep[global_row % occ_count]
-    amp_sym = jnp.where(allowed[:, None], amplitudes, jnp.zeros((), amplitudes.dtype))
-    amp_pad = jnp.pad(amp_sym, ((0, pad_rows - rows_local), (0, 0)))
+    per_i = occ_count // rows_local
+    labels = jnp.concatenate([occ_irrep, jnp.full((pad_rows - rows_local,), -1, occ_irrep.dtype)])
+    label_first = lax.dynamic_slice(occ_irrep, (pidx // per_i,), (1,))
+    label_second = lax.dynamic_slice(labels, ((pidx % per_i) * rows_local,), (pad_rows,))
+    row = lax.broadcasted_iota(jnp.int32, (pad_rows,), 0)
+    allowed = (label_second == label_first) & (row < rows_local)
+    amp_pad = jnp.where(allowed[:, None], jnp.pad(amplitudes, ((0, pad_rows - rows_local), (0, 0))),
+                        jnp.zeros((), amplitudes.dtype))
     g2 = lax.all_gather(amp_pad, PAIR, axis=0, tiled=True)
     n_blocks = g2.shape[0] // pad_rows
     total_rows = n_blocks * rows_local
     window = total_rows // occ_count
-    per_i = n_blocks // window
 
     ladder = jnp.dot(g2, ladder_ints, preferred_element_type=jnp.float32)
     ladder = ladder.reshape(n_blocks, pad_rows, -1)[:, :rows_local, :]

time: 214 us -> 214 us (level)
  local copies, waits for them, and re-layouts: 55.1 us -> 52.6 us
  other arithmetic: 5.79 us -> 8 us
    gather x2 -> x0, local copies, waits for them, and re-layouts: 2.95 us -> none  [the longest x1 1.47 us: body(): occ_irrep[global_row // occ_count] == occ_irrep[global_row % occ_count]]
where the time goes in v9:
time: 214 us; the launch traced here: 213 us
  waiting for transfers between devices  76.1 us (36%)
  local copies, waits for them, and re-layouts  52.6 us (25%)
  blocking collectives  24.6 us (11%)
  Pallas kernels  23.9 us (11%)
  matrix products  14.9 us (7%)
  between operations  13.2 us (6%)
  other arithmetic  8 us (4%)
    all_gather x1, waiting for transfers between devices, body(): g2 = lax.all_gather(amp_pad, PAIR, axis=0, tiled=True)  33.1 us
    all_to_all x1, blocking collectives, body(): lax.all_to_all(cycle_term, PAIR, split_axis=1, concat_axis=2, tiled=True)  24.6 us
    pallas_call x1, Pallas kernels, cycle_matmul(): pl.pallas_call(functools.partial(cycle_kernel, window, vir_full), out_sha...  23.9 us
    reduce_scatter x1, waiting for transfers between devices, body(): cyc = lax.psum_scatter(cyc, 'x', scatter_dimension=0, tiled=True)  23.8 us
    reshape x1, local copies, waits for them, and re-layouts, body(): jnp.transpose(v4, (2, 3, 0, 1))  21 us
    reduce_scatter x1, waiting for transfers between devices, body(): ladder = lax.psum_scatter(ladder, 'x', scatter_dimension=0, tiled=True)  19.2 us
    dot_general x1, matrix products, body(): ladder = jnp.dot(g2, ladder_ints, preferred_element_type=jnp.float32)  14.9 us
    reshape x1, local copies, waits for them, and re-layouts, body(): v4 = cycle_ints.reshape(per_i, rows_local, vir_part, cycle_cols)  14.9 us
  transfers between devices with their start and end apart: 3, of which 3 were waited for; matrix products, arithmetic and copies ran while one was open for 31% of the time, Pallas kernels for 0%

profile of v9, /device:TPU:1, one launch (start us, length us, event | category | flops | bytes accessed | tf_op | source)
XLA Modules:
  0.0 213.3 jit_solution(2604264482810157245)
XLA Ops:
  6.5 0.0 all-gather.2.cloned.1.call-start
  6.5 1.3 dynamic_slice.7
  7.8 1.4 compare_and_fusion
  9.2 2.0 pad_select_fusion
  11.2 0.0 all-gather.2.cloned.1.call-update
  11.2 0.0 reduce-scatter.5.cloned.1.call-start
  11.3 14.9 %copy.12 = bf16[4,60,32,960]{3,1,0,2:T(8,128)(2,1)S(1)} copy(bf16[4,60,32,960]{3,2,1,0:T(8,128)(2,1)} %bitcast.19) | data formatting | bytes 29491200 | tf_op jit(solution)/shard_map/reshape | solution.py:75
  26.1 7.4 %pad.10 = bf16[4,64,32,960]{3,1,0,2:T(8,128)(2,1)} pad(bf16[4,60,32,960]{3,1,0,2:T(8,128)(2,1)S(1)} %copy.12, bf16[]{:T(256)} %constant.54.clone.1), padding=0_0x0_4x0_0x0_0 | pad | bytes 30474242 | tf_op jit(solution)/shard_map/jit(_pad)/pad | solution.py:76
  33.5 0.0 copy-start
  33.5 0.0 slice-start
  33.5 21.0 %copy.13.vt_ref = bf16[32,960,256]{2,1,0:T(8,128)(2,1)} copy(bf16[32,960,256]{1,2,0:T(8,128)(2,1)} %bitcast.18) | data formatting | bytes 31457280 | tf_op jit(solution)/shard_map/reshape | solution.py:77
  54.5 0.0 copy-done
  54.5 0.0 slice-done
  54.5 0.1 compare_convert_fusion
  54.6 33.1 %all-gather.2.cloned.1.call-done.g_ref = bf16[2048,4096]{1,0:T(8,128)(2,1)} async-done(((bf16[64,4096]{1,0:T(8,128)(2,1)}), bf16[2048,4096]{1,0:T(8,128)(2,1)}) %all-gather.2.cloned.1.call-update) | async-done | bytes 16777232 | tf_op jit(solution)/shard_map/all_gather | solution.py:66
  87.7 23.9 %shard_map.46 = f32[8,960,128]{2,1,0:T(8,128)S(1)} custom-call(bf16[32,960,256]{2,1,0:T(8,128)(2,1)} %copy.13.vt_ref, bf16[2048,4096]{1,0:T(8,128)(2,1)} %all-gather.2.cloned.1.call-done.g_ref), custom_call_target="tpu_custom_call" | custom-call | tf_op jit(solution)/shard_map/pallas_call | solution.py:38
  111.5 2.2 %broadcast_multiply_fusion = f32[8,4,240,128]{3,2,1,0:T(8,128)} fusion(f32[8,4,240,128]{3,2,1,0:T(8,128)S(1)} %bitcast.17, f32[8,240]{1,0:T(8,128)S(1)} %compare_convert_fusion), kind=kLoop, calls=%fused_computation | loop fusion | flops 983040 | bytes 7872000 | tf_op jit(solution)/shard_map/mul | solution.py:80
  113.7 0.0 reduce-scatter.5.cloned.1.call-update
  113.8 0.0 reduce-scatter.3.cloned.1.call-start
  113.8 14.9 %fusion = f32[2048,512]{1,0:T(8,128)} fusion(bf16[2048,4096]{1,0:T(8,128)(2,1)} %all-gather.2.cloned.1.call-done.g_ref, bf16[4096,512]{1,0:T(8,128)(2,1)} %param.6), kind=kOutput, calls=%fused_computation.5 | convolution fusion | flops 8589934592 | bytes 25165824 | tf_op jit(solution)/shard_map/dot_general | solution.py:71
  128.7 5.0 %reshape.47 = f32[8,240,512]{2,1,0:T(8,128)} reshape(f32[32,60,512]{2,1,0:T(8,128)} %bitcast.20) | data formatting | bytes 7864320 | tf_op jit(solution)/shard_map/reshape | solution.py:73
  133.7 0.0 reduce-scatter.3.cloned.1.call-update
  133.7 23.8 %reduce-scatter.5.cloned.1.call-done = f32[2,4,240,128]{3,2,1,0:T(8,128)} async-done(((f32[8,4,240,128]{3,2,1,0:T(8,128)}), f32[2,4,240,128]{3,2,1,0:T(8,128)}) %reduce-scatter.5.cloned.1.call-update) | async-done | bytes 983056 | tf_op jit(solution)/shard_map/reduce_scatter | solution.py:81
  157.5 1.7 copy.14
  159.2 24.6 %all_to_all.18 = f32[2,128,4,240]{3,2,0,1:T(4,128)S(1)} all-to-all(f32[2,128,4,240]{3,2,0,1:T(4,128)S(1)} %copy.14), channel_id=1, replica_groups=mesh['z'=4,'y'=4,'core'=2,'x'=4] {'z','y','core'}, dimensions={1} | all-to-all | bytes 1966080 | tf_op jit(solution)/shard_map/all_to_all | solution.py:84
  183.8 0.4 copy.16
  184.2 0.6 copy.17
  184.8 0.4 reshape.51
  185.2 19.2 %reduce-scatter.3.cloned.1.call-done = f32[2,240,512]{2,1,0:T(8,128)} async-done(((f32[8,240,512]{2,1,0:T(8,128)}), f32[2,240,512]{2,1,0:T(8,128)}) %reduce-scatter.3.cloned.1.call-update) | async-done | bytes 983056 | tf_op jit(solution)/shard_map/reduce_scatter | solution.py:86
  204.4 2.3 %add.35 = f32[2,240,512]{2,1,0:T(8,128)} add(f32[2,240,512]{2,1,0:T(8,128)} %reduce-scatter.3.cloned.1.call-done, f32[2,240,512]{2,1,0:T(8,128)S(1)} %reshape.51) | non-fusion elementwise | flops 245760 | bytes 2949120 | tf_op jit(solution)/shard_map/add | solution.py:87
Async XLA Ops:
  6.5 81.1 %all-gather.2.cloned.1.call-start = ((), (), s32[]{:S(2)}) async-start(), calls=%async_computation.3 | async-start | bytes 17301504 | tf_op jit(solution)/shard_map/all_gather | solution.py:66
  11.2 146.3 %reduce-scatter.5.cloned.1.call-start = ((), (), s32[]{:S(2)}) async-start(), calls=%async_computation.5 | async-start | bytes 4915200 | tf_op jit(solution)/shard_map/reduce_scatter | solution.py:81
  33.5 21.0 %copy-start = (s32[240]{0:T(256)S(1)}, s32[240]{0:T(256)}, u32[]{:S(2)}) copy-start(s32[240]{0:T(256)} %param.4) | copy-start | bytes 2884
  33.5 21.0 %slice-start = ((s32[240]{0:T(256)}), s32[8]{0:T(128)S(1)}, s32[]{:S(2)}) async-start(s32[240]{0:T(256)} %param.4), calls=%async_computation.6 | async-start | bytes 1024 | tf_op jit(solution)/shard_map/slice | solution.py:79
  113.8 90.6 %reduce-scatter.3.cloned.1.call-start = ((), (), s32[]{:S(2)}) async-start(), calls=%async_computation.4 | async-start | bytes 4915200 | tf_op jit(solution)/shard_map/reduce_scatter | solution.py:86
Sparse Core Ops, SparseCore 0:
  11.3 76.2 all-gather.1
  113.9 43.5 reduce-scatter.4
  159.9 44.4 reduce-scatter.2

commit v10 on v4

--- a/solution.py
+++ b/solution.py
@@ -10,7 +10,8 @@
 C_STEP = 4
 
 
-def cycle_kernel(vir_full, vt_ref, g_ref, o_ref):
+def cycle_kernel(vir_full, vt_ref, g_ref, *refs):
+    o_ref = refs[-1]
     step = pl.program_id(0)
     n_i = g_ref.shape[0]
     total = None
@@ -31,7 +32,7 @@
             o_ref[q] += piece
 
 
-def cycle_matmul(vt, g4, parity, vir_full):
+def cycle_matmul(vt, g4, parity, vir_full, after=None):
     vir_part, n_cols, rows = vt.shape
     n_i = g4.shape[0]
     steps = vir_part // C_STEP
@@ -42,10 +43,10 @@
         in_specs=[
             pl.BlockSpec((C_STEP, n_cols, rows), lambda s: (s, 0, 0)),
             pl.BlockSpec((n_i, None, rows, C_STEP * vir_full), lambda s: (0, parity, 0, s)),
-        ],
+        ] + ([] if after is None else [pl.BlockSpec(memory_space=pl.ANY)]),
         out_specs=pl.BlockSpec((n_i, n_cols, vir_full), lambda s: (0, 0, 0)),
         compiler_params=pltpu.CompilerParams(dimension_semantics=("arbitrary",), vmem_limit_bytes=48 * 1024 * 1024),
-    )(vt, g4)
+    )(vt, g4, *([] if after is None else [after]))
 
 
 def body(occ_irrep, amplitudes, ladder_ints, cycle_ints):
@@ -74,20 +75,25 @@
     same_irrep = (occ_irrep[:window][:, None] == occ_irrep[None, :]).astype(jnp.float32)
     same4 = same_irrep.reshape(n_x, i_here, occ_count)
 
-    moved_parts = []
-    for parity in range(i_here):
-        cyc = cycle_matmul(vt, g4, parity, vir_full)
-        cyc = cyc.reshape(n_x, vir_local, occ_count, vir_full) * same4[:, parity, None, :, None]
-        cyc = lax.psum_scatter(cyc, "x", scatter_dimension=0, tiled=True)
-        cycle_term = jnp.transpose(cyc, (0, 3, 1, 2))
+    def masked(parity, after=None):
+        cyc = cycle_matmul(vt, g4, parity, vir_full, after)
+        return cyc.reshape(n_x, vir_local, occ_count, vir_full) * same4[:, parity, None, :, None]
+
+    def regroup(cycle_term):
         regrouped = lax.all_to_all(cycle_term, PAIR, split_axis=1, concat_axis=2, tiled=True)
-        moved_parts.append(jnp.transpose(regrouped, (0, 3, 1, 2)).reshape(1, occ_count, vir_local * vir_full))
+        return jnp.transpose(regrouped, (0, 3, 1, 2)).reshape(cycle_term.shape[0], occ_count, vir_local * vir_full)
+
+    term_even = jnp.transpose(masked(0), (0, 3, 1, 2))
+    moved_even = regroup(term_even)
+    odd = lax.psum_scatter(masked(1, term_even), "x", scatter_dimension=0, tiled=True)
+    moved_odd = regroup(jnp.transpose(odd, (0, 3, 1, 2)))
 
     ladder = jnp.dot(g2, ladder_ints, preferred_element_type=jnp.float32)
     ladder = ladder.reshape(n_blocks, pad_rows, -1)[:, :rows_local, :]
-    ladder = ladder.reshape(window, occ_count, vir_local * vir_full)
+    ladder = ladder.reshape(n_x, i_here, occ_count, vir_local * vir_full)
+    ladder = ladder.at[:, 0].add(moved_even).reshape(window, occ_count, vir_local * vir_full)
     ladder = lax.psum_scatter(ladder, "x", scatter_dimension=0, tiled=True)
-    return ladder + jnp.concatenate(moved_parts, axis=0)
+    return ladder.at[1:].add(moved_odd)
 
 
 def solution(mesh):

time: 220 us -> 224 us (1.018)
  waiting for transfers between devices: 83.3 us -> 66.8 us
  blocking collectives: 0 us -> 15.9 us
  local copies, waits for them, and re-layouts: 55.6 us -> 64.8 us
  starting transfers between devices: 13.3 us -> 5.69 us
  other arithmetic: 7.92 us -> 11.3 us
    all_to_all x0 -> x1, blocking collectives: none -> 15.9 us  [regroup(): lax.all_to_all(cycle_term, PAIR, split_axis=1, concat_axis=2, tiled=True)]
    reduce_scatter x2 -> x1, waiting for transfers between devices: 14.6 us -> 0.02 us  [body(): lax.psum_scatter(masked(1, term_even), 'x', scatter_dimension=0, tiled=True)]
    all_to_all x2 -> x1, starting transfers between devices: 13.1 us -> 5.43 us  [regroup(): lax.all_to_all(cycle_term, PAIR, split_axis=1, concat_axis=2, tiled=True)]
    scatter-add x0 -> x2, other arithmetic: none -> 5.19 us  [the longest x1 3.31 us: body(): ladder.at[:, 0].add(moved_even)]
    transpose x4, local copies, waits for them, and re-layouts: 4.55 us -> 7.61 us  [the longest x2 4.37 us: regroup(): jnp.transpose(regrouped, (0, 3, 1, 2))]
    all_to_all x2, local copies, waits for them, and re-layouts: 0.27 us -> 2.82 us  [regroup(): lax.all_to_all(cycle_term, PAIR, split_axis=1, concat_axis=2, tiled=True)]
    all_to_all x2 -> x1, waiting for transfers between devices: 10.8 us -> 8.33 us  [regroup(): lax.all_to_all(cycle_term, PAIR, split_axis=1, concat_axis=2, tiled=True)]
    add x1 -> x0, other arithmetic: 2.34 us -> none  [body(): return ladder + jnp.concatenate(moved_parts, axis=0)]
  transfers between devices with their start and end apart: 6 -> 4, of which waited for: 4 -> 3; matrix products, arithmetic and copies ran while one was open for 32% -> 36% of each run, Pallas kernels for 7% -> 0%
where the time goes in v10:
time: 224 us; the launch traced here: 222 us
  waiting for transfers between devices  66.8 us (30%)
  local copies, waits for them, and re-layouts  64.8 us (29%)
  Pallas kernels  29.5 us (13%)
  blocking collectives  15.9 us (7%)
  matrix products  15 us (7%)
  between operations  13.2 us (6%)
  other arithmetic  11.3 us (5%)
  starting transfers between devices  5.69 us (3%)
    all_gather x1, waiting for transfers between devices, body(): g2 = lax.all_gather(amp_pad, PAIR, axis=0, tiled=True)  32.9 us
    pallas_call x2, Pallas kernels, cycle_matmul(): pl.pallas_call(functools.partial(cycle_kernel, vir_full), out_shape=jax.S...  29.5 us
    reduce_scatter x1, waiting for transfers between devices, body(): ladder = lax.psum_scatter(ladder, 'x', scatter_dimension=0, tiled=True)  25.4 us
    reshape x1, local copies, waits for them, and re-layouts, body(): jnp.transpose(v4, (2, 3, 0, 1))  21 us
    all_to_all x1, blocking collectives, regroup(): lax.all_to_all(cycle_term, PAIR, split_axis=1, concat_axis=2, tiled=True)  15.9 us
    dot_general x1, matrix products, body(): ladder = jnp.dot(g2, ladder_ints, preferred_element_type=jnp.float32)  15 us
    reshape x1, local copies, waits for them, and re-layouts, body(): v4 = cycle_ints.reshape(per_i, rows_local, vir_part, cycle_cols)  14.9 us
    all_to_all x1, waiting for transfers between devices, regroup(): lax.all_to_all(cycle_term, PAIR, split_axis=1, concat_axis=2, tiled=True)  8.33 us
  transfers between devices with their start and end apart: 4, of which 3 were waited for; matrix products, arithmetic and copies ran while one was open for 36% of the time, Pallas kernels for 0%

profile of v10, /device:TPU:1, one launch (start us, length us, event | category | flops | bytes accessed | tf_op | source)
XLA Modules:
  0.0 222.2 jit_solution(7706599516431009594)
XLA Ops:
  6.5 0.0 all-gather.2.cloned.1.call-start
  6.5 1.3 dynamic_slice.6
  7.8 1.4 dynamic-slice_compare_fusion
  9.2 1.1 broadcast_select_fusion
  10.4 0.8 pad.12
  11.2 0.0 all-gather.2.cloned.1.call-update
  11.2 0.0 reduce-scatter.5.cloned.1.call-start
  11.3 14.9 %copy.43 = bf16[4,60,32,960]{3,1,0,2:T(8,128)(2,1)S(1)} copy(bf16[4,60,32,960]{3,2,1,0:T(8,128)(2,1)} %bitcast.39) | data formatting | bytes 29491200 | tf_op jit(solution)/shard_map/reshape | solution.py:71
  26.1 7.4 %pad.13 = bf16[4,64,32,960]{3,1,0,2:T(8,128)(2,1)} pad(bf16[4,60,32,960]{3,1,0,2:T(8,128)(2,1)S(1)} %copy.43, bf16[]{:T(256)} %constant.103.clone.1), padding=0_0x0_4x0_0x0_0 | pad | bytes 30474242 | tf_op jit(solution)/shard_map/jit(_pad)/pad | solution.py:72
  33.5 0.0 slice-start
  33.5 0.0 copy-start
  33.5 21.0 %copy.44.vt_ref = bf16[32,960,256]{2,1,0:T(8,128)(2,1)} copy(bf16[32,960,256]{1,2,0:T(8,128)(2,1)} %bitcast.37) | data formatting | bytes 31457280 | tf_op jit(solution)/shard_map/reshape | solution.py:73
  54.5 0.0 slice-done
  54.5 0.1 eq.31
  54.6 0.1 copy.45
  54.7 0.0 copy-done
  54.7 0.1 compare_convert_fusion
  54.7 32.9 %all-gather.2.cloned.1.call-done = bf16[2048,4096]{1,0:T(8,128)(2,1)} async-done(((bf16[64,4096]{1,0:T(8,128)(2,1)}), bf16[2048,4096]{1,0:T(8,128)(2,1)}) %all-gather.2.cloned.1.call-update) | async-done | bytes 16777232 | tf_op jit(solution)/shard_map/all_gather | solution.py:65
  87.7 14.8 %shard_map.46 = f32[4,960,128]{2,1,0:T(8,128)S(1)} custom-call(bf16[32,960,256]{2,1,0:T(8,128)(2,1)} %copy.44.vt_ref, bf16[4,2,256,4096]{3,2,1,0:T(8,128)(2,1)} %bitcast.35), custom_call_target="tpu_custom_call" | custom-call | tf_op jit(solution)/shard_map/pallas_call | solution.py:39
  102.4 1.9 copy.46
  104.3 2.0 multiply_bitcast_fusion.refs_0_
  106.3 14.8 %shard_map.47 = f32[4,960,128]{2,1,0:T(8,128)S(1)} custom-call(bf16[32,960,256]{2,1,0:T(8,128)(2,1)} %copy.44.vt_ref, bf16[4,2,256,4096]{3,2,1,0:T(8,128)(2,1)} %bitcast.36, f32[4,128,4,240]{3,2,1,0:T(4,128)S(1)} %multiply_bitcast_fusion.refs_0_), custom_call_target="tpu_custom_call" | custom-call | tf_op jit(solution)/shard_map/pallas_call | solution.py:39
  121.0 1.5 broadcast_multiply_fusion
  122.5 0.0 reduce-scatter.5.cloned.1.call-update
  122.6 2.0 copy.47
  124.5 5.4 %all-to-all-start = ((f32[4,128,4,240]{3,2,0,1:T(4,128)}), f32[4,128,4,240]{3,2,0,1:T(4,128)S(1)}, u32[]{:S(2)}, u32[]{:S(2)}) async-start(f32[4,128,4,240]{3,2,0,1:T(4,128)} %copy.47), calls=%async_computation | async-start | bytes 4194304 | tf_op jit(solution)/shard_map/all_to_all | solution.py:83
  130.0 0.2 reduce-scatter.3.cloned.1.call-start
  130.2 15.0 %fusion.2 = f32[2048,512]{1,0:T(8,128)} fusion(bf16[2048,4096]{1,0:T(8,128)(2,1)} %all-gather.2.cloned.1.call-done, bf16[4096,512]{1,0:T(8,128)(2,1)} %param.10), kind=kOutput, calls=%fused_computation.11 | convolution fusion | flops 8589934592 | bytes 25165824 | tf_op jit(solution)/shard_map/dot_general | solution.py:91
  145.2 5.0 %reshape.117 = f32[4,2,240,512]{3,2,1,0:T(8,128)} reshape(f32[32,60,512]{2,1,0:T(8,128)} %bitcast.42) | data formatting | bytes 7864320 | tf_op jit(solution)/shard_map/reshape | solution.py:93
  150.2 8.3 %all-to-all-done = f32[4,128,4,240]{3,2,0,1:T(4,128)S(1)} async-done(((f32[4,128,4,240]{3,2,0,1:T(4,128)}), f32[4,128,4,240]{3,2,0,1:T(4,128)S(1)}, u32[]{:S(2)}, u32[]{:S(2)}) %all-to-all-start) | async-done | bytes 1966112 | tf_op jit(solution)/shard_map/all_to_all | solution.py:83
  158.6 2.7 %copy.48 = f32[4,32,4,4,240]{4,2,3,1,0:T(4,128)} copy(f32[4,32,4,4,240]{4,3,0,2,1:T(4,128)S(1)} %bitcast.40) | data formatting | bytes 3932160 | tf_op jit(solution)/shard_map/all_to_all | solution.py:83
  161.2 4.1 %copy.49 = f32[4,240,4,128]{3,2,1,0:T(4,128)} copy(f32[4,240,4,128]{1,2,3,0:T(4,128)} %bitcast.41) | data formatting | bytes 3932160 | tf_op jit(solution)/shard_map/transpose | solution.py:84
  165.3 2.1 reshape.122
  167.4 3.3 %fusion = f32[4,2,240,512]{3,2,1,0:T(8,128)} fusion(f32[4,2,240,512]{3,2,1,0:T(8,128)} %reshape.117, f32[4,1,240,512]{3,2,1,0:T(8,128)S(1)} %reshape.122), kind=kLoop, calls=%fused_computation.2 | loop fusion | flops 491520 | bytes 5898240 | tf_op jit(solution)/shard_map/scatter-add | solution.py:94
  170.7 0.0 reduce-scatter.3.cloned.1.call-update
  170.7 0.0 reduce-scatter.5.cloned.1.call-done
  170.8 1.3 copy.51
  172.0 15.9 %all_to_all.36 = f32[1,128,4,240]{3,2,0,1:T(4,128)S(1)} all-to-all(f32[1,128,4,240]{3,2,0,1:T(4,128)S(1)} %copy.51), channel_id=1, replica_groups=mesh['z'=4,'y'=4,'core'=2,'x'=4] {'z','y','core'}, dimensions={1} | all-to-all | bytes 983040 | tf_op jit(solution)/shard_map/all_to_all | solution.py:83
  188.0 0.1 copy.52
  188.1 0.3 copy.53
  188.4 25.4 %reduce-scatter.3.cloned.1.call-done = f32[2,240,512]{2,1,0:T(8,128)} async-done(((f32[8,240,512]{2,1,0:T(8,128)}), f32[2,240,512]{2,1,0:T(8,128)}) %reduce-scatter.3.cloned.1.call-update) | async-done | bytes 983056 | tf_op jit(solution)/shard_map/reduce_scatter | solution.py:95
  213.8 1.9 fusion.1
  (1 shorter events, 0.0 us)
Async XLA Ops:
  6.5 81.1 %all-gather.2.cloned.1.call-start = ((), (), s32[]{:S(2)}) async-start(), calls=%async_computation.4 | async-start | bytes 17301504 | tf_op jit(solution)/shard_map/all_gather | solution.py:65
  11.2 159.6 %reduce-scatter.5.cloned.1.call-start = ((), (), s32[]{:S(2)}) async-start(), calls=%async_computation.6 | async-start | bytes 2457600 | tf_op jit(solution)/shard_map/reduce_scatter | solution.py:88
  33.5 21.0 %slice-start = ((s32[240]{0:T(256)}), s32[8]{0:T(128)S(1)}, s32[]{:S(2)}) async-start(s32[240]{0:T(256)} %param.8), calls=%async_computation.7 | async-start | bytes 1024 | tf_op jit(solution)/shard_map/slice | solution.py:75
  33.5 21.2 %copy-start = (s32[240]{0:T(256)S(1)}, s32[240]{0:T(256)}, u32[]{:S(2)}) copy-start(s32[240]{0:T(256)} %param.8) | copy-start | bytes 2884
  124.5 34.0 %all-to-all-start = ((f32[4,128,4,240]{3,2,0,1:T(4,128)}), f32[4,128,4,240]{3,2,0,1:T(4,128)S(1)}, u32[]{:S(2)}, u32[]{:S(2)}) async-start(f32[4,128,4,240]{3,2,0,1:T(4,128)} %copy.47), calls=%async_computation | async-start | bytes 4194304 | tf_op jit(solution)/shard_map/all_to_all | solution.py:83
  130.0 83.8 %reduce-scatter.3.cloned.1.call-start = ((), (), s32[]{:S(2)}) async-start(), calls=%async_computation.5 | async-start | bytes 4915200 | tf_op jit(solution)/shard_map/reduce_scatter | solution.py:95
Sparse Core Ops, SparseCore 0:
  11.3 76.2 all-gather.1
  122.7 27.5 reduce-scatter.4
  170.9 42.8 reduce-scatter.2

commit v11 on v7

--- a/solution.py
+++ b/solution.py
@@ -7,7 +7,7 @@
 from jax.sharding import Mesh, PartitionSpec as P
 
 PAIR = ("z", "y", "core")
-C_STEP = 8
+C_STEP = 4
 
 
 def cycle_kernel(window, vir_full, vt_ref, g_ref, m_ref, o_ref):
@@ -60,13 +60,15 @@
     vir_full = cols_local // vir_part
     vir_local = cycle_cols // occ_count
     pad_rows = -(-rows_local // 16) * 16
+    pidx = lax.axis_index(PAIR)
     per_i = occ_count // rows_local
-    pidx = lax.axis_index(PAIR)
+    labels = jnp.concatenate([occ_irrep, jnp.full((pad_rows - rows_local,), -1, occ_irrep.dtype)])
     label_first = lax.dynamic_slice(occ_irrep, (pidx // per_i,), (1,))
-    label_second = lax.dynamic_slice(occ_irrep, ((pidx % per_i) * rows_local,), (rows_local,))
-    allowed = label_first == label_second
-    amp_sym = jnp.where(allowed[:, None], amplitudes, jnp.zeros((), amplitudes.dtype))
-    amp_pad = jnp.pad(amp_sym, ((0, pad_rows - rows_local), (0, 0)))
+    label_second = lax.dynamic_slice(labels, ((pidx % per_i) * rows_local,), (pad_rows,))
+    row = lax.broadcasted_iota(jnp.int32, (pad_rows,), 0)
+    allowed = (label_second == label_first) & (row < rows_local)
+    amp_pad = jnp.where(allowed[:, None], jnp.pad(amplitudes, ((0, pad_rows - rows_local), (0, 0))),
+                        jnp.zeros((), amplitudes.dtype))
     g2 = lax.all_gather(amp_pad, PAIR, axis=0, tiled=True)
     n_blocks = g2.shape[0] // pad_rows
     total_rows = n_blocks * rows_local

time: 216 us -> 217 us (level)
  no operation moved by 1% of the time
where the time goes in v11:
time: 217 us; the launch traced here: 216 us
  waiting for transfers between devices  72.4 us (33%)
  local copies, waits for them, and re-layouts  58.2 us (27%)
  Pallas kernels  27.4 us (13%)
  blocking collectives  24.6 us (11%)
  matrix products  14.9 us (7%)
  between operations  13.2 us (6%)
  other arithmetic  5.8 us (3%)
    all_gather x1, waiting for transfers between devices, body(): g2 = lax.all_gather(amp_pad, PAIR, axis=0, tiled=True)  29.3 us
    pallas_call x1, Pallas kernels, cycle_matmul(): pl.pallas_call(functools.partial(cycle_kernel, window, vir_full), out_sha...  27.4 us
    all_to_all x1, blocking collectives, body(): lax.all_to_all(cycle_term, PAIR, split_axis=1, concat_axis=2, tiled=True)  24.6 us
    reduce_scatter x1, waiting for transfers between devices, body(): cyc = lax.psum_scatter(cyc, 'x', scatter_dimension=0, tiled=True)  23.9 us
    reshape x1, local copies, waits for them, and re-layouts, body(): jnp.transpose(v4, (2, 3, 0, 1))  21 us
    reduce_scatter x1, waiting for transfers between devices, body(): ladder = lax.psum_scatter(ladder, 'x', scatter_dimension=0, tiled=True)  19.1 us
    reshape x1, local copies, waits for them, and re-layouts, body(): v4 = cycle_ints.reshape(per_i, rows_local, vir_part, cycle_cols)  14.9 us
    dot_general x1, matrix products, body(): ladder = jnp.dot(g2, ladder_ints, preferred_element_type=jnp.float32)  14.9 us
  transfers between devices with their start and end apart: 3, of which 3 were waited for; matrix products, arithmetic and copies ran while one was open for 32% of the time, Pallas kernels for 0%

profile of v11, /device:TPU:1, one launch (start us, length us, event | category | flops | bytes accessed | tf_op | source)
XLA Modules:
  0.0 216.4 jit_solution(5530782927622107295)
XLA Ops:
  6.5 0.0 all-gather.2.cloned.1.call-start
  6.5 1.3 dynamic_slice.7
  7.8 1.4 compare_and_fusion
  9.2 2.0 pad_select_fusion
  11.2 0.0 all-gather.2.cloned.1.call-update
  11.2 0.0 reduce-scatter.5.cloned.1.call-start
  11.3 14.9 %copy.13 = bf16[4,60,32,960]{3,1,0,2:T(8,128)(2,1)S(1)} copy(bf16[4,60,32,960]{3,2,1,0:T(8,128)(2,1)} %bitcast.19) | data formatting | bytes 29491200 | tf_op jit(solution)/shard_map/reshape | solution.py:81
  26.1 7.4 %pad.10 = bf16[4,64,32,960]{3,1,0,2:T(8,128)(2,1)} pad(bf16[4,60,32,960]{3,1,0,2:T(8,128)(2,1)S(1)} %copy.13, bf16[]{:T(256)} %constant.54.clone.1), padding=0_0x0_4x0_0x0_0 | pad | bytes 30474242 | tf_op jit(solution)/shard_map/jit(_pad)/pad | solution.py:82
  33.5 0.0 copy-start.1
  33.5 0.0 slice-start
  33.5 21.0 %copy.14.vt_ref = bf16[32,960,256]{2,1,0:T(8,128)(2,1)} copy(bf16[32,960,256]{1,2,0:T(8,128)(2,1)} %bitcast.18) | data formatting | bytes 31457280 | tf_op jit(solution)/shard_map/reshape | solution.py:83
  54.5 0.0 copy-done.1
  54.5 0.0 slice-done
  54.5 0.1 compare_convert_fusion
  54.6 3.8 %reshape.53.m_ref = f32[8,960,1]{2,1,0:T(8,128)} reshape(f32[8,4,240]{2,1,0:T(4,128)S(1)} %broadcast_in_dim.23) | data formatting | bytes 61440 | tf_op jit(solution)/shard_map/reshape | solution.py:85
  58.4 29.3 %all-gather.2.cloned.1.call-done.g_ref = bf16[2048,4096]{1,0:T(8,128)(2,1)} async-done(((bf16[64,4096]{1,0:T(8,128)(2,1)}), bf16[2048,4096]{1,0:T(8,128)(2,1)}) %all-gather.2.cloned.1.call-update) | async-done | bytes 16777232 | tf_op jit(solution)/shard_map/all_gather | solution.py:72
  87.7 27.4 %shard_map.46 = f32[8,960,128]{2,1,0:T(8,128)S(1)} custom-call(bf16[32,960,256]{2,1,0:T(8,128)(2,1)} %copy.14.vt_ref, bf16[2048,4096]{1,0:T(8,128)(2,1)} %all-gather.2.cloned.1.call-done.g_ref, f32[8,960,1]{2,1,0:T(8,128)} %reshape.53.m_ref), custom_call_target="tpu_custom_call" | custom-call | tf_op jit(solution)/shard_map/pallas_call | solution.py:43
  115.0 0.0 copy-start
  115.0 1.9 copy-done
  116.9 0.0 reduce-scatter.5.cloned.1.call-update
  116.9 0.0 reduce-scatter.3.cloned.1.call-start
  117.0 14.9 %fusion = f32[2048,512]{1,0:T(8,128)} fusion(bf16[2048,4096]{1,0:T(8,128)(2,1)} %all-gather.2.cloned.1.call-done.g_ref, bf16[4096,512]{1,0:T(8,128)(2,1)} %param.6), kind=kOutput, calls=%fused_computation.4 | convolution fusion | flops 8589934592 | bytes 25165824 | tf_op jit(solution)/shard_map/dot_general | solution.py:77
  131.8 5.0 %reshape.47 = f32[8,240,512]{2,1,0:T(8,128)} reshape(f32[32,60,512]{2,1,0:T(8,128)} %bitcast.20) | data formatting | bytes 7864320 | tf_op jit(solution)/shard_map/reshape | solution.py:79
  136.8 0.0 reduce-scatter.3.cloned.1.call-update
  136.8 23.9 %reduce-scatter.5.cloned.1.call-done = f32[2,4,240,128]{3,2,1,0:T(8,128)} async-done(((f32[8,4,240,128]{3,2,1,0:T(8,128)}), f32[2,4,240,128]{3,2,1,0:T(8,128)}) %reduce-scatter.5.cloned.1.call-update) | async-done | bytes 983056 | tf_op jit(solution)/shard_map/reduce_scatter | solution.py:88
  160.7 1.7 copy.16
  162.4 24.6 %all_to_all.18 = f32[2,128,4,240]{3,2,0,1:T(4,128)S(1)} all-to-all(f32[2,128,4,240]{3,2,0,1:T(4,128)S(1)} %copy.16), channel_id=1, replica_groups=mesh['z'=4,'y'=4,'core'=2,'x'=4] {'z','y','core'}, dimensions={1} | all-to-all | bytes 1966080 | tf_op jit(solution)/shard_map/all_to_all | solution.py:91
  187.0 0.4 copy.18
  187.4 0.6 copy.19
  188.0 0.4 reshape.52
  188.4 19.1 %reduce-scatter.3.cloned.1.call-done = f32[2,240,512]{2,1,0:T(8,128)} async-done(((f32[8,240,512]{2,1,0:T(8,128)}), f32[2,240,512]{2,1,0:T(8,128)}) %reduce-scatter.3.cloned.1.call-update) | async-done | bytes 983056 | tf_op jit(solution)/shard_map/reduce_scatter | solution.py:93
  207.5 2.3 %add.35 = f32[2,240,512]{2,1,0:T(8,128)} add(f32[2,240,512]{2,1,0:T(8,128)} %reduce-scatter.3.cloned.1.call-done, f32[2,240,512]{2,1,0:T(8,128)S(1)} %reshape.52) | non-fusion elementwise | flops 245760 | bytes 2949120 | tf_op jit(solution)/shard_map/add | solution.py:94
  (1 shorter events, 0.0 us)
Async XLA Ops:
  6.5 81.1 %all-gather.2.cloned.1.call-start = ((), (), s32[]{:S(2)}) async-start(), calls=%async_computation.3 | async-start | bytes 17301504 | tf_op jit(solution)/shard_map/all_gather | solution.py:72
  11.2 149.5 %reduce-scatter.5.cloned.1.call-start = ((), (), s32[]{:S(2)}) async-start(), calls=%async_computation.5 | async-start | bytes 4915200 | tf_op jit(solution)/shard_map/reduce_scatter | solution.py:88
  33.5 21.0 %copy-start.1 = (s32[240]{0:T(256)S(1)}, s32[240]{0:T(256)}, u32[]{:S(2)}) copy-start(s32[240]{0:T(256)} %param.4) | copy-start | bytes 2884
  33.5 21.0 %slice-start = ((s32[240]{0:T(256)}), s32[8]{0:T(128)S(1)}, s32[]{:S(2)}) async-start(s32[240]{0:T(256)} %param.4), calls=%async_computation.6 | async-start | bytes 1024 | tf_op jit(solution)/shard_map/slice | solution.py:84
  115.0 1.9 copy-start
  116.9 90.6 %reduce-scatter.3.cloned.1.call-start = ((), (), s32[]{:S(2)}) async-start(), calls=%async_computation.4 | async-start | bytes 4915200 | tf_op jit(solution)/shard_map/reduce_scatter | solution.py:93
Sparse Core Ops, SparseCore 0:
  11.3 76.2 all-gather.1
  117.1 43.5 reduce-scatter.4
  163.1 44.3 reduce-scatter.2

commit v12 on v9

--- a/solution.py
+++ b/solution.py
@@ -7,7 +7,7 @@
 from jax.sharding import Mesh, PartitionSpec as P
 
 PAIR = ("z", "y", "core")
-C_STEP = 4
+C_STEP = 2
 
 
 def cycle_kernel(window, vir_full, vt_ref, g_ref, o_ref):

time: 214 us -> 219 us (1.023)
  Pallas kernels: 23.9 us -> 28.7 us
    pallas_call x1, Pallas kernels: 23.9 us -> 28.7 us  [cycle_matmul(): pl.pallas_call(functools.partial(cycle_kernel, window, vir_full), out_sha...]
  transfers between devices with their start and end apart: 3 -> 3, of which waited for: 3 -> 3; matrix products, arithmetic and copies ran while one was open for 31% -> 30% of each run, Pallas kernels for 0% -> 0%
where the time goes in v12:
time: 219 us; the launch traced here: 218 us
  waiting for transfers between devices  76.1 us (35%)
  local copies, waits for them, and re-layouts  52.6 us (24%)
  Pallas kernels  28.7 us (13%)
  blocking collectives  24.6 us (11%)
  matrix products  14.9 us (7%)
  between operations  13.2 us (6%)
  other arithmetic  8 us (4%)
    all_gather x1, waiting for transfers between devices, body(): g2 = lax.all_gather(amp_pad, PAIR, axis=0, tiled=True)  33.1 us
    pallas_call x1, Pallas kernels, cycle_matmul(): pl.pallas_call(functools.partial(cycle_kernel, window, vir_full), out_sha...  28.7 us
    all_to_all x1, blocking collectives, body(): lax.all_to_all(cycle_term, PAIR, split_axis=1, concat_axis=2, tiled=True)  24.6 us
    reduce_scatter x1, waiting for transfers between devices, body(): cyc = lax.psum_scatter(cyc, 'x', scatter_dimension=0, tiled=True)  23.8 us
    reshape x1, local copies, waits for them, and re-layouts, body(): jnp.transpose(v4, (2, 3, 0, 1))  21 us
    reduce_scatter x1, waiting for transfers between devices, body(): ladder = lax.psum_scatter(ladder, 'x', scatter_dimension=0, tiled=True)  19.2 us
    dot_general x1, matrix products, body(): ladder = jnp.dot(g2, ladder_ints, preferred_element_type=jnp.float32)  14.9 us
    reshape x1, local copies, waits for them, and re-layouts, body(): v4 = cycle_ints.reshape(per_i, rows_local, vir_part, cycle_cols)  14.9 us
  transfers between devices with their start and end apart: 3, of which 3 were waited for; matrix products, arithmetic and copies ran while one was open for 30% of the time, Pallas kernels for 0%

profile of v12, /device:TPU:1, one launch (start us, length us, event | category | flops | bytes accessed | tf_op | source)
XLA Modules:
  0.0 218.1 jit_solution(13436931110066216688)
XLA Ops:
  6.5 0.0 all-gather.2.cloned.1.call-start
  6.5 1.3 dynamic_slice.7
  7.8 1.4 compare_and_fusion
  9.2 2.0 pad_select_fusion
  11.2 0.0 all-gather.2.cloned.1.call-update
  11.2 0.0 reduce-scatter.5.cloned.1.call-start
  11.3 14.9 %copy.12 = bf16[4,60,32,960]{3,1,0,2:T(8,128)(2,1)S(1)} copy(bf16[4,60,32,960]{3,2,1,0:T(8,128)(2,1)} %bitcast.19) | data formatting | bytes 29491200 | tf_op jit(solution)/shard_map/reshape | solution.py:75
  26.1 7.4 %pad.10 = bf16[4,64,32,960]{3,1,0,2:T(8,128)(2,1)} pad(bf16[4,60,32,960]{3,1,0,2:T(8,128)(2,1)S(1)} %copy.12, bf16[]{:T(256)} %constant.54.clone.1), padding=0_0x0_4x0_0x0_0 | pad | bytes 30474242 | tf_op jit(solution)/shard_map/jit(_pad)/pad | solution.py:76
  33.5 0.0 copy-start
  33.5 0.0 slice-start
  33.5 21.0 %copy.13.vt_ref = bf16[32,960,256]{2,1,0:T(8,128)(2,1)} copy(bf16[32,960,256]{1,2,0:T(8,128)(2,1)} %bitcast.18) | data formatting | bytes 31457280 | tf_op jit(solution)/shard_map/reshape | solution.py:77
  54.5 0.0 copy-done
  54.5 0.0 slice-done
  54.5 0.1 compare_convert_fusion
  54.6 33.1 %all-gather.2.cloned.1.call-done.g_ref = bf16[2048,4096]{1,0:T(8,128)(2,1)} async-done(((bf16[64,4096]{1,0:T(8,128)(2,1)}), bf16[2048,4096]{1,0:T(8,128)(2,1)}) %all-gather.2.cloned.1.call-update) | async-done | bytes 16777232 | tf_op jit(solution)/shard_map/all_gather | solution.py:66
  87.7 28.7 %shard_map.46 = f32[8,960,128]{2,1,0:T(8,128)S(1)} custom-call(bf16[32,960,256]{2,1,0:T(8,128)(2,1)} %copy.13.vt_ref, bf16[2048,4096]{1,0:T(8,128)(2,1)} %all-gather.2.cloned.1.call-done.g_ref), custom_call_target="tpu_custom_call" | custom-call | tf_op jit(solution)/shard_map/pallas_call | solution.py:38
  116.3 2.2 %broadcast_multiply_fusion = f32[8,4,240,128]{3,2,1,0:T(8,128)} fusion(f32[8,4,240,128]{3,2,1,0:T(8,128)S(1)} %bitcast.17, f32[8,240]{1,0:T(8,128)S(1)} %compare_convert_fusion), kind=kLoop, calls=%fused_computation | loop fusion | flops 983040 | bytes 7872000 | tf_op jit(solution)/shard_map/mul | solution.py:80
  118.6 0.0 reduce-scatter.5.cloned.1.call-update
  118.6 0.0 reduce-scatter.3.cloned.1.call-start
  118.6 14.9 %fusion = f32[2048,512]{1,0:T(8,128)} fusion(bf16[2048,4096]{1,0:T(8,128)(2,1)} %all-gather.2.cloned.1.call-done.g_ref, bf16[4096,512]{1,0:T(8,128)(2,1)} %param.6), kind=kOutput, calls=%fused_computation.5 | convolution fusion | flops 8589934592 | bytes 25165824 | tf_op jit(solution)/shard_map/dot_general | solution.py:71
  133.5 5.0 %reshape.47 = f32[8,240,512]{2,1,0:T(8,128)} reshape(f32[32,60,512]{2,1,0:T(8,128)} %bitcast.20) | data formatting | bytes 7864320 | tf_op jit(solution)/shard_map/reshape | solution.py:73
  138.5 0.0 reduce-scatter.3.cloned.1.call-update
  138.5 23.8 %reduce-scatter.5.cloned.1.call-done = f32[2,4,240,128]{3,2,1,0:T(8,128)} async-done(((f32[8,4,240,128]{3,2,1,0:T(8,128)}), f32[2,4,240,128]{3,2,1,0:T(8,128)}) %reduce-scatter.5.cloned.1.call-update) | async-done | bytes 983056 | tf_op jit(solution)/shard_map/reduce_scatter | solution.py:81
  162.3 1.7 copy.14
  164.0 24.6 %all_to_all.18 = f32[2,128,4,240]{3,2,0,1:T(4,128)S(1)} all-to-all(f32[2,128,4,240]{3,2,0,1:T(4,128)S(1)} %copy.14), channel_id=1, replica_groups=mesh['z'=4,'y'=4,'core'=2,'x'=4] {'z','y','core'}, dimensions={1} | all-to-all | bytes 1966080 | tf_op jit(solution)/shard_map/all_to_all | solution.py:84
  188.6 0.4 copy.16
  189.1 0.6 copy.17
  189.6 0.4 reshape.51
  190.0 19.2 %reduce-scatter.3.cloned.1.call-done = f32[2,240,512]{2,1,0:T(8,128)} async-done(((f32[8,240,512]{2,1,0:T(8,128)}), f32[2,240,512]{2,1,0:T(8,128)}) %reduce-scatter.3.cloned.1.call-update) | async-done | bytes 983056 | tf_op jit(solution)/shard_map/reduce_scatter | solution.py:86
  209.2 2.3 %add.35 = f32[2,240,512]{2,1,0:T(8,128)} add(f32[2,240,512]{2,1,0:T(8,128)} %reduce-scatter.3.cloned.1.call-done, f32[2,240,512]{2,1,0:T(8,128)S(1)} %reshape.51) | non-fusion elementwise | flops 245760 | bytes 2949120 | tf_op jit(solution)/shard_map/add | solution.py:87
Async XLA Ops:
  6.5 81.1 %all-gather.2.cloned.1.call-start = ((), (), s32[]{:S(2)}) async-start(), calls=%async_computation.3 | async-start | bytes 17301504 | tf_op jit(solution)/shard_map/all_gather | solution.py:66
  11.2 151.1 %reduce-scatter.5.cloned.1.call-start = ((), (), s32[]{:S(2)}) async-start(), calls=%async_computation.5 | async-start | bytes 4915200 | tf_op jit(solution)/shard_map/reduce_scatter | solution.py:81
  33.5 21.0 %copy-start = (s32[240]{0:T(256)S(1)}, s32[240]{0:T(256)}, u32[]{:S(2)}) copy-start(s32[240]{0:T(256)} %param.4) | copy-start | bytes 2884
  33.5 21.0 %slice-start = ((s32[240]{0:T(256)}), s32[8]{0:T(128)S(1)}, s32[]{:S(2)}) async-start(s32[240]{0:T(256)} %param.4), calls=%async_computation.6 | async-start | bytes 1024 | tf_op jit(solution)/shard_map/slice | solution.py:79
  118.6 90.6 %reduce-scatter.3.cloned.1.call-start = ((), (), s32[]{:S(2)}) async-start(), calls=%async_computation.4 | async-start | bytes 4915200 | tf_op jit(solution)/shard_map/reduce_scatter | solution.py:86
Sparse Core Ops, SparseCore 0:
  11.3 76.2 all-gather.1
  118.7 43.5 reduce-scatter.4
  164.8 44.4 reduce-scatter.2

commit v13 on v9

--- a/solution.py
+++ b/solution.py
@@ -77,9 +77,11 @@
     vt = jnp.transpose(v4, (2, 3, 0, 1)).reshape(vir_part, cycle_cols, per_i * pad_rows)
     cyc = cycle_matmul(vt, g2, window, vir_full)
     same_irrep = (occ_irrep[:window][:, None] == occ_irrep[None, :]).astype(jnp.float32)
-    cyc = cyc.reshape(window, vir_local, occ_count, vir_full) * same_irrep[:, None, :, None]
+    cyc = cyc.reshape(window, vir_local, occ_count, vir_full)
     cyc = lax.psum_scatter(cyc, "x", scatter_dimension=0, tiled=True)
     rows_here = cyc.shape[0]
+    same_here = lax.dynamic_slice_in_dim(same_irrep, lax.axis_index("x") * rows_here, rows_here, axis=0)
+    cyc = cyc * same_here[:, None, :, None]
     cycle_term = jnp.transpose(cyc, (0, 3, 1, 2))
     regrouped = lax.all_to_all(cycle_term, PAIR, split_axis=1, concat_axis=2, tiled=True)
     moved = jnp.transpose(regrouped, (0, 3, 1, 2)).reshape(rows_here, occ_count, vir_local * vir_full)

time: 214 us -> 214 us (level)
    mul x1 -> x0, other arithmetic: 2.2 us -> none  [body(): cyc.reshape(window, vir_local, occ_count, vir_full)]
where the time goes in v13:
time: 214 us; the launch traced here: 213 us
  waiting for transfers between devices  75.9 us (35%)
  local copies, waits for them, and re-layouts  53.3 us (25%)
  blocking collectives  24.6 us (11%)
  Pallas kernels  23.9 us (11%)
  matrix products  14.9 us (7%)
  between operations  13.2 us (6%)
  other arithmetic  7.13 us (3%)
    all_gather x1, waiting for transfers between devices, body(): g2 = lax.all_gather(amp_pad, PAIR, axis=0, tiled=True)  33.2 us
    all_to_all x1, blocking collectives, body(): lax.all_to_all(cycle_term, PAIR, split_axis=1, concat_axis=2, tiled=True)  24.6 us
    pallas_call x1, Pallas kernels, cycle_matmul(): pl.pallas_call(functools.partial(cycle_kernel, window, vir_full), out_sha...  23.9 us
    reduce_scatter x1, waiting for transfers between devices, body(): cyc = lax.psum_scatter(cyc, 'x', scatter_dimension=0, tiled=True)  23.7 us
    reshape x1, local copies, waits for them, and re-layouts, body(): jnp.transpose(v4, (2, 3, 0, 1))  20.9 us
    reduce_scatter x1, waiting for transfers between devices, body(): ladder = lax.psum_scatter(ladder, 'x', scatter_dimension=0, tiled=True)  19 us
    reshape x1, local copies, waits for them, and re-layouts, body(): v4 = cycle_ints.reshape(per_i, rows_local, vir_part, cycle_cols)  14.9 us
    dot_general x1, matrix products, body(): ladder = jnp.dot(g2, ladder_ints, preferred_element_type=jnp.float32)  14.9 us
  transfers between devices with their start and end apart: 3, of which 3 were waited for; matrix products, arithmetic and copies ran while one was open for 31% of the time, Pallas kernels for 0%

profile of v13, /device:TPU:1, one launch (start us, length us, event | category | flops | bytes accessed | tf_op | source)
XLA Modules:
  0.0 212.9 jit_solution(6918965612271110790)
XLA Ops:
  6.5 0.0 all-gather.2.cloned.1.call-start
  6.5 1.3 dynamic_slice.10
  7.8 1.4 compare_and_fusion
  9.2 2.0 pad_select_fusion
  11.2 0.0 all-gather.2.cloned.1.call-update
  11.2 0.0 reduce-scatter.5.cloned.1.call-start
  11.3 14.9 %copy.12 = bf16[4,60,32,960]{3,1,0,2:T(8,128)(2,1)S(1)} copy(bf16[4,60,32,960]{3,2,1,0:T(8,128)(2,1)} %bitcast.20) | data formatting | bytes 29491200 | tf_op jit(solution)/shard_map/reshape | solution.py:75
  26.1 7.4 %pad.10 = bf16[4,64,32,960]{3,1,0,2:T(8,128)(2,1)} pad(bf16[4,60,32,960]{3,1,0,2:T(8,128)(2,1)S(1)} %copy.12, bf16[]{:T(256)} %constant.56.clone.1), padding=0_0x0_4x0_0x0_0 | pad | bytes 30474242 | tf_op jit(solution)/shard_map/jit(_pad)/pad | solution.py:76
  33.5 20.9 %copy.13.vt_ref = bf16[32,960,256]{2,1,0:T(8,128)(2,1)} copy(bf16[32,960,256]{1,2,0:T(8,128)(2,1)} %bitcast.19) | data formatting | bytes 31457280 | tf_op jit(solution)/shard_map/reshape | solution.py:77
  54.5 33.2 %all-gather.2.cloned.1.call-done.g_ref = bf16[2048,4096]{1,0:T(8,128)(2,1)} async-done(((bf16[64,4096]{1,0:T(8,128)(2,1)}), bf16[2048,4096]{1,0:T(8,128)(2,1)}) %all-gather.2.cloned.1.call-update) | async-done | bytes 16777232 | tf_op jit(solution)/shard_map/all_gather | solution.py:66
  87.7 23.9 %shard_map.46 = f32[8,960,128]{2,1,0:T(8,128)S(1)} custom-call(bf16[32,960,256]{2,1,0:T(8,128)(2,1)} %copy.13.vt_ref, bf16[2048,4096]{1,0:T(8,128)(2,1)} %all-gather.2.cloned.1.call-done.g_ref), custom_call_target="tpu_custom_call" | custom-call | tf_op jit(solution)/shard_map/pallas_call | solution.py:38
  111.5 0.0 copy-start
  111.5 1.9 copy-done
  113.4 0.0 reduce-scatter.5.cloned.1.call-update
  113.4 0.0 slice-start
  113.4 0.0 copy-start.1
  113.5 0.0 reduce-scatter.3.cloned.1.call-start
  113.5 14.9 %fusion = f32[2048,512]{1,0:T(8,128)} fusion(bf16[2048,4096]{1,0:T(8,128)(2,1)} %all-gather.2.cloned.1.call-done.g_ref, bf16[4096,512]{1,0:T(8,128)(2,1)} %param.6), kind=kOutput, calls=%fused_computation.5 | convolution fusion | flops 8589934592 | bytes 25165824 | tf_op jit(solution)/shard_map/dot_general | solution.py:71
  128.4 5.0 %reshape.23 = f32[8,240,512]{2,1,0:T(8,128)} reshape(f32[32,60,512]{2,1,0:T(8,128)} %bitcast.21) | data formatting | bytes 7864320 | tf_op jit(solution)/shard_map/reshape | solution.py:73
  133.3 0.0 reduce-scatter.3.cloned.1.call-update
  133.4 0.0 slice-done
  133.4 0.1 dynamic-slice
  133.5 0.0 copy-done.1
  133.5 0.1 compare_convert_fusion
  133.5 23.7 %reduce-scatter.5.cloned.1.call-done = f32[2,4,240,128]{3,2,1,0:T(8,128)} async-done(((f32[8,4,240,128]{3,2,1,0:T(8,128)}), f32[2,4,240,128]{3,2,1,0:T(8,128)}) %reduce-scatter.5.cloned.1.call-update) | async-done | bytes 983056 | tf_op jit(solution)/shard_map/reduce_scatter | solution.py:81
  157.2 1.3 multiply_bitcast_fusion
  158.5 0.5 copy.14
  159.0 24.6 %all_to_all.18 = f32[2,128,4,240]{3,2,0,1:T(4,128)S(1)} all-to-all(f32[2,128,4,240]{3,2,0,1:T(4,128)S(1)} %copy.14), channel_id=1, replica_groups=mesh['z'=4,'y'=4,'core'=2,'x'=4] {'z','y','core'}, dimensions={1} | all-to-all | bytes 1966080 | tf_op jit(solution)/shard_map/all_to_all | solution.py:86
  183.6 0.4 copy.16
  184.1 0.6 copy.17
  184.6 0.4 reshape.27
  185.0 19.0 %reduce-scatter.3.cloned.1.call-done = f32[2,240,512]{2,1,0:T(8,128)} async-done(((f32[8,240,512]{2,1,0:T(8,128)}), f32[2,240,512]{2,1,0:T(8,128)}) %reduce-scatter.3.cloned.1.call-update) | async-done | bytes 983056 | tf_op jit(solution)/shard_map/reduce_scatter | solution.py:88
  204.1 2.3 %add.39 = f32[2,240,512]{2,1,0:T(8,128)} add(f32[2,240,512]{2,1,0:T(8,128)} %reduce-scatter.3.cloned.1.call-done, f32[2,240,512]{2,1,0:T(8,128)S(1)} %reshape.27) | non-fusion elementwise | flops 245760 | bytes 2949120 | tf_op jit(solution)/shard_map/add | solution.py:89
Async XLA Ops:
  6.5 81.1 %all-gather.2.cloned.1.call-start = ((), (), s32[]{:S(2)}) async-start(), calls=%async_computation.3 | async-start | bytes 17301504 | tf_op jit(solution)/shard_map/all_gather | solution.py:66
  11.2 146.0 %reduce-scatter.5.cloned.1.call-start = ((), (), s32[]{:S(2)}) async-start(), calls=%async_computation.5 | async-start | bytes 4915200 | tf_op jit(solution)/shard_map/reduce_scatter | solution.py:81
  111.5 1.9 copy-start
  113.4 19.9 %slice-start = ((s32[240]{0:T(256)}), s32[8]{0:T(128)S(1)}, s32[]{:S(2)}) async-start(s32[240]{0:T(256)} %param.4), calls=%async_computation.6 | async-start | bytes 1024 | tf_op jit(solution)/shard_map/slice | solution.py:79
  113.4 20.0 %copy-start.1 = (s32[240]{0:T(256)S(1)}, s32[240]{0:T(256)}, u32[]{:S(2)}) copy-start(s32[240]{0:T(256)} %param.4) | copy-start | bytes 2884
  113.5 90.6 %reduce-scatter.3.cloned.1.call-start = ((), (), s32[]{:S(2)}) async-start(), calls=%async_computation.4 | async-start | bytes 4915200 | tf_op jit(solution)/shard_map/reduce_scatter | solution.py:88
Sparse Core Ops, SparseCore 0:
  11.3 76.2 all-gather.1
  113.5 43.5 reduce-scatter.4
  159.6 44.4 reduce-scatter.2
